TPU v7x, 768 devices: a whole 4x8x12 slice. The times are simulated.
768 devices in a mesh: grp: 96 (over z, x, core), blk: 8 (over y).
Axes of the slice: x: 4, y: 8, z: 12, core: 2. Of those that a mesh axis runs over, the one named last changes fastest.
Arguments:
- query: bfloat16 [196608, 512], P(('grp', 'blk')), may hold values from -6 to 6
- key: bfloat16 [196608, 512], P(('grp', 'blk')), may hold values from -6 to 6
- value: bfloat16 [196608, 512], P(('grp', 'blk')), may hold values from -6 to 6
- out_grad: bfloat16 [196608, 512], P(('grp', 'blk')), may hold values from -6 to 6
- partner: int32 [2, 196608], P(None, ('grp', 'blk')), may hold values from 0 to 127, as said below
- tiles: int32 [1536, 6], P(('grp', 'blk')), may hold values from 0 to 15, as said below
- tile_count: int32 [1536], P(('grp', 'blk')), may hold values from 1 to 6, as said below
Outputs:
- attended: bfloat16 [196608, 512], P(('grp', 'blk'))
- query_grad: bfloat16 [196608, 512], P(('grp', 'blk'))
- key_grad: bfloat16 [196608, 512], P(('grp', 'blk'))
- value_grad: bfloat16 [196608, 512], P(('grp', 'blk'))
Inputs may be any that keep to these rules, and one draw needn't show every extreme that they name: `partner`: the matching of every round is symmetric: match[r, match[r, n]] = n for every node n. `tiles`: the entries of a row are distinct; the first entry of block k's row is k's own block within its cluster; block a lists block b among its first tile_count entries exactly when b lists a. `tile_count`: some block of every cluster uses all 6 slots.
All inputs are finite; a program needn't handle non-finite values.
Results may differ from a plain program's by a relative error of at most 0.014.
Values may be sent and summed in bfloat16 or wider, within the bound.
No kernel may reach another device: no remote copies, remote signals or barrier semaphores. Data moves between devices by JAX's collectives and lax.ppermute only.
A program may use at most 64 MiB of HBM per device.

v0:
```python
import jax
import jax.numpy as jnp
from jax import lax
from jax.sharding import PartitionSpec as P

HEADS = 8
BLOCK = 128
TMAX = 6
ROUNDS = 2


NEG_BIG = -1e30


def passed_along(x, axis, by):
    size = lax.axis_size(axis)
    return lax.ppermute(x, axis, [(i, (i + by) % size) for i in range(size)])


def settle(values):
    return lax.optimization_barrier(values.astype(jnp.bfloat16)).astype(jnp.float32)


def move_rows(load, offset):
    return passed_along(load, "grp", offset)


def move_terms(load, offset):
    return passed_along(load, "grp", offset)


def fetch_partners(load, slots, offset, mover):
    half = load.shape[0] // 2
    ahead = mover(load[half:], -offset)
    behind = mover(load[:half], offset)
    return jnp.concatenate([ahead[slots[:half]], behind[slots[half:]]], 0)


def join_heads(stack):
    moved = jnp.moveaxis(stack, 0, -2)
    return moved.reshape(moved.shape[:-2] + (moved.shape[-2] * moved.shape[-1],))


def shards(query, key, value, out_grad, partner, tiles, tile_count):
    f32 = jnp.float32
    bf16 = jnp.bfloat16
    nodes, width = query.shape
    head_dim = width // HEADS
    scale = head_dim ** (-0.5)
    span = min(width, 128)
    groups = width // span
    per_group = span // head_dim
    blocks_dev = nodes // BLOCK
    team = lax.axis_size("blk")
    cluster_blocks = blocks_dev * team
    keys_tile = TMAX * BLOCK
    both = jnp.concatenate([key, value], 1)
    cluster_rows = lax.all_gather(both, "blk", axis=0, tiled=True)
    partner_rows = jnp.stack(
        [fetch_partners(both, partner[step], step + 1, move_rows) for step in range(ROUNDS)]
    )
    tiled = cluster_rows.reshape(cluster_blocks, BLOCK, 2 * width)[tiles]
    live = jnp.arange(TMAX, dtype=jnp.int32)[None, :] < tile_count[:, None]
    key_live = jnp.broadcast_to(live[:, :, None], (blocks_dev, TMAX, BLOCK)).reshape(
        blocks_dev, keys_tile
    )

    def head_group(index):
        left = index * span
        right = width + index * span
        q_part = lax.dynamic_slice_in_dim(query, left, span, 1).reshape(
            blocks_dev, BLOCK, per_group, head_dim
        )
        g_part = lax.dynamic_slice_in_dim(out_grad, left, span, 1).reshape(
            blocks_dev, BLOCK, per_group, head_dim
        )
        k_tile = lax.dynamic_slice_in_dim(tiled, left, span, 3).reshape(
            blocks_dev, keys_tile, per_group, head_dim
        )
        v_tile = lax.dynamic_slice_in_dim(tiled, right, span, 3).reshape(
            blocks_dev, keys_tile, per_group, head_dim
        )
        pair_shape = (ROUNDS, blocks_dev, BLOCK, per_group, head_dim)
        k_pair = lax.dynamic_slice_in_dim(partner_rows, left, span, 2).reshape(pair_shape)
        v_pair = lax.dynamic_slice_in_dim(partner_rows, right, span, 2).reshape(pair_shape)
        s_loc = jnp.einsum("bqhd,bkhd->bhqk", q_part, k_tile, preferred_element_type=f32) * scale
        s_loc = jnp.where(key_live[:, None, None, :], s_loc, NEG_BIG)
        s_pair = jnp.einsum("bqhd,rbqhd->bhqr", q_part, k_pair, preferred_element_type=f32) * scale
        top = jnp.maximum(jnp.max(s_loc, -1), jnp.max(s_pair, -1))
        e_loc = jnp.exp(s_loc - top[..., None])
        e_pair = jnp.exp(s_pair - top[..., None])
        total = jnp.sum(e_loc, -1) + jnp.sum(e_pair, -1)
        p_loc = e_loc / total[..., None]
        p_pair = e_pair / total[..., None]
        w_loc = p_loc.astype(bf16)
        w_pair = p_pair.astype(bf16)
        out_full = jnp.einsum("bhqk,bkhd->bqhd", w_loc, v_tile, preferred_element_type=f32)
        out_full = out_full + jnp.einsum(
            "bhqr,rbqhd->bqhd", w_pair, v_pair, preferred_element_type=f32
        )
        delta = jnp.transpose(jnp.sum(g_part.astype(f32) * out_full, -1), (0, 2, 1))
        d_loc = jnp.einsum("bqhd,bkhd->bhqk", g_part, v_tile, preferred_element_type=f32)
        d_pair = jnp.einsum("bqhd,rbqhd->bhqr", g_part, v_pair, preferred_element_type=f32)
        z_loc = (p_loc * (d_loc - delta[..., None])).astype(bf16)
        z_pair = (p_pair * (d_pair - delta[..., None])).astype(bf16)
        q_grad = jnp.einsum("bhqk,bkhd->bqhd", z_loc, k_tile, preferred_element_type=f32)
        q_grad = (
            q_grad + jnp.einsum("bhqr,rbqhd->bqhd", z_pair, k_pair, preferred_element_type=f32)
        ) * scale
        t_key = (
            jnp.einsum("bhqr,bqhd->rbqhd", z_pair, q_part, preferred_element_type=f32) * scale
        ).astype(bf16)
        t_val = jnp.einsum("bhqr,bqhd->rbqhd", w_pair, g_part, preferred_element_type=f32).astype(
            bf16
        )
        log_total = top + jnp.log(total)
        results = (
            out_full.reshape(nodes, span),
            q_grad.reshape(nodes, span),
            t_key.reshape(ROUNDS, nodes, span),
            t_val.reshape(ROUNDS, nodes, span),
            log_total,
            delta,
        )
        c_key = (
            jnp.einsum("bhqk,bqhd->bkhd", z_loc, q_part, preferred_element_type=f32) * scale
        ).reshape(blocks_dev, TMAX, BLOCK, span)
        c_val = jnp.einsum("bhqk,bqhd->bkhd", w_loc, g_part, preferred_element_type=f32).reshape(
            blocks_dev, TMAX, BLOCK, span
        )
        empty = jnp.zeros((cluster_blocks, BLOCK, span), f32)
        results = results + (
            empty.at[tiles].add(c_key).reshape(cluster_blocks * BLOCK, span),
            empty.at[tiles].add(c_val).reshape(cluster_blocks * BLOCK, span),
        )
        return results

    outputs = lax.map(head_group, jnp.arange(groups, dtype=jnp.int32))
    attended = join_heads(outputs[0]).astype(bf16)
    query_grad = join_heads(outputs[1]).astype(bf16)
    t_key = join_heads(outputs[2])
    t_val = join_heads(outputs[3])
    k_sum, v_sum = (
        lax.psum_scatter(
            settle(join_heads(outputs[6])).astype(jnp.bfloat16),
            "blk",
            scatter_dimension=0,
            tiled=True,
        ).astype(jnp.float32),
        lax.psum_scatter(
            settle(join_heads(outputs[7])).astype(jnp.bfloat16),
            "blk",
            scatter_dimension=0,
            tiled=True,
        ).astype(jnp.float32),
    )
    returned = jnp.stack(
        [
            fetch_partners(
                jnp.concatenate([t_key[step], t_val[step]], 1), partner[step], step + 1, move_terms
            )
            for step in range(ROUNDS)
        ]
    )
    returned = jnp.sum(returned.astype(f32), 0)
    key_grad = (k_sum + returned[:, :width]).astype(bf16)
    value_grad = (v_sum + returned[:, width:]).astype(bf16)
    return (attended, query_grad, key_grad, value_grad)


def solution(mesh):
    in_specs = (
        P(("grp", "blk"), None),
        P(("grp", "blk"), None),
        P(("grp", "blk"), None),
        P(("grp", "blk"), None),
        P(None, ("grp", "blk")),
        P(("grp", "blk"), None),
        P(("grp", "blk")),
    )
    out_specs = (
        P(("grp", "blk"), None),
        P(("grp", "blk"), None),
        P(("grp", "blk"), None),
        P(("grp", "blk"), None),
    )
    return jax.shard_map(shards, mesh=mesh, in_specs=in_specs, out_specs=out_specs, check_vma=False)
```

profile of v0, /device:TPU:1, one launch (start us, length us, event | category | flops | bytes accessed | tf_op | source)
XLA Modules:
  0.0 298.3 jit_solution(3313180572507086053)
XLA Ops:
  10.1 1.1 fusion.28
  11.2 3.9 %collective-permute-start.3 = (bf16[128,1024]{1,0:T(8,128)(2,1)S(1)}, bf16[128,1024]{1,0:T(8,128)(2,1)S(1)}, u32[]{:S(2)}, u32[]{:S(2)}) collective-permute-start(bf16[128,1024]{1,0:T(8,128)(2,1)S(1)} %get-tuple-element.334), channel_id=1, source_target_pairs={{0,16},{8,24},{16,32},{24,40},{32,48},{40,56},{48,64},{56,72},{64,... | collective-permute-start | bytes 786440 | tf_op jit(solution)/shard_map/ppermute | solution.py:17
  15.1 4.0 %collective-permute-start.1 = (bf16[128,1024]{1,0:T(8,128)(2,1)S(1)}, bf16[128,1024]{1,0:T(8,128)(2,1)S(1)}, u32[]{:S(2)}, u32[]{:S(2)}) collective-permute-start(bf16[128,1024]{1,0:T(8,128)(2,1)S(1)} %get-tuple-element.334), channel_id=1, source_target_pairs={{0,8},{8,16},{16,24},{24,32},{32,40},{40,48},{48,56},{56,64},{64,7... | collective-permute-start | bytes 786440 | tf_op jit(solution)/shard_map/ppermute | solution.py:17
  19.1 13.3 %collective-permute-start.2 = (bf16[128,1024]{1,0:T(8,128)(2,1)S(1)}, bf16[128,1024]{1,0:T(8,128)(2,1)S(1)}, u32[]{:S(2)}, u32[]{:S(2)}) collective-permute-start(bf16[128,1024]{1,0:T(8,128)(2,1)S(1)} %get-tuple-element.333), channel_id=1, source_target_pairs={{0,752},{8,760},{16,0},{24,8},{32,16},{40,24},{48,32},{56,40},{64,... | collective-permute-start | bytes 786440 | tf_op jit(solution)/shard_map/ppermute | solution.py:17
  32.4 2.9 collective-permute-start
  39.1 1.4 collective-permute-done
  41.5 1.5 copy.122
  43.0 34.8 %all-gather.2.cloned.1.call-done = bf16[2048,1024]{1,0:T(8,128)(2,1)} async-done(((bf16[256,1024]{1,0:T(8,128)(2,1)}), bf16[2048,1024]{1,0:T(8,128)(2,1)}) %all-gather.2.cloned.1.call-update) | async-done | bytes 4194320 | tf_op jit(solution)/shard_map/all_gather | solution.py:58
  77.9 2.9 gather_fusion
  80.8 4.8 %copy.120 = bf16[2,6,128,1024]{2,1,3,0:T(8,128)(2,1)} copy(bf16[2,6,128,1024]{3,2,1,0:T(8,128)(2,1)S(1)} %bitcast.194) | data formatting | bytes 6291456
  86.2 108.1 %while.23 = (s32[]{:T(128)}, bf16[4,256,128]{1,2,0:T(8,128)(2,1)}, bf16[4,256,128]{1,2,0:T(8,128)(2,1)}, bf16[4,2,256,128]{2,3,1,0:T(8,128)(2,1)}, bf16[4,2,256,...) while((s32[]{:T(128)}, bf16[4,256,128]{1,2,0:T(8,128)(2,1)}, ...), condition=%wide.region_8.9_spmd.clone, body=%wide.region_0.8_spmd.clone.sunk | while | flops 309147168 | bytes 47453524 | solution.py:138
  86.2 1.3 dynamic_slice.65
  88.2 1.4 constant_dynamic-slice_fusion.10
  94.0 1.0 constant_dynamic-slice_fusion.13
  96.9 1.0 multiply_reduce_fusion.15
  97.9 1.6 multiply_convert_fusion.6
  104.8 1.4 scatter_fusion
  106.2 1.1 fusion.78
  107.4 2.4 copy.241
  110.7 1.4 scatter_fusion.1
  112.1 1.1 bitcast_dynamic-update-slice_fusion.3
  113.3 1.3 dynamic_slice.65
  115.2 1.4 constant_dynamic-slice_fusion.10
  121.0 1.0 constant_dynamic-slice_fusion.13
  123.9 1.0 multiply_reduce_fusion.15
  125.0 1.6 multiply_convert_fusion.6
  131.9 1.4 scatter_fusion
  133.3 1.1 fusion.78
  134.4 2.4 copy.241
  137.8 1.4 scatter_fusion.1
  139.2 1.1 bitcast_dynamic-update-slice_fusion.3
  140.3 1.3 dynamic_slice.65
  142.2 1.4 constant_dynamic-slice_fusion.10
  148.0 1.0 constant_dynamic-slice_fusion.13
  150.9 1.0 multiply_reduce_fusion.15
  152.0 1.6 multiply_convert_fusion.6
  158.9 1.4 scatter_fusion
  160.3 1.1 fusion.78
  161.4 2.4 copy.241
  164.8 1.4 scatter_fusion.1
  166.2 1.1 bitcast_dynamic-update-slice_fusion.3
  167.3 1.3 dynamic_slice.65
  169.2 1.4 constant_dynamic-slice_fusion.10
  175.0 1.0 constant_dynamic-slice_fusion.13
  177.9 1.0 multiply_reduce_fusion.15
  179.0 1.6 multiply_convert_fusion.6
  185.9 1.4 scatter_fusion
  187.3 1.1 fusion.78
  188.4 2.4 copy.241
  191.8 1.4 scatter_fusion.1
  193.2 1.1 bitcast_dynamic-update-slice_fusion.3
  194.3 3.1 %copy_bitcast_fusion.1 = bf16[2048,512]{1,0:T(8,128)(2,1)} fusion(bf16[4,2048,128]{2,1,0:T(8,128)(2,1)} %get-tuple-element.187), kind=kLoop, calls=%fused_computation.68 | loop fusion | bytes 4194304 | tf_op jit(solution)/shard_map/convert_element_type | solution.py:21
  197.5 1.5 copy-done.13
  199.0 1.5 copy_bitcast_fusion.2
  200.6 1.0 copy-done.14
  202.1 3.1 %collective-permute-start.7 = (bf16[128,1024]{1,0:T(8,128)(2,1)S(1)}, bf16[128,1024]{1,0:T(8,128)(2,1)S(1)}, u32[]{:S(2)}, u32[]{:S(2)}) collective-permute-start(bf16[128,1024]{1,0:T(8,128)(2,1)S(1)} %get-tuple-element.332), channel_id=1, source_target_pairs={{0,16},{8,24},{16,32},{24,40},{32,48},{40,56},{48,64},{56,72},{64,... | collective-permute-start | bytes 786440 | tf_op jit(solution)/shard_map/ppermute | solution.py:17
  205.2 7.4 %collective-permute-start.6 = (bf16[128,1024]{1,0:T(8,128)(2,1)S(1)}, bf16[128,1024]{1,0:T(8,128)(2,1)S(1)}, u32[]{:S(2)}, u32[]{:S(2)}) collective-permute-start(bf16[128,1024]{1,0:T(8,128)(2,1)S(1)} %get-tuple-element.331), channel_id=1, source_target_pairs={{0,752},{8,760},{16,0},{24,8},{32,16},{40,24},{48,32},{56,40},{64,... | collective-permute-start | bytes 786440 | tf_op jit(solution)/shard_map/ppermute | solution.py:17
  213.0 1.9 collective-permute-start.5
  214.9 2.9 collective-permute-start.4
  220.6 1.0 gather_fusion.7
  221.6 1.0 gather_fusion.6
  224.3 16.1 %reduce-scatter.5.cloned.1.call-done = bf16[256,512]{1,0:T(8,128)(2,1)} async-done(((bf16[2048,512]{1,0:T(8,128)(2,1)}), bf16[256,512]{1,0:T(8,128)(2,1)}) %reduce-scatter.5.cloned.1.call-update) | async-done | bytes 262160 | tf_op jit(solution)/shard_map/reduce_scatter | solution.py:150
  240.4 49.4 %reduce-scatter.3.cloned.1.call-done = bf16[256,512]{1,0:T(8,128)(2,1)} async-done(((bf16[2048,512]{1,0:T(8,128)(2,1)}), bf16[256,512]{1,0:T(8,128)(2,1)}) %reduce-scatter.3.cloned.1.call-update) | async-done | bytes 262160 | tf_op jit(solution)/shard_map/reduce_scatter | solution.py:144
  289.8 2.0 fusion.16
  (407 shorter events, 62.0 us)
Async XLA Ops:
  7.2 28.1 %copy-start.18 = (s32[2,6]{1,0:T(2,128)S(1)}, s32[2,6]{1,0:T(2,128)}, u32[]{:S(2)}) copy-start(s32[2,6]{1,0:T(2,128)} %param.14) | copy-start | bytes 148
  7.2 28.2 %copy-start.26 = (s32[2,256]{1,0:T(2,128)S(1)}, s32[2,256]{1,0:T(2,128)}, u32[]{:S(2)}) copy-start(s32[2,256]{1,0:T(2,128)} %param.13) | copy-start | bytes 6148
  7.2 28.3 %copy-start.27 = (s32[2]{0:T(128)S(1)}, s32[2]{0:T(128)}, u32[]{:S(2)}) copy-start(s32[2]{0:T(128)} %param.15) | copy-start | bytes 28
  7.2 70.7 %all-gather.2.cloned.1.call-start = ((), (), s32[]{:S(2)}) async-start(), calls=%async_computation.2 | async-start | bytes 4718592 | tf_op jit(solution)/shard_map/all_gather | solution.py:58
  10.0 230.4 %reduce-scatter.5.cloned.1.call-start = ((), (), s32[]{:S(2)}) async-start(), calls=%async_computation.4 | async-start | bytes 2359296 | tf_op jit(solution)/shard_map/reduce_scatter | solution.py:150
  11.2 24.4 %collective-permute-start.3 = (bf16[128,1024]{1,0:T(8,128)(2,1)S(1)}, bf16[128,1024]{1,0:T(8,128)(2,1)S(1)}, u32[]{:S(2)}, u32[]{:S(2)}) collective-permute-start(bf16[128,1024]{1,0:T(8,128)(2,1)S(1)} %get-tuple-element.334), channel_id=1, source_target_pairs={{0,16},{8,24},{16,32},{24,40},{32,48},{40,56},{48,64},{56,72},{64,... | collective-permute-start | bytes 786440 | tf_op jit(solution)/shard_map/ppermute | solution.py:17
  15.1 23.1 %collective-permute-start.1 = (bf16[128,1024]{1,0:T(8,128)(2,1)S(1)}, bf16[128,1024]{1,0:T(8,128)(2,1)S(1)}, u32[]{:S(2)}, u32[]{:S(2)}) collective-permute-start(bf16[128,1024]{1,0:T(8,128)(2,1)S(1)} %get-tuple-element.334), channel_id=1, source_target_pairs={{0,8},{8,16},{16,24},{24,32},{32,40},{40,48},{48,56},{56,64},{64,7... | collective-permute-start | bytes 786440 | tf_op jit(solution)/shard_map/ppermute | solution.py:17
  19.1 18.2 %collective-permute-start.2 = (bf16[128,1024]{1,0:T(8,128)(2,1)S(1)}, bf16[128,1024]{1,0:T(8,128)(2,1)S(1)}, u32[]{:S(2)}, u32[]{:S(2)}) collective-permute-start(bf16[128,1024]{1,0:T(8,128)(2,1)S(1)} %get-tuple-element.333), channel_id=1, source_target_pairs={{0,752},{8,760},{16,0},{24,8},{32,16},{40,24},{48,32},{56,40},{64,... | collective-permute-start | bytes 786440 | tf_op jit(solution)/shard_map/ppermute | solution.py:17
  32.4 8.1 %collective-permute-start = (bf16[128,1024]{1,0:T(8,128)(2,1)S(1)}, bf16[128,1024]{1,0:T(8,128)(2,1)S(1)}, u32[]{:S(2)}, u32[]{:S(2)}) collective-permute-start(bf16[128,1024]{1,0:T(8,128)(2,1)S(1)} %get-tuple-element.333), channel_id=1, source_target_pairs={{0,760},{8,0},{16,8},{24,16},{32,24},{40,32},{48,40},{56,48},{64,5... | collective-permute-start | bytes 786440 | tf_op jit(solution)/shard_map/ppermute | solution.py:17
  35.4 2.8 copy-start.24
  35.4 2.8 copy-start.25
  35.4 2.8 copy-start.23
  35.4 5.0 %copy-start.22 = (s32[1024]{0:T(1024)}, s32[1024]{0:T(1024)S(1)}, u32[]{:S(2)}) copy-start(s32[1024]{0:T(1024)S(1)} %get-tuple-element.342) | copy-start | bytes 12292
  86.2 6.4 %copy-start.20 = (pred[2,6]{1,0:T(4,128)(4,1)}, pred[2,6]{1,0:T(4,128)(4,1)S(1)}, u32[]{:S(2)}) copy-start(pred[2,6]{1,0:T(4,128)(4,1)S(1)} %get-tuple-element.525) | copy-start | bytes 40 | tf_op jit(solution)/shard_map/while
  90.5 7.4 %copy-start.3 = (bf16[2,768,2,64]{1,3,2,0:T(8,128)(2,1)}, bf16[2,768,2,64]{1,3,2,0:T(8,128)(2,1)S(1)}, u32[]{:S(2)}) copy-start(bf16[2,768,2,64]{1,3,2,0:T(8,128)(2,1)S(1)} %reshape.399) | copy-start | bytes 1179652 | tf_op jit(solution)/shard_map/while
  91.6 6.3 %copy-start = (bf16[2,128,2,64]{1,0,3,2:T(2,128)(2,1)}, bf16[2,128,2,64]{1,0,3,2:T(2,128)(2,1)S(1)}, u32[]{:S(2)}) copy-start(bf16[2,128,2,64]{1,0,3,2:T(2,128)(2,1)S(1)} %reshape.400) | copy-start | bytes 196612 | tf_op jit(solution)/shard_map/while
  92.6 2.3 copy-start.8
  97.9 1.7 copy-start.1
  97.9 1.8 copy-start.7
  97.9 1.9 copy-start.5
  99.6 1.8 copy-start.2
  99.6 2.1 copy-start.10
  100.1 2.6 copy-start.19
  104.7 1.5 copy-start.9
  113.3 6.4 %copy-start.20 = (pred[2,6]{1,0:T(4,128)(4,1)}, pred[2,6]{1,0:T(4,128)(4,1)S(1)}, u32[]{:S(2)}) copy-start(pred[2,6]{1,0:T(4,128)(4,1)S(1)} %get-tuple-element.525) | copy-start | bytes 40 | tf_op jit(solution)/shard_map/while
  117.5 7.4 %copy-start.3 = (bf16[2,768,2,64]{1,3,2,0:T(8,128)(2,1)}, bf16[2,768,2,64]{1,3,2,0:T(8,128)(2,1)S(1)}, u32[]{:S(2)}) copy-start(bf16[2,768,2,64]{1,3,2,0:T(8,128)(2,1)S(1)} %reshape.399) | copy-start | bytes 1179652 | tf_op jit(solution)/shard_map/while
  118.6 6.3 %copy-start = (bf16[2,128,2,64]{1,0,3,2:T(2,128)(2,1)}, bf16[2,128,2,64]{1,0,3,2:T(2,128)(2,1)S(1)}, u32[]{:S(2)}) copy-start(bf16[2,128,2,64]{1,0,3,2:T(2,128)(2,1)S(1)} %reshape.400) | copy-start | bytes 196612 | tf_op jit(solution)/shard_map/while
  119.7 2.3 copy-start.8
  124.9 1.7 copy-start.1
  124.9 1.8 copy-start.7
  125.0 1.9 copy-start.5
  126.6 1.8 copy-start.2
  126.6 2.1 copy-start.10
  127.1 2.6 copy-start.19
  131.8 1.5 copy-start.9
  140.3 6.4 %copy-start.20 = (pred[2,6]{1,0:T(4,128)(4,1)}, pred[2,6]{1,0:T(4,128)(4,1)S(1)}, u32[]{:S(2)}) copy-start(pred[2,6]{1,0:T(4,128)(4,1)S(1)} %get-tuple-element.525) | copy-start | bytes 40 | tf_op jit(solution)/shard_map/while
  144.5 7.4 %copy-start.3 = (bf16[2,768,2,64]{1,3,2,0:T(8,128)(2,1)}, bf16[2,768,2,64]{1,3,2,0:T(8,128)(2,1)S(1)}, u32[]{:S(2)}) copy-start(bf16[2,768,2,64]{1,3,2,0:T(8,128)(2,1)S(1)} %reshape.399) | copy-start | bytes 1179652 | tf_op jit(solution)/shard_map/while
  145.6 6.3 %copy-start = (bf16[2,128,2,64]{1,0,3,2:T(2,128)(2,1)}, bf16[2,128,2,64]{1,0,3,2:T(2,128)(2,1)S(1)}, u32[]{:S(2)}) copy-start(bf16[2,128,2,64]{1,0,3,2:T(2,128)(2,1)S(1)} %reshape.400) | copy-start | bytes 196612 | tf_op jit(solution)/shard_map/while
  146.7 2.3 copy-start.8
  151.9 1.7 copy-start.1
  152.0 1.8 copy-start.7
  152.0 1.9 copy-start.5
  153.6 1.8 copy-start.2
  153.6 2.1 copy-start.10
  154.1 2.6 copy-start.19
  158.8 1.5 copy-start.9
  167.3 6.4 %copy-start.20 = (pred[2,6]{1,0:T(4,128)(4,1)}, pred[2,6]{1,0:T(4,128)(4,1)S(1)}, u32[]{:S(2)}) copy-start(pred[2,6]{1,0:T(4,128)(4,1)S(1)} %get-tuple-element.525) | copy-start | bytes 40 | tf_op jit(solution)/shard_map/while
  171.5 7.4 %copy-start.3 = (bf16[2,768,2,64]{1,3,2,0:T(8,128)(2,1)}, bf16[2,768,2,64]{1,3,2,0:T(8,128)(2,1)S(1)}, u32[]{:S(2)}) copy-start(bf16[2,768,2,64]{1,3,2,0:T(8,128)(2,1)S(1)} %reshape.399) | copy-start | bytes 1179652 | tf_op jit(solution)/shard_map/while
  172.6 6.3 %copy-start = (bf16[2,128,2,64]{1,0,3,2:T(2,128)(2,1)}, bf16[2,128,2,64]{1,0,3,2:T(2,128)(2,1)S(1)}, u32[]{:S(2)}) copy-start(bf16[2,128,2,64]{1,0,3,2:T(2,128)(2,1)S(1)} %reshape.400) | copy-start | bytes 196612 | tf_op jit(solution)/shard_map/while
  173.7 2.3 copy-start.8
  179.0 1.7 copy-start.1
  179.0 1.8 copy-start.7
  179.0 1.9 copy-start.5
  180.6 1.8 copy-start.2
  180.6 2.1 copy-start.10
  181.1 2.6 copy-start.19
  197.5 1.6 copy-start.13
  197.5 92.3 %reduce-scatter.3.cloned.1.call-start = ((), (), s32[]{:S(2)}) async-start(), calls=%async_computation.3 | async-start | bytes 2359296 | tf_op jit(solution)/shard_map/reduce_scatter | solution.py:144
  201.9 16.0 %copy-start.16 = (bf16[4,256,128]{1,2,0:T(8,128)(2,1)S(1)}, bf16[4,256,128]{1,2,0:T(8,128)(2,1)}, u32[]{:S(2)}) copy-start(bf16[4,256,128]{1,2,0:T(8,128)(2,1)} %get-tuple-element.182) | copy-start | bytes 786436
  201.9 16.9 %copy-start.17 = (bf16[4,256,128]{1,2,0:T(8,128)(2,1)S(1)}, bf16[4,256,128]{1,2,0:T(8,128)(2,1)}, u32[]{:S(2)}) copy-start(bf16[4,256,128]{1,2,0:T(8,128)(2,1)} %get-tuple-element.183) | copy-start | bytes 786436
  202.1 17.5 %collective-permute-start.7 = (bf16[128,1024]{1,0:T(8,128)(2,1)S(1)}, bf16[128,1024]{1,0:T(8,128)(2,1)S(1)}, u32[]{:S(2)}, u32[]{:S(2)}) collective-permute-start(bf16[128,1024]{1,0:T(8,128)(2,1)S(1)} %get-tuple-element.332), channel_id=1, source_target_pairs={{0,16},{8,24},{16,32},{24,40},{32,48},{40,56},{48,64},{56,72},{64,... | collective-permute-start | bytes 786440 | tf_op jit(solution)/shard_map/ppermute | solution.py:17
  205.2 15.4 %collective-permute-start.6 = (bf16[128,1024]{1,0:T(8,128)(2,1)S(1)}, bf16[128,1024]{1,0:T(8,128)(2,1)S(1)}, u32[]{:S(2)}, u32[]{:S(2)}) collective-permute-start(bf16[128,1024]{1,0:T(8,128)(2,1)S(1)} %get-tuple-element.331), channel_id=1, source_target_pairs={{0,752},{8,760},{16,0},{24,8},{32,16},{40,24},{48,32},{56,40},{64,... | collective-permute-start | bytes 786440 | tf_op jit(solution)/shard_map/ppermute | solution.py:17
  213.0 8.6 %collective-permute-start.5 = (bf16[128,1024]{1,0:T(8,128)(2,1)S(1)}, bf16[128,1024]{1,0:T(8,128)(2,1)S(1)}, u32[]{:S(2)}, u32[]{:S(2)}) collective-permute-start(bf16[128,1024]{1,0:T(8,128)(2,1)S(1)} %get-tuple-element.326), channel_id=1, source_target_pairs={{0,8},{8,16},{16,24},{24,32},{32,40},{40,48},{48,56},{56,64},{64,7... | collective-permute-start | bytes 786440 | tf_op jit(solution)/shard_map/ppermute | solution.py:17
  214.9 8.1 %collective-permute-start.4 = (bf16[128,1024]{1,0:T(8,128)(2,1)S(1)}, bf16[128,1024]{1,0:T(8,128)(2,1)S(1)}, u32[]{:S(2)}, u32[]{:S(2)}) collective-permute-start(bf16[128,1024]{1,0:T(8,128)(2,1)S(1)} %get-tuple-element.325), channel_id=1, source_target_pairs={{0,760},{8,0},{16,8},{24,16},{32,24},{40,32},{48,40},{56,48},{64,5... | collective-permute-start | bytes 786440 | tf_op jit(solution)/shard_map/ppermute | solution.py:17
  (20 other events, 18.6 us)
Sparse Core Ops, SparseCore 0:
  10.4 67.4 all-gather.1
  197.6 42.7 reduce-scatter.4
  243.5 46.1 reduce-scatter.2
where the time goes:
time: 303 us; the launch traced here: 298 us
  waiting for transfers between devices  103 us (34%)
  local copies, waits for them, and re-layouts  93.7 us (31%)
  starting transfers between devices  39.6 us (13%)
  other arithmetic  23.4 us (8%)
  matrix products  19.6 us (6%)
  between operations  14.2 us (5%)
  loops' own time  4.65 us (2%)
    reduce_scatter x1, waiting for transfers between devices, shards(): lax.psum_scatter(settle(join_heads(outputs[6])).astype(jnp.bfloat16), 'bl...  49.4 us
    ppermute x8, starting transfers between devices, passed_along(): return lax.ppermute(x, axis, [(i, (i + by) % size) for i in range(size)])  39.5 us
    all_gather x1, waiting for transfers between devices, shards(): cluster_rows = lax.all_gather(both, 'blk', axis=0, tiled=True)  34.8 us
    reduce_scatter x1, waiting for transfers between devices, shards(): lax.psum_scatter(settle(join_heads(outputs[7])).astype(jnp.bfloat16), 'bl...  16.1 us
    reshape x8, local copies, waits for them, and re-layouts, head_group(): c_key = (jnp.einsum('bhqk,bqhd->bkhd', z_loc, q_part, preferred_element_t...  13 us
    unnamed x29, local copies, waits for them, and re-layouts  10.7 us
    dynamic_update_slice x12, local copies, waits for them, and re-layouts, shards(): outputs = lax.map(head_group, jnp.arange(groups, dtype=jnp.int32))  10.1 us
    gather x8, local copies, waits for them, and re-layouts, fetch_partners(): return jnp.concatenate([ahead[slots[:half]], behind[slots[half:]]], 0)  7.37 us
  transfers between devices with their start and end apart: 11, of which 6 were waited for; matrix products, arithmetic and copies ran while one was open for 5% of the time, Pallas kernels for 0%

commit v1 on v0

v1 whole, which is shorter than its diff:
```python
import jax
import jax.numpy as jnp
from jax import lax
from jax.sharding import PartitionSpec as P

HEADS = 8
BLOCK = 128
TMAX = 6
ROUNDS = 2


NEG_BIG = -1e30


def passed_along(x, axis, by):
    size = lax.axis_size(axis)
    return lax.ppermute(x, axis, [(i, (i + by) % size) for i in range(size)])


def fetch_partners(load, slots, offset):
    half = load.shape[0] // 2
    ahead = passed_along(load[half:], "grp", -offset)
    behind = passed_along(load[:half], "grp", offset)
    return jnp.concatenate([ahead[slots[:half]], behind[slots[half:]]], 0)


def shards(query, key, value, out_grad, partner, tiles, tile_count):
    f32 = jnp.float32
    bf16 = jnp.bfloat16
    nodes, width = query.shape
    head_dim = width // HEADS
    scale = head_dim ** (-0.5)
    blocks_dev = nodes // BLOCK
    team = lax.axis_size("blk")
    cluster_blocks = blocks_dev * team
    keys_tile = TMAX * BLOCK
    heads4 = (blocks_dev, BLOCK, HEADS, head_dim)

    both = jnp.concatenate([key, value], 1)
    kv_cluster = lax.all_gather(both, "blk", axis=0, tiled=True)
    qg_cluster = lax.all_gather(jnp.concatenate([query, out_grad], 1), "blk", axis=0, tiled=True)
    partner_rows = jnp.stack(
        [fetch_partners(both, partner[step], step + 1) for step in range(ROUNDS)]
    )
    live = jnp.arange(TMAX, dtype=jnp.int32)[None, :] < tile_count[:, None]
    tile_live = jnp.broadcast_to(live[:, :, None], (blocks_dev, TMAX, BLOCK)).reshape(
        blocks_dev, keys_tile
    )

    kv_tiles = kv_cluster.reshape(cluster_blocks, BLOCK, 2 * width)[tiles].reshape(
        blocks_dev, keys_tile, 2 * width
    )
    k_tile = kv_tiles[..., :width].reshape(blocks_dev, keys_tile, HEADS, head_dim)
    v_tile = kv_tiles[..., width:].reshape(blocks_dev, keys_tile, HEADS, head_dim)
    pair_shape = (ROUNDS,) + heads4
    k_pair = partner_rows[..., :width].reshape(pair_shape)
    v_pair = partner_rows[..., width:].reshape(pair_shape)
    q4 = query.reshape(heads4)
    g4 = out_grad.reshape(heads4)

    s_loc = jnp.einsum("bqhd,bkhd->bhqk", q4, k_tile, preferred_element_type=f32) * scale
    s_loc = jnp.where(tile_live[:, None, None, :], s_loc, NEG_BIG)
    s_pair = jnp.einsum("bqhd,rbqhd->bhqr", q4, k_pair, preferred_element_type=f32) * scale
    top = jnp.maximum(jnp.max(s_loc, -1), jnp.max(s_pair, -1))
    e_loc = jnp.exp(s_loc - top[..., None])
    e_pair = jnp.exp(s_pair - top[..., None])
    total = jnp.sum(e_loc, -1) + jnp.sum(e_pair, -1)
    p_loc = e_loc / total[..., None]
    p_pair = e_pair / total[..., None]
    w_loc = p_loc.astype(bf16)
    w_pair = p_pair.astype(bf16)
    out_full = jnp.einsum("bhqk,bkhd->bqhd", w_loc, v_tile, preferred_element_type=f32)
    out_full = out_full + jnp.einsum("bhqr,rbqhd->bqhd", w_pair, v_pair, preferred_element_type=f32)
    delta = jnp.transpose(jnp.sum(g4.astype(f32) * out_full, -1), (0, 2, 1))
    d_loc = jnp.einsum("bqhd,bkhd->bhqk", g4, v_tile, preferred_element_type=f32)
    d_pair = jnp.einsum("bqhd,rbqhd->bhqr", g4, v_pair, preferred_element_type=f32)
    z_loc = (p_loc * (d_loc - delta[..., None])).astype(bf16)
    z_pair = (p_pair * (d_pair - delta[..., None])).astype(bf16)
    q_grad = jnp.einsum("bhqk,bkhd->bqhd", z_loc, k_tile, preferred_element_type=f32)
    q_grad = (
        q_grad + jnp.einsum("bhqr,rbqhd->bqhd", z_pair, k_pair, preferred_element_type=f32)
    ) * scale
    t_key = (
        jnp.einsum("bhqr,bqhd->rbqhd", z_pair, q4, preferred_element_type=f32) * scale
    ).astype(bf16)
    t_val = jnp.einsum("bhqr,bqhd->rbqhd", w_pair, g4, preferred_element_type=f32).astype(bf16)
    terms = jnp.concatenate(
        [t_key.reshape(ROUNDS, nodes, width), t_val.reshape(ROUNDS, nodes, width)], 2
    )
    returned = jnp.stack(
        [fetch_partners(terms[step], partner[step], step + 1) for step in range(ROUNDS)]
    )
    returned = jnp.sum(returned.astype(f32), 0)

    stats = jnp.stack([top, total, delta], 1)
    stats = jnp.transpose(stats, (0, 3, 1, 2)).reshape(nodes, 3 * HEADS)
    stats_cluster = lax.all_gather(stats, "blk", axis=0, tiled=True)

    qg_tiles = qg_cluster.reshape(cluster_blocks, BLOCK, 2 * width)[tiles].reshape(
        blocks_dev, keys_tile, 2 * width
    )
    q_tile = qg_tiles[..., :width].reshape(blocks_dev, keys_tile, HEADS, head_dim)
    g_tile = qg_tiles[..., width:].reshape(blocks_dev, keys_tile, HEADS, head_dim)
    st = stats_cluster.reshape(cluster_blocks, BLOCK, 3, HEADS)[tiles].reshape(
        blocks_dev, keys_tile, 3, HEADS
    )
    st = jnp.transpose(st, (0, 2, 3, 1))
    top_t, total_t, delta_t = st[:, 0], st[:, 1], st[:, 2]
    k4 = key.reshape(heads4)
    v4 = value.reshape(heads4)
    s_key = jnp.einsum("bkhd,bqhd->bhkq", k4, q_tile, preferred_element_type=f32) * scale
    s_key = jnp.where(tile_live[:, None, None, :], s_key, NEG_BIG)
    p_key = jnp.exp(s_key - top_t[:, :, None, :]) / total_t[:, :, None, :]
    w_key = p_key.astype(bf16)
    d_key = jnp.einsum("bkhd,bqhd->bhkq", v4, g_tile, preferred_element_type=f32)
    z_key = (p_key * (d_key - delta_t[:, :, None, :])).astype(bf16)
    k_sum = jnp.einsum("bhkq,bqhd->bkhd", z_key, q_tile, preferred_element_type=f32) * scale
    v_sum = jnp.einsum("bhkq,bqhd->bkhd", w_key, g_tile, preferred_element_type=f32)

    attended = out_full.reshape(nodes, width).astype(bf16)
    query_grad = q_grad.reshape(nodes, width).astype(bf16)
    key_grad = (k_sum.reshape(nodes, width) + returned[:, :width]).astype(bf16)
    value_grad = (v_sum.reshape(nodes, width) + returned[:, width:]).astype(bf16)
    return (attended, query_grad, key_grad, value_grad)


def solution(mesh):
    in_specs = (
        P(("grp", "blk"), None),
        P(("grp", "blk"), None),
        P(("grp", "blk"), None),
        P(("grp", "blk"), None),
        P(None, ("grp", "blk")),
        P(("grp", "blk"), None),
        P(("grp", "blk")),
    )
    out_specs = (
        P(("grp", "blk"), None),
        P(("grp", "blk"), None),
        P(("grp", "blk"), None),
        P(("grp", "blk"), None),
    )
    return jax.shard_map(shards, mesh=mesh, in_specs=in_specs, out_specs=out_specs, check_vma=False)
```

time: 303 us -> 232 us (0.77)
  local copies, waits for them, and re-layouts: 93.7 us -> 43.5 us
  waiting for transfers between devices: 103 us -> 58.5 us
  blocking collectives: 0 us -> 18.7 us
  matrix products: 19.6 us -> 32.6 us
  other arithmetic: 23.4 us -> 15.1 us
  starting transfers between devices: 39.6 us -> 45.3 us
  loops' own time: 4.65 us -> 0 us
    reduce_scatter x2 -> x0, waiting for transfers between devices: 65.4 us -> none  [the longest x1 49.4 us: shards(): lax.psum_scatter(settle(join_heads(outputs[6])).astype(jnp.bfloat16), 'bl...]
    all_gather x1 -> x2, waiting for transfers between devices: 34.8 us -> 58.4 us  [the longest x1 31.8 us: shards(): lax.all_gather(jnp.concatenate([query, out_grad], 1), 'blk', axis=0, tile...]
    dynamic_slice x28 -> x0, local copies, waits for them, and re-layouts: 22.7 us -> none  [the longest x4 5.57 us: head_group(): lax.dynamic_slice_in_dim(tiled, left, span, 3)]
    all_gather x0 -> x1, blocking collectives: none -> 18.7 us  [shards(): stats_cluster = lax.all_gather(stats, 'blk', axis=0, tiled=True)]
    reshape x40 -> x16, local copies, waits for them, and re-layouts: 23.9 us -> 5.98 us  [the longest x2 1.38 us: shards(): t_key.reshape(ROUNDS, nodes, width)]
    slice x3 -> x9, local copies, waits for them, and re-layouts: 1.14 us -> 14.1 us  [the longest x2 3.75 us: shards(): kv_tiles[..., :width].reshape(blocks_dev, keys_tile, HEADS, head_dim)]
    dot_general x24 -> x6, matrix products: 19.6 us -> 32.6 us  [the longest x1 7.32 us: shards(): jnp.einsum('bkhd,bqhd->bhkq', k4, q_tile, preferred_element_type=f32)]
    scatter-add x8 -> x0, other arithmetic: 11.1 us -> none  [the longest x4 5.54 us: head_group(): empty.at[tiles].add(c_val).reshape(cluster_blocks * BLOCK, span)]
  transfers between devices with their start and end apart: 11 -> 10, of which waited for: 6 -> 2; matrix products, arithmetic and copies ran while one was open for 5% -> 31% of each run, Pallas kernels for 0% -> 0%
where the time goes in v1:
time: 232 us; the launch traced here: 228 us
  waiting for transfers between devices  58.5 us (25%)
  starting transfers between devices  45.3 us (20%)
  local copies, waits for them, and re-layouts  43.5 us (19%)
  matrix products  32.6 us (14%)
  blocking collectives  18.7 us (8%)
  other arithmetic  15.1 us (7%)
  between operations  14.8 us (6%)
    ppermute x8, starting transfers between devices, passed_along(): return lax.ppermute(x, axis, [(i, (i + by) % size) for i in range(size)])  45.2 us
    all_gather x1, waiting for transfers between devices, shards(): lax.all_gather(jnp.concatenate([query, out_grad], 1), 'blk', axis=0, tile...  31.8 us
    all_gather x1, waiting for transfers between devices, shards(): kv_cluster = lax.all_gather(both, 'blk', axis=0, tiled=True)  26.6 us
    all_gather x1, blocking collectives, shards(): stats_cluster = lax.all_gather(stats, 'blk', axis=0, tiled=True)  18.7 us
    unnamed x52, local copies, waits for them, and re-layouts  7.68 us
    dot_general x1, matrix products, shards(): jnp.einsum('bkhd,bqhd->bhkq', k4, q_tile, preferred_element_type=f32)  7.32 us
    gather x8, local copies, waits for them, and re-layouts, fetch_partners(): return jnp.concatenate([ahead[slots[:half]], behind[slots[half:]]], 0)  6.89 us
    dot_general x1, matrix products, shards(): jnp.einsum('bhqk,bkhd->bqhd', z_loc, k_tile, preferred_element_type=f32)  6.74 us
  transfers between devices with their start and end apart: 10, of which 2 were waited for; matrix products, arithmetic and copies ran while one was open for 31% of the time, Pallas kernels for 0%

profile of v1, /device:TPU:1, one launch (start us, length us, event | category | flops | bytes accessed | tf_op | source)
XLA Modules:
  0.0 228.4 jit_solution(12094623230351822690)
XLA Ops:
  7.3 1.0 constant_dynamic-update-slice_fusion.1
  8.3 1.0 constant_dynamic-update-slice_fusion
  9.3 0.8 copy-done.6
  10.2 1.9 fusion.72
  12.1 3.9 %collective-permute-start.3 = (bf16[128,1024]{1,0:T(8,128)(2,1)}, bf16[128,1024]{1,0:T(8,128)(2,1)S(1)}, u32[]{:S(2)}, u32[]{:S(2)}) collective-permute-start(bf16[128,1024]{1,0:T(8,128)(2,1)} %get-tuple-element.39), channel_id=1, source_target_pairs={{0,16},{8,24},{16,32},{24,40},{32,48},{40,56},{48,64},{56,72},{64,... | collective-permute-start | bytes 786440 | tf_op jit(solution)/shard_map/ppermute | solution.py:17
  16.0 4.0 %collective-permute-start.1 = (bf16[128,1024]{1,0:T(8,128)(2,1)}, bf16[128,1024]{1,0:T(8,128)(2,1)S(1)}, u32[]{:S(2)}, u32[]{:S(2)}) collective-permute-start(bf16[128,1024]{1,0:T(8,128)(2,1)} %get-tuple-element.39), channel_id=1, source_target_pairs={{0,8},{8,16},{16,24},{24,32},{32,40},{40,48},{48,56},{56,64},{64,7... | collective-permute-start | bytes 786440 | tf_op jit(solution)/shard_map/ppermute | solution.py:17
  20.0 13.3 %collective-permute-start.2 = (bf16[128,1024]{1,0:T(8,128)(2,1)}, bf16[128,1024]{1,0:T(8,128)(2,1)S(1)}, u32[]{:S(2)}, u32[]{:S(2)}) collective-permute-start(bf16[128,1024]{1,0:T(8,128)(2,1)} %get-tuple-element.38), channel_id=1, source_target_pairs={{0,752},{8,760},{16,0},{24,8},{32,16},{40,24},{48,32},{56,40},{64,... | collective-permute-start | bytes 786440 | tf_op jit(solution)/shard_map/ppermute | solution.py:17
  33.3 2.9 %collective-permute-start = (bf16[128,1024]{1,0:T(8,128)(2,1)}, bf16[128,1024]{1,0:T(8,128)(2,1)S(1)}, u32[]{:S(2)}, u32[]{:S(2)}) collective-permute-start(bf16[128,1024]{1,0:T(8,128)(2,1)} %get-tuple-element.38), channel_id=1, source_target_pairs={{0,760},{8,0},{16,8},{24,16},{32,24},{40,32},{48,40},{56,48},{64,5... | collective-permute-start | bytes 786440 | tf_op jit(solution)/shard_map/ppermute | solution.py:17
  36.1 1.9 pad_maximum_fusion.1
  39.0 1.1 reshape.383
  40.1 1.1 reshape.384
  41.3 1.2 copy.153
  42.5 1.2 fusion.73
  43.7 0.9 gather_fusion.4
  44.6 0.9 gather_fusion.3
  45.5 0.9 gather_fusion.2
  46.4 0.9 gather_fusion.1
  47.3 0.9 pad_maximum_fusion
  48.5 1.4 copy.133
  50.1 0.6 multiply_reduce_fusion.3
  50.7 0.6 multiply_reduce_fusion.1
  51.3 26.6 %all-gather.3.cloned.1.call-done = bf16[2048,1024]{1,0:T(8,128)(2,1)} async-done(((bf16[256,1024]{1,0:T(8,128)(2,1)}), bf16[2048,1024]{1,0:T(8,128)(2,1)}) %all-gather.3.cloned.1.call-update) | async-done | bytes 4194320 | tf_op jit(solution)/shard_map/all_gather | solution.py:40
  77.9 2.9 %gather_fusion = bf16[12,128,1024]{2,1,0:T(8,128)(2,1)S(1)} fusion(bf16[16,128,1024]{2,1,0:T(8,128)(2,1)} %bitcast.177, s32[1024]{0:T(1024)S(1)} %pad_clamp_fusion.4), kind=kCustom, calls=%fused_computation | custom fusion | bytes 6291504 | tf_op jit(solution)/shard_map/gather | solution.py:50
  80.8 2.0 fusion.71
  82.8 1.8 copy.124
  84.6 1.9 bitcast_reduce_fusion
  86.5 1.4 fusion.3
  88.0 1.1 copy-done
  89.1 1.6 copy.123
  90.7 2.0 multiply_reduce_fusion.2
  92.8 6.2 %multiply_reduce_fusion.4 = (f32[2,128,8]{1,2,0:T(8,128)S(1)}, bf16[2,128,8,64]{1,3,2,0:T(8,128)(2,1)}) fusion(bf16[2,128,8,64]{1,0,3,2:T(2,128)(2,1)S(1)} %reshape.262, f32[2,128,8,64]{1,0,3,2:T(2,128)S(1)} %multiply_reduce_fusion.2, bf16[2,768,8,64]{1,3,2,0:T(8,128)(2,1)} %bitcast.178, f32[2,8,128]{2,1,0:T(8,128)S(1)} %copy_add_fusion, ...), kind=kOutput, calls=%fused_computation.70 | convolution fusion | flops 209844224 | bytes 8939008 | tf_op jit(solution)/shard_map/bhqk,bkhd->bqhd/dot_general | solution.py:72
  99.1 1.6 multiply_reduce_fusion
  100.7 6.7 %fusion.37 = bf16[2,128,8,64]{1,3,2,0:T(8,128)(2,1)} fusion(bf16[2,768,8,64]{1,3,2,0:T(8,128)(2,1)S(1)} %bitcast.175, f32[2,8,128]{2,1,0:T(8,128)S(1)} %bitcast.191, bf16[2,768,8,64]{1,3,2,0:T(8,128)(2,1)S(1)} %bitcast.179, f32[2,8,768,128]{3,2,1,0:T(8,128)} %copy-done, f32[2,8,128]{2,1,0:T(8,128)S(1)} %copy_add_fusion, ...), kind=kOutput, calls=%fused_computation.46 | convolution fusion | flops 414056448 | bytes 10511872 | tf_op jit(solution)/shard_map/bhqk,bkhd->bqhd/dot_general | solution.py:79
  107.4 31.8 %all-gather.5.cloned.1.call-done = bf16[2048,1024]{1,0:T(8,128)(2,1)} async-done(((bf16[256,1024]{1,0:T(8,128)(2,1)}), bf16[2048,1024]{1,0:T(8,128)(2,1)}) %all-gather.5.cloned.1.call-update) | async-done | bytes 4194320 | tf_op jit(solution)/shard_map/all_gather | solution.py:41
  139.2 2.9 %gather_fusion.5 = bf16[12,128,1024]{2,1,0:T(8,128)(2,1)S(1)} fusion(bf16[16,128,1024]{2,1,0:T(8,128)(2,1)} %bitcast.176, s32[1024]{0:T(1024)S(1)} %pad_clamp_fusion.4), kind=kCustom, calls=%fused_computation.5 | custom fusion | bytes 6291504 | tf_op jit(solution)/shard_map/gather | solution.py:99
  142.2 2.0 fusion.70
  144.1 1.7 copy.148
  145.8 18.7 %all_gather.11 = f32[2048,24]{0,1:T(8,128)S(1)} all-gather(f32[256,24]{0,1:T(8,128)S(1)} %maximum_bitcast_fusion.4), channel_id=1, replica_groups=mesh['grp'=96,'blk'=8] {'blk'}, dimensions={0}, use_global_device_ids=true | all-gather | bytes 221184 | tf_op jit(solution)/shard_map/all_gather | solution.py:97
  164.7 0.6 gather_fusion.6
  165.4 0.6 copy-done.1
  166.1 1.6 copy.141
  167.6 1.6 fusion.42
  169.3 0.3 reshape.273
  169.6 1.0 copy.154
  170.7 0.5 fusion.43
  171.1 0.3 reshape.274
  171.7 1.1 fusion.53
  172.8 3.1 %collective-permute-start.7 = (bf16[128,1024]{1,0:T(8,128)(2,1)}, bf16[128,1024]{1,0:T(8,128)(2,1)S(1)}, u32[]{:S(2)}, u32[]{:S(2)}) collective-permute-start(bf16[128,1024]{1,0:T(8,128)(2,1)} %get-tuple-element.32), channel_id=1, source_target_pairs={{0,16},{8,24},{16,32},{24,40},{32,48},{40,56},{48,64},{56,72},{64,... | collective-permute-start | bytes 786440 | tf_op jit(solution)/shard_map/ppermute | solution.py:17
  175.9 7.3 %collective-permute-start.6 = (bf16[128,1024]{1,0:T(8,128)(2,1)}, bf16[128,1024]{1,0:T(8,128)(2,1)S(1)}, u32[]{:S(2)}, u32[]{:S(2)}) collective-permute-start(bf16[128,1024]{1,0:T(8,128)(2,1)} %get-tuple-element.33), channel_id=1, source_target_pairs={{0,752},{8,760},{16,0},{24,8},{32,16},{40,24},{48,32},{56,40},{64,... | collective-permute-start | bytes 786440 | tf_op jit(solution)/shard_map/ppermute | solution.py:17
  183.2 5.2 %collective-permute-start.5 = (bf16[128,1024]{1,0:T(8,128)(2,1)}, bf16[128,1024]{1,0:T(8,128)(2,1)S(1)}, u32[]{:S(2)}, u32[]{:S(2)}) collective-permute-start(bf16[128,1024]{1,0:T(8,128)(2,1)} %get-tuple-element.31), channel_id=1, source_target_pairs={{0,8},{8,16},{16,24},{24,32},{32,40},{40,48},{48,56},{56,64},{64,7... | collective-permute-start | bytes 786440 | tf_op jit(solution)/shard_map/ppermute | solution.py:17
  188.4 5.6 %collective-permute-start.4 = (bf16[128,1024]{1,0:T(8,128)(2,1)}, bf16[128,1024]{1,0:T(8,128)(2,1)S(1)}, u32[]{:S(2)}, u32[]{:S(2)}) collective-permute-start(bf16[128,1024]{1,0:T(8,128)(2,1)} %get-tuple-element.30), channel_id=1, source_target_pairs={{0,760},{8,0},{16,8},{24,16},{32,24},{40,32},{48,40},{56,48},{64,5... | collective-permute-start | bytes 786440 | tf_op jit(solution)/shard_map/ppermute | solution.py:17
  194.1 7.3 %exponential_divide_fusion = f32[2,8,768,128]{3,2,1,0:T(8,128)} fusion(f32[2,8,768]{2,1,0:T(8,128)S(1)} %copy.147, f32[2,8,768]{2,1,0:T(8,128)S(1)} %copy.146, pred[2,768]{1,0:T(4,128)(4,1)S(1)} %bitcast.189, bf16[2,768,8,64]{1,3,2,0:T(8,128)(2,1)} %bitcast.172, bf16[2,128,8,64]{3,2,1,0:T(8,128)(2,1)} %reshape.383), kind=kOutput, calls=%fused_computation.17 | convolution fusion | flops 207618048 | bytes 8226304 | tf_op jit(solution)/shard_map/bkhd,bqhd->bhkq/dot_general | solution.py:111
  201.4 6.2 %fusion.36 = f32[2,128,8,64]{1,3,2,0:T(8,128)S(1)} fusion(bf16[2,768,8,64]{1,3,2,0:T(8,128)(2,1)} %bitcast.173, f32[2,8,768,128]{3,2,1,0:T(8,128)} %exponential_divide_fusion, f32[2,8,768]{2,1,0:T(8,128)S(1)} %copy.151, bf16[2,768,8,64]{1,3,2,0:T(8,128)(2,1)S(1)} %bitcast.168, bf16[2,128,8,64]{3,2,1,0:T(8,128)(2,1)} %reshape.384), kind=kOutput, calls=%fused_computation.45 | convolution fusion | flops 407502848 | bytes 10272768 | tf_op jit(solution)/shard_map/bhkq,bqhd->bkhd/dot_general | solution.py:117
  207.6 4.2 %fusion.23 = f32[2,128,8,64]{1,3,2,0:T(8,128)} fusion(bf16[2,768,8,64]{1,3,2,0:T(8,128)(2,1)S(1)} %bitcast.169, f32[2,8,768,128]{3,2,1,0:T(8,128)} %exponential_divide_fusion), kind=kOutput, calls=%fused_computation.40 | convolution fusion | flops 202899456 | bytes 8388608 | tf_op jit(solution)/shard_map/bhkq,bqhd->bkhd/dot_general | solution.py:118
  212.2 1.0 reshape.381
  213.2 1.2 copy.194
  214.5 1.0 reshape.382
  215.5 0.4 copy.200
  216.2 0.4 copy.199
  216.8 0.9 gather_fusion.10
  217.7 0.9 gather_fusion.9
  218.6 0.9 gather_fusion.8
  219.5 0.9 gather_fusion.7
  220.6 0.9 fusion.45
  (98 shorter events, 3.4 us)
Async XLA Ops:
  7.2 30.9 %copy-start.15 = (bf16[256,512]{1,0:T(8,128)(2,1)S(1)}, bf16[256,512]{1,0:T(8,128)(2,1)}, u32[]{:S(2)}) copy-start(bf16[256,512]{1,0:T(8,128)(2,1)} %param.10) | copy-start | bytes 786436
  7.2 31.1 %copy-start.20 = (s32[2]{0:T(128)S(1)}, s32[2]{0:T(128)}, u32[]{:S(2)}) copy-start(s32[2]{0:T(128)} %param.13) | copy-start | bytes 28
  7.2 31.3 %copy-start.19 = (s32[2,6]{1,0:T(2,128)S(1)}, s32[2,6]{1,0:T(2,128)}, u32[]{:S(2)}) copy-start(s32[2,6]{1,0:T(2,128)} %param.12) | copy-start | bytes 148
  7.2 31.3 %copy-start.18 = (s32[2,256]{1,0:T(2,128)S(1)}, s32[2,256]{1,0:T(2,128)}, u32[]{:S(2)}) copy-start(s32[2,256]{1,0:T(2,128)} %param.11) | copy-start | bytes 6148
  7.2 70.7 %all-gather.3.cloned.1.call-start = ((), (), s32[]{:S(2)}) async-start(), calls=%async_computation | async-start | bytes 4718592 | tf_op jit(solution)/shard_map/all_gather | solution.py:40
  8.3 30.6 %copy-start.16 = (bf16[256,512]{1,0:T(8,128)(2,1)S(1)}, bf16[256,512]{1,0:T(8,128)(2,1)}, u32[]{:S(2)}) copy-start(bf16[256,512]{1,0:T(8,128)(2,1)} %param.7) | copy-start | bytes 786436
  9.3 0.8 copy-start.6
  9.3 29.7 %copy-start.13 = (bf16[256,512]{1,0:T(8,128)(2,1)S(1)}, bf16[256,512]{1,0:T(8,128)(2,1)}, u32[]{:S(2)}) copy-start(bf16[256,512]{1,0:T(8,128)(2,1)} %param.8) | copy-start | bytes 786436
  10.1 30.0 %copy-start.14 = (bf16[256,512]{1,0:T(8,128)(2,1)S(1)}, bf16[256,512]{1,0:T(8,128)(2,1)}, u32[]{:S(2)}) copy-start(bf16[256,512]{1,0:T(8,128)(2,1)} %param.9) | copy-start | bytes 786436
  10.1 129.1 %all-gather.5.cloned.1.call-start = ((), (), s32[]{:S(2)}) async-start(), calls=%async_computation.1 | async-start | bytes 4718592 | tf_op jit(solution)/shard_map/all_gather | solution.py:41
  12.1 31.7 %collective-permute-start.3 = (bf16[128,1024]{1,0:T(8,128)(2,1)}, bf16[128,1024]{1,0:T(8,128)(2,1)S(1)}, u32[]{:S(2)}, u32[]{:S(2)}) collective-permute-start(bf16[128,1024]{1,0:T(8,128)(2,1)} %get-tuple-element.39), channel_id=1, source_target_pairs={{0,16},{8,24},{16,32},{24,40},{32,48},{40,56},{48,64},{56,72},{64,... | collective-permute-start | bytes 786440 | tf_op jit(solution)/shard_map/ppermute | solution.py:17
  16.0 29.5 %collective-permute-start.1 = (bf16[128,1024]{1,0:T(8,128)(2,1)}, bf16[128,1024]{1,0:T(8,128)(2,1)S(1)}, u32[]{:S(2)}, u32[]{:S(2)}) collective-permute-start(bf16[128,1024]{1,0:T(8,128)(2,1)} %get-tuple-element.39), channel_id=1, source_target_pairs={{0,8},{8,16},{16,24},{24,32},{32,40},{40,48},{48,56},{56,64},{64,7... | collective-permute-start | bytes 786440 | tf_op jit(solution)/shard_map/ppermute | solution.py:17
  20.0 24.6 %collective-permute-start.2 = (bf16[128,1024]{1,0:T(8,128)(2,1)}, bf16[128,1024]{1,0:T(8,128)(2,1)S(1)}, u32[]{:S(2)}, u32[]{:S(2)}) collective-permute-start(bf16[128,1024]{1,0:T(8,128)(2,1)} %get-tuple-element.38), channel_id=1, source_target_pairs={{0,752},{8,760},{16,0},{24,8},{32,16},{40,24},{48,32},{56,40},{64,... | collective-permute-start | bytes 786440 | tf_op jit(solution)/shard_map/ppermute | solution.py:17
  33.3 13.1 %collective-permute-start = (bf16[128,1024]{1,0:T(8,128)(2,1)}, bf16[128,1024]{1,0:T(8,128)(2,1)S(1)}, u32[]{:S(2)}, u32[]{:S(2)}) collective-permute-start(bf16[128,1024]{1,0:T(8,128)(2,1)} %get-tuple-element.38), channel_id=1, source_target_pairs={{0,760},{8,0},{16,8},{24,16},{32,24},{40,32},{48,40},{56,48},{64,5... | collective-permute-start | bytes 786440 | tf_op jit(solution)/shard_map/ppermute | solution.py:17
  41.3 4.2 %copy-start.7 = (bf16[2,128,8,64]{1,0,3,2:T(2,128)(2,1)}, bf16[2,128,8,64]{1,0,3,2:T(2,128)(2,1)S(1)}, u32[]{:S(2)}) copy-start(bf16[2,128,8,64]{1,0,3,2:T(2,128)(2,1)S(1)} %reshape.259) | copy-start | bytes 786436
  48.5 29.3 %copy-start.3 = (bf16[2,2,128,8,64]{2,1,4,3,0:T(2,128)(2,1)}, bf16[2,2,128,8,64]{2,1,4,3,0:T(2,128)(2,1)S(1)}, u32[]{:S(2)}) copy-start(bf16[2,2,128,8,64]{2,1,4,3,0:T(2,128)(2,1)S(1)} %reshape.260) | copy-start | bytes 1572868
  50.1 27.7 %copy-start.5 = (bf16[2,2,128,8,64]{2,1,4,3,0:T(2,128)(2,1)}, bf16[2,2,128,8,64]{2,1,4,3,0:T(2,128)(2,1)S(1)}, u32[]{:S(2)}) copy-start(bf16[2,2,128,8,64]{2,1,4,3,0:T(2,128)(2,1)S(1)} %reshape.261) | copy-start | bytes 1572868
  82.8 1.8 copy-start.8
  86.5 2.7 %copy-start = (f32[2,8,768,128]{3,2,1,0:T(8,128)}, f32[2,8,768,128]{3,2,1,0:T(8,128)S(1)}, u32[]{:S(2)}) copy-start(f32[2,8,768,128]{3,2,1,0:T(8,128)S(1)} %get-tuple-element.50) | copy-start | bytes 18874372
  86.5 2.6 %copy-start.2 = (bf16[2,768,512]{2,1,0:T(8,128)(2,1)S(1)}, bf16[2,768,512]{2,1,0:T(8,128)(2,1)}, u32[]{:S(2)}) copy-start(bf16[2,768,512]{2,1,0:T(8,128)(2,1)} %get-tuple-element.27) | copy-start | bytes 4718596
  92.8 6.3 %copy-start.4 = (bf16[2,2,128,8,64]{2,1,4,3,0:T(2,128)(2,1)S(1)}, bf16[2,2,128,8,64]{2,1,4,3,0:T(2,128)(2,1)}, u32[]{:S(2)}) copy-start(bf16[2,2,128,8,64]{2,1,4,3,0:T(2,128)(2,1)} %copy-done.3) | copy-start | bytes 1572868
  92.8 7.9 %copy-start.12 = (bf16[2,768,512]{1,2,0:T(8,128)(2,1)S(1)}, bf16[2,768,512]{1,2,0:T(8,128)(2,1)}, u32[]{:S(2)}) copy-start(bf16[2,768,512]{1,2,0:T(8,128)(2,1)} %copy.123) | copy-start | bytes 4718596
  164.7 1.4 copy-start.1
  167.6 3.0 %copy-start.10 = (f32[2,128,8,64]{1,0,3,2:T(2,128)S(1)}, f32[2,128,8,64]{1,0,3,2:T(2,128)}, u32[]{:S(2)}) copy-start(f32[2,128,8,64]{1,0,3,2:T(2,128)} %copy.153) | copy-start | bytes 1572868
  170.7 1.0 copy-start.11
  172.8 44.0 %collective-permute-start.7 = (bf16[128,1024]{1,0:T(8,128)(2,1)}, bf16[128,1024]{1,0:T(8,128)(2,1)S(1)}, u32[]{:S(2)}, u32[]{:S(2)}) collective-permute-start(bf16[128,1024]{1,0:T(8,128)(2,1)} %get-tuple-element.32), channel_id=1, source_target_pairs={{0,16},{8,24},{16,32},{24,40},{32,48},{40,56},{48,64},{56,72},{64,... | collective-permute-start | bytes 786440 | tf_op jit(solution)/shard_map/ppermute | solution.py:17
  175.9 41.8 %collective-permute-start.6 = (bf16[128,1024]{1,0:T(8,128)(2,1)}, bf16[128,1024]{1,0:T(8,128)(2,1)S(1)}, u32[]{:S(2)}, u32[]{:S(2)}) collective-permute-start(bf16[128,1024]{1,0:T(8,128)(2,1)} %get-tuple-element.33), channel_id=1, source_target_pairs={{0,752},{8,760},{16,0},{24,8},{32,16},{40,24},{48,32},{56,40},{64,... | collective-permute-start | bytes 786440 | tf_op jit(solution)/shard_map/ppermute | solution.py:17
  183.2 35.4 %collective-permute-start.5 = (bf16[128,1024]{1,0:T(8,128)(2,1)}, bf16[128,1024]{1,0:T(8,128)(2,1)S(1)}, u32[]{:S(2)}, u32[]{:S(2)}) collective-permute-start(bf16[128,1024]{1,0:T(8,128)(2,1)} %get-tuple-element.31), channel_id=1, source_target_pairs={{0,8},{8,16},{16,24},{24,32},{32,40},{40,48},{48,56},{56,64},{64,7... | collective-permute-start | bytes 786440 | tf_op jit(solution)/shard_map/ppermute | solution.py:17
  188.4 31.1 %collective-permute-start.4 = (bf16[128,1024]{1,0:T(8,128)(2,1)}, bf16[128,1024]{1,0:T(8,128)(2,1)S(1)}, u32[]{:S(2)}, u32[]{:S(2)}) collective-permute-start(bf16[128,1024]{1,0:T(8,128)(2,1)} %get-tuple-element.30), channel_id=1, source_target_pairs={{0,760},{8,0},{16,8},{24,16},{32,24},{40,32},{48,40},{56,48},{64,5... | collective-permute-start | bytes 786440 | tf_op jit(solution)/shard_map/ppermute | solution.py:17
  207.6 4.3 %copy-start.17 = (bf16[2,128,8,64]{1,3,2,0:T(8,128)(2,1)S(1)}, bf16[2,128,8,64]{1,3,2,0:T(8,128)(2,1)}, u32[]{:S(2)}) copy-start(bf16[2,128,8,64]{1,3,2,0:T(8,128)(2,1)} %get-tuple-element.37) | copy-start | bytes 786436
  211.9 3.6 %copy-start.9 = (f32[2,128,8,64]{1,3,2,0:T(8,128)S(1)}, f32[2,128,8,64]{1,3,2,0:T(8,128)}, u32[]{:S(2)}) copy-start(f32[2,128,8,64]{1,3,2,0:T(8,128)} %fusion.23) | copy-start | bytes 1572868
Sparse Core Ops, SparseCore 0:
  10.4 67.4 all-gather.2
  80.2 58.9 all-gather.4

commit v2 on v1

--- a/solution.py
+++ b/solution.py
@@ -91,10 +91,12 @@
         [fetch_partners(terms[step], partner[step], step + 1) for step in range(ROUNDS)]
     )
     returned = jnp.sum(returned.astype(f32), 0)
+    returned, qg_cluster = lax.optimization_barrier((returned, qg_cluster))
 
     stats = jnp.stack([top, total, delta], 1)
     stats = jnp.transpose(stats, (0, 3, 1, 2)).reshape(nodes, 3 * HEADS)
-    stats_cluster = lax.all_gather(stats, "blk", axis=0, tiled=True)
+    stats = jnp.pad(stats, ((0, 0), (0, 128 - 3 * HEADS)))
+    stats_cluster = lax.all_gather(stats, "blk", axis=0, tiled=True)[:, : 3 * HEADS]
 
     qg_tiles = qg_cluster.reshape(cluster_blocks, BLOCK, 2 * width)[tiles].reshape(
         blocks_dev, keys_tile, 2 * width
@@ -109,10 +111,11 @@
     k4 = key.reshape(heads4)
     v4 = value.reshape(heads4)
     s_key = jnp.einsum("bkhd,bqhd->bhkq", k4, q_tile, preferred_element_type=f32) * scale
+    d_key = jnp.einsum("bkhd,bqhd->bhkq", v4, g_tile, preferred_element_type=f32)
+    s_key, d_key = lax.optimization_barrier((s_key, d_key))
     s_key = jnp.where(tile_live[:, None, None, :], s_key, NEG_BIG)
     p_key = jnp.exp(s_key - top_t[:, :, None, :]) / total_t[:, :, None, :]
     w_key = p_key.astype(bf16)
-    d_key = jnp.einsum("bkhd,bqhd->bhkq", v4, g_tile, preferred_element_type=f32)
     z_key = (p_key * (d_key - delta_t[:, :, None, :])).astype(bf16)
     k_sum = jnp.einsum("bhkq,bqhd->bkhd", z_key, q_tile, preferred_element_type=f32) * scale
     v_sum = jnp.einsum("bhkq,bqhd->bkhd", w_key, g_tile, preferred_element_type=f32)

time: 232 us -> 212 us (0.914)
  the two profiles are of different devices: /device:TPU:1 before, /device:TPU:2 now
where the time goes in v2:
time: 212 us
  waiting for transfers between devices  55.1 us (26%)
  local copies, waits for them, and re-layouts  49.9 us (24%)
  matrix products  38.3 us (18%)
  starting transfers between devices  37.1 us (18%)
  other arithmetic  16.8 us (8%)
  between operations  14.5 us (7%)
    ppermute x8, starting transfers between devices, passed_along(): return lax.ppermute(x, axis, [(i, (i + by) % size) for i in range(size)])  37 us
    all_gather x1, waiting for transfers between devices, shards(): lax.all_gather(stats, 'blk', axis=0, tiled=True)[:, :3 * HEADS]  28.3 us
    all_gather x1, waiting for transfers between devices, shards(): kv_cluster = lax.all_gather(both, 'blk', axis=0, tiled=True)  23.7 us
    unnamed x49, local copies, waits for them, and re-layouts  10.4 us
    dot_general x1, matrix products, shards(): jnp.einsum('bhkq,bqhd->bkhd', w_key, g_tile, preferred_element_type=f32)  8.77 us
    gather x8, local copies, waits for them, and re-layouts, fetch_partners(): return jnp.concatenate([ahead[slots[:half]], behind[slots[half:]]], 0)  6.89 us
    dot_general x1, matrix products, shards(): jnp.einsum('bhqk,bkhd->bqhd', z_loc, k_tile, preferred_element_type=f32)  6.56 us
    dot_general x1, matrix products, shards(): jnp.einsum('bhkq,bqhd->bkhd', z_key, q_tile, preferred_element_type=f32)  6.4 us
  transfers between devices with their start and end apart: 11, of which 3 were waited for; matrix products, arithmetic and copies ran while one was open for 37% of the time, Pallas kernels for 0%

profile of v2, /device:TPU:2, one launch (start us, length us, event | category | flops | bytes accessed | tf_op | source)
XLA Modules:
  0.0 211.6 jit_solution(2341910083585130632)
XLA Ops:
  7.2 1.0 constant_dynamic-update-slice_fusion.1
  8.3 1.0 constant_dynamic-update-slice_fusion
  9.3 0.8 copy-done.6
  10.1 1.9 fusion.69
  12.0 11.4 %collective-permute-start.2 = (bf16[128,1024]{1,0:T(8,128)(2,1)}, bf16[128,1024]{1,0:T(8,128)(2,1)S(1)}, u32[]{:S(2)}, u32[]{:S(2)}) collective-permute-start(bf16[128,1024]{1,0:T(8,128)(2,1)} %get-tuple-element.46), channel_id=1, source_target_pairs={{0,752},{8,760},{16,0},{24,8},{32,16},{40,24},{48,32},{56,40},{64,... | collective-permute-start | bytes 786440 | tf_op jit(solution)/shard_map/ppermute | solution.py:17
  23.4 6.9 %collective-permute-start = (bf16[128,1024]{1,0:T(8,128)(2,1)}, bf16[128,1024]{1,0:T(8,128)(2,1)S(1)}, u32[]{:S(2)}, u32[]{:S(2)}) collective-permute-start(bf16[128,1024]{1,0:T(8,128)(2,1)} %get-tuple-element.46), channel_id=1, source_target_pairs={{0,760},{8,0},{16,8},{24,16},{32,24},{40,32},{48,40},{56,48},{64,5... | collective-permute-start | bytes 786440 | tf_op jit(solution)/shard_map/ppermute | solution.py:17
  30.4 1.9 collective-permute-start.3
  32.3 1.9 collective-permute-start.1
  34.2 1.9 pad_maximum_fusion.1
  36.2 1.1 copy.145
  37.3 0.7 compare_select_fusion
  38.1 0.8 fusion.59
  38.9 0.7 iota_compare_fusion
  40.0 1.1 copy.135
  41.1 1.1 reshape.383
  42.2 1.1 reshape.384
  43.3 1.2 copy.151
  44.5 1.2 fusion.70
  45.7 0.9 gather_fusion.3
  46.6 0.9 gather_fusion.1
  47.5 0.9 gather_fusion.4
  48.3 0.9 gather_fusion.2
  49.3 1.0 pad_maximum_fusion
  50.6 1.4 copy.137
  53.3 23.7 %all-gather.4.cloned.1.call-done = bf16[2048,1024]{1,0:T(8,128)(2,1)} async-done(((bf16[256,1024]{1,0:T(8,128)(2,1)}), bf16[2048,1024]{1,0:T(8,128)(2,1)}) %all-gather.4.cloned.1.call-update) | async-done | bytes 4194320 | tf_op jit(solution)/shard_map/all_gather | solution.py:40
  77.0 2.9 %gather_fusion = bf16[12,128,1024]{2,1,0:T(8,128)(2,1)S(1)} fusion(bf16[16,128,1024]{2,1,0:T(8,128)(2,1)} %bitcast.186, s32[1024]{0:T(1024)S(1)} %pad_clamp_fusion.4), kind=kCustom, calls=%fused_computation | custom fusion | bytes 6291504 | tf_op jit(solution)/shard_map/gather | solution.py:50
  79.9 1.9 fusion.68
  81.9 1.8 copy.134
  83.7 2.6 %copy.133 = bf16[2,768,512]{1,2,0:T(8,128)(2,1)} copy(bf16[2,768,512]{2,1,0:T(8,128)(2,1)} %get-tuple-element.35) | data formatting | bytes 3145728 | tf_op jit(solution)/shard_map/slice | solution.py:54
  86.2 1.8 bitcast_reduce_fusion
  88.2 2.6 %copy-done = f32[2,8,768,128]{3,2,1,0:T(8,128)} copy-done((f32[2,8,768,128]{3,2,1,0:T(8,128)}, f32[2,8,768,128]{3,2,1,0:T(8,128)S(1)}, u32[]{:S(2)}) %copy-start) | copy-done | bytes 6291480
  90.7 1.4 fusion.3
  93.0 1.0 copy.153
  94.1 0.7 multiply_reduce_fusion.2
  94.8 6.2 %multiply_reduce_fusion.4 = (f32[2,128,8]{1,2,0:T(8,128)S(1)}, bf16[2,128,8,64]{1,3,2,0:T(8,128)(2,1)}) fusion(bf16[2,128,8,64]{1,0,3,2:T(2,128)(2,1)S(1)} %reshape.262, f32[2,128,8,64]{1,0,3,2:T(2,128)S(1)} %multiply_reduce_fusion.2, bf16[2,768,8,64]{1,3,2,0:T(8,128)(2,1)} %bitcast.187, f32[2,8,128]{2,1,0:T(8,128)S(1)} %copy_add_fusion, ...), kind=kOutput, calls=%fused_computation.69 | convolution fusion | flops 209844224 | bytes 8939008 | tf_op jit(solution)/shard_map/bhqk,bkhd->bqhd/dot_general | solution.py:72
  102.2 2.1 fusion.48
  104.3 1.9 collective-permute-start.4
  106.2 2.4 %collective-permute-start.5 = (bf16[128,1024]{1,0:T(8,128)(2,1)}, bf16[128,1024]{1,0:T(8,128)(2,1)S(1)}, u32[]{:S(2)}, u32[]{:S(2)}) collective-permute-start(bf16[128,1024]{1,0:T(8,128)(2,1)} %get-tuple-element.39), channel_id=1, source_target_pairs={{0,8},{8,16},{16,24},{24,32},{32,40},{40,48},{48,56},{56,64},{64,7... | collective-permute-start | bytes 786440 | tf_op jit(solution)/shard_map/ppermute | solution.py:17
  108.6 3.4 %collective-permute-start.7 = (bf16[128,1024]{1,0:T(8,128)(2,1)}, bf16[128,1024]{1,0:T(8,128)(2,1)S(1)}, u32[]{:S(2)}, u32[]{:S(2)}) collective-permute-start(bf16[128,1024]{1,0:T(8,128)(2,1)} %get-tuple-element.40), channel_id=1, source_target_pairs={{0,16},{8,24},{16,32},{24,40},{32,48},{40,56},{48,64},{56,72},{64,... | collective-permute-start | bytes 786440 | tf_op jit(solution)/shard_map/ppermute | solution.py:17
  112.0 7.1 %collective-permute-start.6 = (bf16[128,1024]{1,0:T(8,128)(2,1)}, bf16[128,1024]{1,0:T(8,128)(2,1)S(1)}, u32[]{:S(2)}, u32[]{:S(2)}) collective-permute-start(bf16[128,1024]{1,0:T(8,128)(2,1)} %get-tuple-element.41), channel_id=1, source_target_pairs={{0,752},{8,760},{16,0},{24,8},{32,16},{40,24},{48,32},{56,40},{64,... | collective-permute-start | bytes 786440 | tf_op jit(solution)/shard_map/ppermute | solution.py:17
  119.1 0.7 pad.4
  119.8 1.5 multiply_reduce_fusion
  121.4 6.6 %fusion.35 = bf16[2,128,8,64]{1,3,2,0:T(8,128)(2,1)S(1)} fusion(bf16[2,768,8,64]{1,3,2,0:T(8,128)(2,1)S(1)} %bitcast.176, f32[2,8,128]{2,1,0:T(8,128)S(1)} %bitcast.201, bf16[2,768,8,64]{1,3,2,0:T(8,128)(2,1)} %bitcast.188, f32[2,8,768,128]{3,2,1,0:T(8,128)} %copy-done, f32[2,8,128]{2,1,0:T(8,128)S(1)} %copy_add_fusion, ...), kind=kOutput, calls=%fused_computation.47 | convolution fusion | flops 414056448 | bytes 10511872 | tf_op jit(solution)/shard_map/bhqk,bkhd->bqhd/dot_general | solution.py:79
  128.2 1.0 reshape.382
  129.6 1.0 reshape.381
  130.6 0.9 gather_fusion.5
  131.5 0.9 gather_fusion.6
  132.4 0.9 gather_fusion.8
  133.2 0.9 gather_fusion.7
  134.2 1.2 convert_reduce_fusion
  135.4 3.0 %all-gather.6.cloned.1.call-done = bf16[2048,1024]{1,0:T(8,128)(2,1)} async-done(((bf16[256,1024]{1,0:T(8,128)(2,1)}), bf16[2048,1024]{1,0:T(8,128)(2,1)}) %all-gather.6.cloned.1.call-update) | async-done | bytes 4194320 | tf_op jit(solution)/shard_map/all_gather | solution.py:41
  138.3 2.9 %gather_fusion.9 = bf16[12,128,1024]{2,1,0:T(8,128)(2,1)S(1)} fusion(bf16[16,128,1024]{2,1,0:T(8,128)(2,1)} %bitcast.185, s32[1024]{0:T(1024)S(1)} %pad_clamp_fusion.4), kind=kCustom, calls=%fused_computation.9 | custom fusion | bytes 6291504 | tf_op jit(solution)/shard_map/gather | solution.py:101
  141.3 1.9 fusion.67
  143.2 1.7 copy.157
  144.9 1.7 copy.154
  146.7 4.8 %multiply_bitcast_fusion = f32[2,8,128,768]{2,3,1,0:T(8,128)} fusion(bf16[2,768,8,64]{1,3,2,0:T(8,128)(2,1)S(1)} %bitcast.179, bf16[2,128,8,64]{3,2,1,0:T(8,128)(2,1)} %reshape.383), kind=kOutput, calls=%fused_computation.18 | convolution fusion | flops 202899456 | bytes 8126464 | tf_op jit(solution)/shard_map/bkhd,bqhd->bhkq/dot_general | solution.py:113
  151.5 3.7 %convolution_bitcast_fusion = f32[2,8,128,768]{2,3,1,0:T(8,128)} fusion(bf16[2,768,8,64]{1,3,2,0:T(8,128)(2,1)S(1)} %bitcast.177, bf16[2,128,8,64]{3,2,1,0:T(8,128)(2,1)S(1)} %copy-done.9), kind=kOutput, calls=%fused_computation.31 | convolution fusion | flops 201326592 | bytes 8126464 | tf_op jit(solution)/shard_map/bkhd,bqhd->bhkq/dot_general | solution.py:114
  155.2 28.3 %all-gather.8.cloned.1.call-done = f32[2048,128]{0,1:T(8,128)} async-done(((f32[256,128]{0,1:T(8,128)}), f32[2048,128]{0,1:T(8,128)}) %all-gather.8.cloned.1.call-update) | async-done | bytes 1048592 | tf_op jit(solution)/shard_map/all_gather | solution.py:99
  183.5 0.9 slice_bitcast_fusion
  185.4 8.8 %fusion.24 = f32[2,128,8,64]{1,3,2,0:T(8,128)} fusion(bf16[2,768,8,64]{1,3,2,0:T(8,128)(2,1)S(1)} %bitcast.178, f32[2,8,768]{2,1,0:T(8,128)S(1)} %copy.163, f32[2,8,768]{2,1,0:T(8,128)S(1)} %copy.162, f32[2,8,128,768]{2,3,1,0:T(8,128)} %multiply_bitcast_fusion, pred[2,768]{1,0:T(4,128)(4,1)S(1)} %bitcast.197), kind=kOutput, calls=%fused_computation.42 | convolution fusion | flops 207618048 | bytes 8488448 | tf_op jit(solution)/shard_map/bhkq,bqhd->bkhd/dot_general | solution.py:121
  194.2 6.4 %fusion.34 = f32[2,128,8,64]{1,3,2,0:T(8,128)} fusion(bf16[2,768,8,64]{1,3,2,0:T(8,128)(2,1)S(1)} %bitcast.180, f32[2,8,128,768]{2,3,1,0:T(8,128)S(1)} %bitcast.184, f32[2,8,768]{2,1,0:T(8,128)S(1)} %copy.164, f32[2,8,768]{2,1,0:T(8,128)S(1)} %copy.163, f32[2,8,768]{2,1,0:T(8,128)S(1)} %copy.162, f32[2,8,128,768]{2,3,1,0:T(8,128)S(1)} %bitcast.182, ...), kind=kOutput, calls=%fused_computation.46 | convolution fusion | flops 210894848 | bytes 14829056 | tf_op jit(solution)/shard_map/bhkq,bqhd->bkhd/dot_general | solution.py:120
  200.6 1.5 copy.213
  202.4 1.4 copy.214
  204.1 0.9 add_convert_fusion
  (101 shorter events, 6.5 us)
Async XLA Ops:
  7.2 33.9 %copy-start.12 = (bf16[256,512]{1,0:T(8,128)(2,1)S(1)}, bf16[256,512]{1,0:T(8,128)(2,1)}, u32[]{:S(2)}) copy-start(bf16[256,512]{1,0:T(8,128)(2,1)} %param.8) | copy-start | bytes 786436
  7.2 35.0 %copy-start.13 = (bf16[256,512]{1,0:T(8,128)(2,1)S(1)}, bf16[256,512]{1,0:T(8,128)(2,1)}, u32[]{:S(2)}) copy-start(bf16[256,512]{1,0:T(8,128)(2,1)} %param.9) | copy-start | bytes 786436
  7.2 69.8 %all-gather.4.cloned.1.call-start = ((), (), s32[]{:S(2)}) async-start(), calls=%async_computation | async-start | bytes 4718592 | tf_op jit(solution)/shard_map/all_gather | solution.py:40
  9.2 0.8 copy-start.6
  10.1 128.3 %all-gather.6.cloned.1.call-start = ((), (), s32[]{:S(2)}) async-start(), calls=%async_computation.1 | async-start | bytes 4718592 | tf_op jit(solution)/shard_map/all_gather | solution.py:41
  12.0 33.8 %collective-permute-start.2 = (bf16[128,1024]{1,0:T(8,128)(2,1)}, bf16[128,1024]{1,0:T(8,128)(2,1)S(1)}, u32[]{:S(2)}, u32[]{:S(2)}) collective-permute-start(bf16[128,1024]{1,0:T(8,128)(2,1)} %get-tuple-element.46), channel_id=1, source_target_pairs={{0,752},{8,760},{16,0},{24,8},{32,16},{40,24},{48,32},{56,40},{64,... | collective-permute-start | bytes 786440 | tf_op jit(solution)/shard_map/ppermute | solution.py:17
  23.4 23.2 %collective-permute-start = (bf16[128,1024]{1,0:T(8,128)(2,1)}, bf16[128,1024]{1,0:T(8,128)(2,1)S(1)}, u32[]{:S(2)}, u32[]{:S(2)}) collective-permute-start(bf16[128,1024]{1,0:T(8,128)(2,1)} %get-tuple-element.46), channel_id=1, source_target_pairs={{0,760},{8,0},{16,8},{24,16},{32,24},{40,32},{48,40},{56,48},{64,5... | collective-permute-start | bytes 786440 | tf_op jit(solution)/shard_map/ppermute | solution.py:17
  30.4 17.1 %collective-permute-start.3 = (bf16[128,1024]{1,0:T(8,128)(2,1)}, bf16[128,1024]{1,0:T(8,128)(2,1)S(1)}, u32[]{:S(2)}, u32[]{:S(2)}) collective-permute-start(bf16[128,1024]{1,0:T(8,128)(2,1)} %get-tuple-element.47), channel_id=1, source_target_pairs={{0,16},{8,24},{16,32},{24,40},{32,48},{40,56},{48,64},{56,72},{64,... | collective-permute-start | bytes 786440 | tf_op jit(solution)/shard_map/ppermute | solution.py:17
  32.3 16.0 %collective-permute-start.1 = (bf16[128,1024]{1,0:T(8,128)(2,1)}, bf16[128,1024]{1,0:T(8,128)(2,1)S(1)}, u32[]{:S(2)}, u32[]{:S(2)}) collective-permute-start(bf16[128,1024]{1,0:T(8,128)(2,1)} %get-tuple-element.47), channel_id=1, source_target_pairs={{0,8},{8,16},{16,24},{24,32},{32,40},{40,48},{48,56},{56,64},{64,7... | collective-permute-start | bytes 786440 | tf_op jit(solution)/shard_map/ppermute | solution.py:17
  36.1 147.3 %all-gather.8.cloned.1.call-start = ((), (), s32[]{:S(2)}) async-start(), calls=%async_computation.2 | async-start | bytes 1179648 | tf_op jit(solution)/shard_map/all_gather | solution.py:99
  43.3 5.9 %copy-start.7 = (bf16[2,128,8,64]{1,0,3,2:T(2,128)(2,1)}, bf16[2,128,8,64]{1,0,3,2:T(2,128)(2,1)S(1)}, u32[]{:S(2)}) copy-start(bf16[2,128,8,64]{1,0,3,2:T(2,128)(2,1)S(1)} %reshape.259) | copy-start | bytes 786436
  50.6 26.4 %copy-start.3 = (bf16[2,2,128,8,64]{2,1,4,3,0:T(2,128)(2,1)}, bf16[2,2,128,8,64]{2,1,4,3,0:T(2,128)(2,1)S(1)}, u32[]{:S(2)}) copy-start(bf16[2,2,128,8,64]{2,1,4,3,0:T(2,128)(2,1)S(1)} %reshape.261) | copy-start | bytes 1572868
  52.2 24.8 %copy-start.1 = (bf16[2,2,128,8,64]{2,1,4,3,0:T(2,128)(2,1)}, bf16[2,2,128,8,64]{2,1,4,3,0:T(2,128)(2,1)S(1)}, u32[]{:S(2)}) copy-start(bf16[2,2,128,8,64]{2,1,4,3,0:T(2,128)(2,1)S(1)} %reshape.260) | copy-start | bytes 1572868
  81.9 4.3 %copy-start.8 = (bf16[2,128,8,64]{1,0,3,2:T(2,128)(2,1)S(1)}, bf16[2,128,8,64]{1,0,3,2:T(2,128)(2,1)}, u32[]{:S(2)}) copy-start(bf16[2,128,8,64]{1,0,3,2:T(2,128)(2,1)} %copy-done.7) | copy-start | bytes 786436
  86.2 6.0 %copy-start.11 = (f32[2,128,8,64]{1,0,3,2:T(2,128)S(1)}, f32[2,128,8,64]{1,0,3,2:T(2,128)}, u32[]{:S(2)}) copy-start(f32[2,128,8,64]{1,0,3,2:T(2,128)} %copy.151) | copy-start | bytes 1572868
  88.1 2.7 %copy-start = (f32[2,8,768,128]{3,2,1,0:T(8,128)}, f32[2,8,768,128]{3,2,1,0:T(8,128)S(1)}, u32[]{:S(2)}) copy-start(f32[2,8,768,128]{3,2,1,0:T(8,128)S(1)} %get-tuple-element.58) | copy-start | bytes 18874372
  88.1 6.0 %copy-start.4 = (bf16[2,2,128,8,64]{2,1,4,3,0:T(2,128)(2,1)S(1)}, bf16[2,2,128,8,64]{2,1,4,3,0:T(2,128)(2,1)}, u32[]{:S(2)}) copy-start(bf16[2,2,128,8,64]{2,1,4,3,0:T(2,128)(2,1)} %copy-done.3) | copy-start | bytes 1572868
  94.8 6.3 %copy-start.10 = (f32[2,128,8,64]{1,0,3,2:T(2,128)S(1)}, f32[2,128,8,64]{1,0,3,2:T(2,128)}, u32[]{:S(2)}) copy-start(f32[2,128,8,64]{1,0,3,2:T(2,128)} %get-tuple-element.48) | copy-start | bytes 1572868
  94.8 24.9 %copy-start.2 = (bf16[2,2,128,8,64]{2,1,4,3,0:T(2,128)(2,1)S(1)}, bf16[2,2,128,8,64]{2,1,4,3,0:T(2,128)(2,1)}, u32[]{:S(2)}) copy-start(bf16[2,2,128,8,64]{2,1,4,3,0:T(2,128)(2,1)} %copy-done.1) | copy-start | bytes 1572868
  104.3 26.3 %collective-permute-start.4 = (bf16[128,1024]{1,0:T(8,128)(2,1)}, bf16[128,1024]{1,0:T(8,128)(2,1)S(1)}, u32[]{:S(2)}, u32[]{:S(2)}) collective-permute-start(bf16[128,1024]{1,0:T(8,128)(2,1)} %get-tuple-element.38), channel_id=1, source_target_pairs={{0,760},{8,0},{16,8},{24,16},{32,24},{40,32},{48,40},{56,48},{64,5... | collective-permute-start | bytes 786440 | tf_op jit(solution)/shard_map/ppermute | solution.py:17
  106.2 25.2 %collective-permute-start.5 = (bf16[128,1024]{1,0:T(8,128)(2,1)}, bf16[128,1024]{1,0:T(8,128)(2,1)S(1)}, u32[]{:S(2)}, u32[]{:S(2)}) collective-permute-start(bf16[128,1024]{1,0:T(8,128)(2,1)} %get-tuple-element.39), channel_id=1, source_target_pairs={{0,8},{8,16},{16,24},{24,32},{32,40},{40,48},{48,56},{56,64},{64,7... | collective-permute-start | bytes 786440 | tf_op jit(solution)/shard_map/ppermute | solution.py:17
  108.6 23.7 %collective-permute-start.7 = (bf16[128,1024]{1,0:T(8,128)(2,1)}, bf16[128,1024]{1,0:T(8,128)(2,1)S(1)}, u32[]{:S(2)}, u32[]{:S(2)}) collective-permute-start(bf16[128,1024]{1,0:T(8,128)(2,1)} %get-tuple-element.40), channel_id=1, source_target_pairs={{0,16},{8,24},{16,32},{24,40},{32,48},{40,56},{48,64},{56,72},{64,... | collective-permute-start | bytes 786440 | tf_op jit(solution)/shard_map/ppermute | solution.py:17
  112.0 21.2 %collective-permute-start.6 = (bf16[128,1024]{1,0:T(8,128)(2,1)}, bf16[128,1024]{1,0:T(8,128)(2,1)S(1)}, u32[]{:S(2)}, u32[]{:S(2)}) collective-permute-start(bf16[128,1024]{1,0:T(8,128)(2,1)} %get-tuple-element.41), channel_id=1, source_target_pairs={{0,752},{8,760},{16,0},{24,8},{32,16},{40,24},{48,32},{56,40},{64,... | collective-permute-start | bytes 786440 | tf_op jit(solution)/shard_map/ppermute | solution.py:17
  121.3 7.9 %copy-start.14 = (bf16[2,128,8,64]{1,3,2,0:T(8,128)(2,1)S(1)}, bf16[2,128,8,64]{1,3,2,0:T(8,128)(2,1)}, u32[]{:S(2)}) copy-start(bf16[2,128,8,64]{1,3,2,0:T(8,128)(2,1)} %get-tuple-element.45) | copy-start | bytes 786436
  146.7 4.8 %copy-start.9 = (bf16[2,128,8,64]{3,2,1,0:T(8,128)(2,1)S(1)}, bf16[2,128,8,64]{3,2,1,0:T(8,128)(2,1)}, u32[]{:S(2)}) copy-start(bf16[2,128,8,64]{3,2,1,0:T(8,128)(2,1)} %reshape.384) | copy-start | bytes 786436
  185.3 8.9 %slice-start = ((s8[6291456]{0:T(1024)(128)(4,1)}), s8[4194304]{0:T(1024)(128)(4,1)S(1)}, s32[]{:S(2)}) async-start(s8[6291456]{0:T(1024)(128)(4,1)} %bitcast.181), calls=%async_computation.3 | async-start | bytes 8388608
  185.3 8.9 %slice-start.2 = ((s8[6291456]{0:T(1024)(128)(4,1)}), s8[4194304]{0:T(1024)(128)(4,1)S(1)}, s32[]{:S(2)}) async-start(s8[6291456]{0:T(1024)(128)(4,1)} %bitcast.183), calls=%async_computation.5 | async-start | bytes 8388608
  185.3 8.8 %slice-start.1 = ((s8[6291456]{0:T(1024)(128)(4,1)}), s8[2097152]{0:T(1024)(128)(4,1)S(1)}, s32[]{:S(2)}) async-start(s8[6291456]{0:T(1024)(128)(4,1)} %bitcast.181), calls=%async_computation.4 | async-start | bytes 4194304
  185.3 8.8 %slice-start.3 = ((s8[6291456]{0:T(1024)(128)(4,1)}), s8[2097152]{0:T(1024)(128)(4,1)S(1)}, s32[]{:S(2)}) async-start(s8[6291456]{0:T(1024)(128)(4,1)} %bitcast.183), calls=%async_computation.6 | async-start | bytes 4194304
  200.6 3.5 %copy-start.5 = (f32[256,1024]{1,0:T(8,128)S(1)}, f32[256,1024]{1,0:T(8,128)}, u32[]{:S(2)}) copy-start(f32[256,1024]{1,0:T(8,128)} %convert_reduce_fusion) | copy-start | bytes 3145732
Sparse Core Ops, SparseCore 0:
  10.4 66.5 all-gather.3
  79.4 58.9 all-gather.5
  140.7 42.7 all-gather.7

commit v3 on v2

--- a/solution.py
+++ b/solution.py
@@ -93,20 +93,19 @@
     returned = jnp.sum(returned.astype(f32), 0)
     returned, qg_cluster = lax.optimization_barrier((returned, qg_cluster))
 
-    stats = jnp.stack([top, total, delta], 1)
-    stats = jnp.transpose(stats, (0, 3, 1, 2)).reshape(nodes, 3 * HEADS)
-    stats = jnp.pad(stats, ((0, 0), (0, 128 - 3 * HEADS)))
-    stats_cluster = lax.all_gather(stats, "blk", axis=0, tiled=True)[:, : 3 * HEADS]
+    stats = jnp.stack([top, total, delta], 1).reshape(blocks_dev * 3 * HEADS, BLOCK)
+    rows = stats.shape[0]
+    stats = jnp.pad(stats, ((0, nodes - rows), (0, 0)))
+    stats_cluster = lax.all_gather(stats, "blk", axis=0, tiled=True)
+    stats_cluster = stats_cluster.reshape(team, nodes, BLOCK)[:, :rows]
 
     qg_tiles = qg_cluster.reshape(cluster_blocks, BLOCK, 2 * width)[tiles].reshape(
         blocks_dev, keys_tile, 2 * width
     )
     q_tile = qg_tiles[..., :width].reshape(blocks_dev, keys_tile, HEADS, head_dim)
     g_tile = qg_tiles[..., width:].reshape(blocks_dev, keys_tile, HEADS, head_dim)
-    st = stats_cluster.reshape(cluster_blocks, BLOCK, 3, HEADS)[tiles].reshape(
-        blocks_dev, keys_tile, 3, HEADS
-    )
-    st = jnp.transpose(st, (0, 2, 3, 1))
+    st = stats_cluster.reshape(cluster_blocks, 3, HEADS, BLOCK)[tiles]
+    st = jnp.transpose(st, (0, 2, 3, 1, 4)).reshape(blocks_dev, 3, HEADS, keys_tile)
     top_t, total_t, delta_t = st[:, 0], st[:, 1], st[:, 2]
     k4 = key.reshape(heads4)
     v4 = value.reshape(heads4)

time: 212 us -> 209 us (0.986)
  local copies, waits for them, and re-layouts: 49.9 us -> 47.5 us
where the time goes in v3:
time: 209 us; the launch traced here: 208 us
  waiting for transfers between devices  55 us (26%)
  local copies, waits for them, and re-layouts  47.5 us (23%)
  matrix products  37.6 us (18%)
  starting transfers between devices  37.1 us (18%)
  other arithmetic  16.8 us (8%)
  between operations  14.5 us (7%)
    ppermute x8, starting transfers between devices, passed_along(): return lax.ppermute(x, axis, [(i, (i + by) % size) for i in range(size)])  37 us
    all_gather x1, waiting for transfers between devices, shards(): stats_cluster = lax.all_gather(stats, 'blk', axis=0, tiled=True)  28.3 us
    all_gather x1, waiting for transfers between devices, shards(): kv_cluster = lax.all_gather(both, 'blk', axis=0, tiled=True)  23.7 us
    unnamed x49, local copies, waits for them, and re-layouts  9.42 us
    dot_general x1, matrix products, shards(): jnp.einsum('bhkq,bqhd->bkhd', w_key, g_tile, preferred_element_type=f32)  8.77 us
    gather x8, local copies, waits for them, and re-layouts, fetch_partners(): return jnp.concatenate([ahead[slots[:half]], behind[slots[half:]]], 0)  6.89 us
    dot_general x1, matrix products, shards(): jnp.einsum('bhqk,bkhd->bqhd', z_loc, k_tile, preferred_element_type=f32)  6.56 us
    dot_general x1, matrix products, shards(): jnp.einsum('bhqk,bkhd->bqhd', w_loc, v_tile, preferred_element_type=f32)  6.24 us
  transfers between devices with their start and end apart: 11, of which 3 were waited for; matrix products, arithmetic and copies ran while one was open for 37% of the time, Pallas kernels for 0%

profile of v3, /device:TPU:2, one launch (start us, length us, event | category | flops | bytes accessed | tf_op | source)
XLA Modules:
  0.0 208.4 jit_solution(14536111295180860879)
XLA Ops:
  7.2 1.0 constant_dynamic-update-slice_fusion.1
  8.3 1.0 constant_dynamic-update-slice_fusion
  9.3 0.8 copy-done.6
  10.1 1.9 fusion.69
  12.0 11.4 %collective-permute-start.2 = (bf16[128,1024]{1,0:T(8,128)(2,1)}, bf16[128,1024]{1,0:T(8,128)(2,1)S(1)}, u32[]{:S(2)}, u32[]{:S(2)}) collective-permute-start(bf16[128,1024]{1,0:T(8,128)(2,1)} %get-tuple-element.42), channel_id=1, source_target_pairs={{0,752},{8,760},{16,0},{24,8},{32,16},{40,24},{48,32},{56,40},{64,... | collective-permute-start | bytes 786440 | tf_op jit(solution)/shard_map/ppermute | solution.py:17
  23.5 6.9 %collective-permute-start = (bf16[128,1024]{1,0:T(8,128)(2,1)}, bf16[128,1024]{1,0:T(8,128)(2,1)S(1)}, u32[]{:S(2)}, u32[]{:S(2)}) collective-permute-start(bf16[128,1024]{1,0:T(8,128)(2,1)} %get-tuple-element.42), channel_id=1, source_target_pairs={{0,760},{8,0},{16,8},{24,16},{32,24},{40,32},{48,40},{56,48},{64,5... | collective-permute-start | bytes 786440 | tf_op jit(solution)/shard_map/ppermute | solution.py:17
  30.4 1.9 collective-permute-start.3
  32.3 1.9 collective-permute-start.1
  34.2 1.9 pad_maximum_fusion.1
  36.2 1.1 copy.102
  37.3 0.7 compare_select_fusion
  38.1 0.8 fusion.59
  38.9 0.7 iota_compare_fusion
  40.0 1.1 copy.92
  41.1 1.1 reshape.386
  42.2 1.1 reshape.387
  43.3 1.2 copy.108
  44.5 1.2 fusion.70
  45.7 0.9 gather_fusion.3
  46.6 0.9 gather_fusion.1
  47.5 0.9 gather_fusion.4
  48.4 0.9 gather_fusion.2
  49.3 1.0 pad_maximum_fusion
  50.6 1.4 copy.94
  52.2 0.6 multiply_reduce_fusion.3
  53.3 23.7 %all-gather.4.cloned.1.call-done = bf16[2048,1024]{1,0:T(8,128)(2,1)} async-done(((bf16[256,1024]{1,0:T(8,128)(2,1)}), bf16[2048,1024]{1,0:T(8,128)(2,1)}) %all-gather.4.cloned.1.call-update) | async-done | bytes 4194320 | tf_op jit(solution)/shard_map/all_gather | solution.py:40
  77.0 2.9 %gather_fusion = bf16[12,128,1024]{2,1,0:T(8,128)(2,1)S(1)} fusion(bf16[16,128,1024]{2,1,0:T(8,128)(2,1)} %bitcast.180, s32[1024]{0:T(1024)S(1)} %pad_clamp_fusion.4), kind=kCustom, calls=%fused_computation | custom fusion | bytes 6291504 | tf_op jit(solution)/shard_map/gather | solution.py:50
  79.9 2.0 fusion.68
  81.9 1.8 copy.91
  83.7 2.6 %copy.90 = bf16[2,768,512]{1,2,0:T(8,128)(2,1)} copy(bf16[2,768,512]{2,1,0:T(8,128)(2,1)} %get-tuple-element.31) | data formatting | bytes 3145728 | tf_op jit(solution)/shard_map/slice | solution.py:54
  86.3 1.8 bitcast_reduce_fusion
  88.2 2.6 %copy-done = f32[2,8,768,128]{3,2,1,0:T(8,128)} copy-done((f32[2,8,768,128]{3,2,1,0:T(8,128)}, f32[2,8,768,128]{3,2,1,0:T(8,128)S(1)}, u32[]{:S(2)}) %copy-start) | copy-done | bytes 6291480
  90.7 1.4 fusion.3
  93.1 1.0 copy.110
  94.1 0.7 multiply_reduce_fusion.2
  94.8 6.2 %multiply_reduce_fusion.4 = (f32[2,128,8]{1,2,0:T(8,128)S(1)}, bf16[2,128,8,64]{1,3,2,0:T(8,128)(2,1)}) fusion(bf16[2,128,8,64]{1,0,3,2:T(2,128)(2,1)S(1)} %reshape.265, f32[2,128,8,64]{1,0,3,2:T(2,128)S(1)} %multiply_reduce_fusion.2, bf16[2,768,8,64]{1,3,2,0:T(8,128)(2,1)} %bitcast.181, f32[2,8,128]{2,1,0:T(8,128)S(1)} %copy_add_fusion, ...), kind=kOutput, calls=%fused_computation.69 | convolution fusion | flops 209844224 | bytes 8939008 | tf_op jit(solution)/shard_map/bhqk,bkhd->bqhd/dot_general | solution.py:72
  102.2 2.1 %fusion.48 = (bf16[128,1024]{1,0:T(8,128)(2,1)}, bf16[128,1024]{1,0:T(8,128)(2,1)}, bf16[128,1024]{1,0:T(8,128)(2,1)}, bf16[128,1024]{1,0:T(8,128)(2,1)}) fusion(bf16[2,256,512]{2,1,0:T(8,128)(2,1)S(1)} %copy.109, bf16[2,256,512]{2,1,0:T(8,128)(2,1)} %copy.110), kind=kLoop, calls=%fused_computation.73 | loop fusion | flops 2097152 | bytes 2097152 | tf_op jit(solution)/shard_map/slice | solution.py:22
  104.3 1.9 collective-permute-start.4
  106.3 2.4 %collective-permute-start.5 = (bf16[128,1024]{1,0:T(8,128)(2,1)}, bf16[128,1024]{1,0:T(8,128)(2,1)S(1)}, u32[]{:S(2)}, u32[]{:S(2)}) collective-permute-start(bf16[128,1024]{1,0:T(8,128)(2,1)} %get-tuple-element.35), channel_id=1, source_target_pairs={{0,8},{8,16},{16,24},{24,32},{32,40},{40,48},{48,56},{56,64},{64,7... | collective-permute-start | bytes 786440 | tf_op jit(solution)/shard_map/ppermute | solution.py:17
  108.7 3.4 %collective-permute-start.7 = (bf16[128,1024]{1,0:T(8,128)(2,1)}, bf16[128,1024]{1,0:T(8,128)(2,1)S(1)}, u32[]{:S(2)}, u32[]{:S(2)}) collective-permute-start(bf16[128,1024]{1,0:T(8,128)(2,1)} %get-tuple-element.36), channel_id=1, source_target_pairs={{0,16},{8,24},{16,32},{24,40},{32,48},{40,56},{48,64},{56,72},{64,... | collective-permute-start | bytes 786440 | tf_op jit(solution)/shard_map/ppermute | solution.py:17
  112.1 7.1 %collective-permute-start.6 = (bf16[128,1024]{1,0:T(8,128)(2,1)}, bf16[128,1024]{1,0:T(8,128)(2,1)S(1)}, u32[]{:S(2)}, u32[]{:S(2)}) collective-permute-start(bf16[128,1024]{1,0:T(8,128)(2,1)} %get-tuple-element.37), channel_id=1, source_target_pairs={{0,752},{8,760},{16,0},{24,8},{32,16},{40,24},{48,32},{56,40},{64,... | collective-permute-start | bytes 786440 | tf_op jit(solution)/shard_map/ppermute | solution.py:17
  119.1 0.7 pad.4
  119.8 1.5 multiply_reduce_fusion
  121.4 6.6 %fusion.35 = bf16[2,128,8,64]{1,3,2,0:T(8,128)(2,1)S(1)} fusion(bf16[2,768,8,64]{1,3,2,0:T(8,128)(2,1)S(1)} %bitcast.170, f32[2,8,128]{2,1,0:T(8,128)S(1)} %bitcast.198, bf16[2,768,8,64]{1,3,2,0:T(8,128)(2,1)} %bitcast.182, f32[2,8,768,128]{3,2,1,0:T(8,128)} %copy-done, f32[2,8,128]{2,1,0:T(8,128)S(1)} %copy_add_fusion, ...), kind=kOutput, calls=%fused_computation.47 | convolution fusion | flops 414056448 | bytes 10511872 | tf_op jit(solution)/shard_map/bhqk,bkhd->bqhd/dot_general | solution.py:79
  128.3 1.0 reshape.385
  129.6 1.0 reshape.384
  130.6 0.9 gather_fusion.5
  131.5 0.9 gather_fusion.6
  132.4 0.9 gather_fusion.8
  133.2 0.9 gather_fusion.7
  134.2 1.2 convert_reduce_fusion
  135.4 3.0 %all-gather.6.cloned.1.call-done = bf16[2048,1024]{1,0:T(8,128)(2,1)} async-done(((bf16[256,1024]{1,0:T(8,128)(2,1)}), bf16[2048,1024]{1,0:T(8,128)(2,1)}) %all-gather.6.cloned.1.call-update) | async-done | bytes 4194320 | tf_op jit(solution)/shard_map/all_gather | solution.py:41
  138.3 2.9 %gather_fusion.9 = bf16[12,128,1024]{2,1,0:T(8,128)(2,1)S(1)} fusion(bf16[16,128,1024]{2,1,0:T(8,128)(2,1)} %bitcast.179, s32[1024]{0:T(1024)S(1)} %pad_clamp_fusion.4), kind=kCustom, calls=%fused_computation.9 | custom fusion | bytes 6291504 | tf_op jit(solution)/shard_map/gather | solution.py:102
  141.3 1.9 fusion.67
  143.2 1.7 copy.114
  144.9 1.7 copy.111
  146.7 4.8 %multiply_bitcast_fusion = f32[2,8,128,768]{2,3,1,0:T(8,128)} fusion(bf16[2,768,8,64]{1,3,2,0:T(8,128)(2,1)S(1)} %bitcast.171, bf16[2,128,8,64]{3,2,1,0:T(8,128)(2,1)} %reshape.386), kind=kOutput, calls=%fused_computation.18 | convolution fusion | flops 202899456 | bytes 8126464 | tf_op jit(solution)/shard_map/bkhd,bqhd->bhkq/dot_general | solution.py:112
  151.5 3.7 %convolution_bitcast_fusion = f32[2,8,128,768]{2,3,1,0:T(8,128)} fusion(bf16[2,768,8,64]{1,3,2,0:T(8,128)(2,1)S(1)} %bitcast.173, bf16[2,128,8,64]{3,2,1,0:T(8,128)(2,1)S(1)} %copy-done.9), kind=kOutput, calls=%fused_computation.31 | convolution fusion | flops 201326592 | bytes 8126464 | tf_op jit(solution)/shard_map/bkhd,bqhd->bhkq/dot_general | solution.py:113
  155.1 28.3 %all-gather.8.cloned.1.call-done = f32[2048,128]{1,0:T(8,128)} async-done(((f32[256,128]{1,0:T(8,128)}), f32[2048,128]{1,0:T(8,128)}) %all-gather.8.cloned.1.call-update) | async-done | bytes 1048592 | tf_op jit(solution)/shard_map/all_gather | solution.py:99
  183.5 0.9 slice.176
  184.4 0.6 gather_fusion.10
  185.1 8.8 %fusion.24 = f32[2,128,8,64]{1,3,2,0:T(8,128)} fusion(bf16[2,768,8,64]{1,3,2,0:T(8,128)(2,1)S(1)} %bitcast.174, f32[2,8,768]{2,1,0:T(8,128)S(1)} %get-tuple-element.48, f32[2,8,768]{2,1,0:T(8,128)S(1)} %get-tuple-element.46, f32[2,8,128,768]{2,3,1,0:T(8,128)} %multiply_bitcast_fusion, pred[2,768]{1,0:T(4,128)(4,1)S(1)} %bitcast.193), kind=kOutput, calls=%fused_computation.42 | convolution fusion | flops 207618048 | bytes 8488448 | tf_op jit(solution)/shard_map/bhkq,bqhd->bkhd/dot_general | solution.py:120
  193.9 5.7 %fusion.34 = f32[2,128,8,64]{1,3,2,0:T(8,128)S(1)} fusion(bf16[2,768,8,64]{1,3,2,0:T(8,128)(2,1)S(1)} %bitcast.172, f32[2,8,128,768]{2,3,1,0:T(8,128)S(1)} %bitcast.178, f32[2,8,768]{2,1,0:T(8,128)S(1)} %get-tuple-element.47, f32[2,8,768]{2,1,0:T(8,128)S(1)} %get-tuple-element.48, f32[2,8,768]{2,1,0:T(8,128)S(1)} %get-tuple-element.46, ...), kind=kOutput, calls=%fused_computation.46 | convolution fusion | flops 210894848 | bytes 14829056 | tf_op jit(solution)/shard_map/bhkq,bqhd->bkhd/dot_general | solution.py:119
  201.0 0.9 add_convert_fusion
  (98 shorter events, 5.9 us)
Async XLA Ops:
  7.2 33.9 %copy-start.12 = (bf16[256,512]{1,0:T(8,128)(2,1)S(1)}, bf16[256,512]{1,0:T(8,128)(2,1)}, u32[]{:S(2)}) copy-start(bf16[256,512]{1,0:T(8,128)(2,1)} %param.8) | copy-start | bytes 786436
  7.2 35.0 %copy-start.13 = (bf16[256,512]{1,0:T(8,128)(2,1)S(1)}, bf16[256,512]{1,0:T(8,128)(2,1)}, u32[]{:S(2)}) copy-start(bf16[256,512]{1,0:T(8,128)(2,1)} %param.9) | copy-start | bytes 786436
  7.2 69.8 %all-gather.4.cloned.1.call-start = ((), (), s32[]{:S(2)}) async-start(), calls=%async_computation | async-start | bytes 4718592 | tf_op jit(solution)/shard_map/all_gather | solution.py:40
  9.2 0.8 copy-start.6
  10.1 128.2 %all-gather.6.cloned.1.call-start = ((), (), s32[]{:S(2)}) async-start(), calls=%async_computation.1 | async-start | bytes 4718592 | tf_op jit(solution)/shard_map/all_gather | solution.py:41
  12.0 33.7 %collective-permute-start.2 = (bf16[128,1024]{1,0:T(8,128)(2,1)}, bf16[128,1024]{1,0:T(8,128)(2,1)S(1)}, u32[]{:S(2)}, u32[]{:S(2)}) collective-permute-start(bf16[128,1024]{1,0:T(8,128)(2,1)} %get-tuple-element.42), channel_id=1, source_target_pairs={{0,752},{8,760},{16,0},{24,8},{32,16},{40,24},{48,32},{56,40},{64,... | collective-permute-start | bytes 786440 | tf_op jit(solution)/shard_map/ppermute | solution.py:17
  23.5 23.2 %collective-permute-start = (bf16[128,1024]{1,0:T(8,128)(2,1)}, bf16[128,1024]{1,0:T(8,128)(2,1)S(1)}, u32[]{:S(2)}, u32[]{:S(2)}) collective-permute-start(bf16[128,1024]{1,0:T(8,128)(2,1)} %get-tuple-element.42), channel_id=1, source_target_pairs={{0,760},{8,0},{16,8},{24,16},{32,24},{40,32},{48,40},{56,48},{64,5... | collective-permute-start | bytes 786440 | tf_op jit(solution)/shard_map/ppermute | solution.py:17
  30.4 17.1 %collective-permute-start.3 = (bf16[128,1024]{1,0:T(8,128)(2,1)}, bf16[128,1024]{1,0:T(8,128)(2,1)S(1)}, u32[]{:S(2)}, u32[]{:S(2)}) collective-permute-start(bf16[128,1024]{1,0:T(8,128)(2,1)} %get-tuple-element.43), channel_id=1, source_target_pairs={{0,16},{8,24},{16,32},{24,40},{32,48},{40,56},{48,64},{56,72},{64,... | collective-permute-start | bytes 786440 | tf_op jit(solution)/shard_map/ppermute | solution.py:17
  32.3 16.0 %collective-permute-start.1 = (bf16[128,1024]{1,0:T(8,128)(2,1)}, bf16[128,1024]{1,0:T(8,128)(2,1)S(1)}, u32[]{:S(2)}, u32[]{:S(2)}) collective-permute-start(bf16[128,1024]{1,0:T(8,128)(2,1)} %get-tuple-element.43), channel_id=1, source_target_pairs={{0,8},{8,16},{16,24},{24,32},{32,40},{40,48},{48,56},{56,64},{64,7... | collective-permute-start | bytes 786440 | tf_op jit(solution)/shard_map/ppermute | solution.py:17
  36.2 147.3 %all-gather.8.cloned.1.call-start = ((), (), s32[]{:S(2)}) async-start(), calls=%async_computation.2 | async-start | bytes 1179648 | tf_op jit(solution)/shard_map/all_gather | solution.py:99
  43.3 5.9 %copy-start.7 = (bf16[2,128,8,64]{1,0,3,2:T(2,128)(2,1)}, bf16[2,128,8,64]{1,0,3,2:T(2,128)(2,1)S(1)}, u32[]{:S(2)}) copy-start(bf16[2,128,8,64]{1,0,3,2:T(2,128)(2,1)S(1)} %reshape.262) | copy-start | bytes 786436
  50.6 26.4 %copy-start.3 = (bf16[2,2,128,8,64]{2,1,4,3,0:T(2,128)(2,1)}, bf16[2,2,128,8,64]{2,1,4,3,0:T(2,128)(2,1)S(1)}, u32[]{:S(2)}) copy-start(bf16[2,2,128,8,64]{2,1,4,3,0:T(2,128)(2,1)S(1)} %reshape.264) | copy-start | bytes 1572868
  52.2 24.8 %copy-start.1 = (bf16[2,2,128,8,64]{2,1,4,3,0:T(2,128)(2,1)}, bf16[2,2,128,8,64]{2,1,4,3,0:T(2,128)(2,1)S(1)}, u32[]{:S(2)}) copy-start(bf16[2,2,128,8,64]{2,1,4,3,0:T(2,128)(2,1)S(1)} %reshape.263) | copy-start | bytes 1572868
  81.9 4.3 %copy-start.8 = (bf16[2,128,8,64]{1,0,3,2:T(2,128)(2,1)S(1)}, bf16[2,128,8,64]{1,0,3,2:T(2,128)(2,1)}, u32[]{:S(2)}) copy-start(bf16[2,128,8,64]{1,0,3,2:T(2,128)(2,1)} %copy-done.7) | copy-start | bytes 786436
  86.2 6.0 %copy-start.11 = (f32[2,128,8,64]{1,0,3,2:T(2,128)S(1)}, f32[2,128,8,64]{1,0,3,2:T(2,128)}, u32[]{:S(2)}) copy-start(f32[2,128,8,64]{1,0,3,2:T(2,128)} %copy.108) | copy-start | bytes 1572868
  88.1 2.7 %copy-start = (f32[2,8,768,128]{3,2,1,0:T(8,128)}, f32[2,8,768,128]{3,2,1,0:T(8,128)S(1)}, u32[]{:S(2)}) copy-start(f32[2,8,768,128]{3,2,1,0:T(8,128)S(1)} %get-tuple-element.54) | copy-start | bytes 18874372
  88.1 6.0 %copy-start.4 = (bf16[2,2,128,8,64]{2,1,4,3,0:T(2,128)(2,1)S(1)}, bf16[2,2,128,8,64]{2,1,4,3,0:T(2,128)(2,1)}, u32[]{:S(2)}) copy-start(bf16[2,2,128,8,64]{2,1,4,3,0:T(2,128)(2,1)} %copy-done.3) | copy-start | bytes 1572868
  94.8 6.3 %copy-start.10 = (f32[2,128,8,64]{1,0,3,2:T(2,128)S(1)}, f32[2,128,8,64]{1,0,3,2:T(2,128)}, u32[]{:S(2)}) copy-start(f32[2,128,8,64]{1,0,3,2:T(2,128)} %get-tuple-element.44) | copy-start | bytes 1572868
  94.8 25.0 %copy-start.2 = (bf16[2,2,128,8,64]{2,1,4,3,0:T(2,128)(2,1)S(1)}, bf16[2,2,128,8,64]{2,1,4,3,0:T(2,128)(2,1)}, u32[]{:S(2)}) copy-start(bf16[2,2,128,8,64]{2,1,4,3,0:T(2,128)(2,1)} %copy-done.1) | copy-start | bytes 1572868
  104.3 26.3 %collective-permute-start.4 = (bf16[128,1024]{1,0:T(8,128)(2,1)}, bf16[128,1024]{1,0:T(8,128)(2,1)S(1)}, u32[]{:S(2)}, u32[]{:S(2)}) collective-permute-start(bf16[128,1024]{1,0:T(8,128)(2,1)} %get-tuple-element.34), channel_id=1, source_target_pairs={{0,760},{8,0},{16,8},{24,16},{32,24},{40,32},{48,40},{56,48},{64,5... | collective-permute-start | bytes 786440 | tf_op jit(solution)/shard_map/ppermute | solution.py:17
  106.3 25.2 %collective-permute-start.5 = (bf16[128,1024]{1,0:T(8,128)(2,1)}, bf16[128,1024]{1,0:T(8,128)(2,1)S(1)}, u32[]{:S(2)}, u32[]{:S(2)}) collective-permute-start(bf16[128,1024]{1,0:T(8,128)(2,1)} %get-tuple-element.35), channel_id=1, source_target_pairs={{0,8},{8,16},{16,24},{24,32},{32,40},{40,48},{48,56},{56,64},{64,7... | collective-permute-start | bytes 786440 | tf_op jit(solution)/shard_map/ppermute | solution.py:17
  108.7 23.7 %collective-permute-start.7 = (bf16[128,1024]{1,0:T(8,128)(2,1)}, bf16[128,1024]{1,0:T(8,128)(2,1)S(1)}, u32[]{:S(2)}, u32[]{:S(2)}) collective-permute-start(bf16[128,1024]{1,0:T(8,128)(2,1)} %get-tuple-element.36), channel_id=1, source_target_pairs={{0,16},{8,24},{16,32},{24,40},{32,48},{40,56},{48,64},{56,72},{64,... | collective-permute-start | bytes 786440 | tf_op jit(solution)/shard_map/ppermute | solution.py:17
  112.1 21.2 %collective-permute-start.6 = (bf16[128,1024]{1,0:T(8,128)(2,1)}, bf16[128,1024]{1,0:T(8,128)(2,1)S(1)}, u32[]{:S(2)}, u32[]{:S(2)}) collective-permute-start(bf16[128,1024]{1,0:T(8,128)(2,1)} %get-tuple-element.37), channel_id=1, source_target_pairs={{0,752},{8,760},{16,0},{24,8},{32,16},{40,24},{48,32},{56,40},{64,... | collective-permute-start | bytes 786440 | tf_op jit(solution)/shard_map/ppermute | solution.py:17
  121.4 7.9 %copy-start.15 = (bf16[2,128,8,64]{1,3,2,0:T(8,128)(2,1)S(1)}, bf16[2,128,8,64]{1,3,2,0:T(8,128)(2,1)}, u32[]{:S(2)}) copy-start(bf16[2,128,8,64]{1,3,2,0:T(8,128)(2,1)} %get-tuple-element.41) | copy-start | bytes 786436
  146.7 4.8 %copy-start.9 = (bf16[2,128,8,64]{3,2,1,0:T(8,128)(2,1)S(1)}, bf16[2,128,8,64]{3,2,1,0:T(8,128)(2,1)}, u32[]{:S(2)}) copy-start(bf16[2,128,8,64]{3,2,1,0:T(8,128)(2,1)} %reshape.387) | copy-start | bytes 786436
  185.0 8.8 %slice-start = ((s8[6291456]{0:T(1024)(128)(4,1)}), s8[4194304]{0:T(1024)(128)(4,1)S(1)}, s32[]{:S(2)}) async-start(s8[6291456]{0:T(1024)(128)(4,1)} %bitcast.175), calls=%async_computation.3 | async-start | bytes 8388608
  185.0 8.8 %slice-start.2 = ((s8[6291456]{0:T(1024)(128)(4,1)}), s8[4194304]{0:T(1024)(128)(4,1)S(1)}, s32[]{:S(2)}) async-start(s8[6291456]{0:T(1024)(128)(4,1)} %bitcast.177), calls=%async_computation.5 | async-start | bytes 8388608
  185.0 8.8 %slice-start.1 = ((s8[6291456]{0:T(1024)(128)(4,1)}), s8[2097152]{0:T(1024)(128)(4,1)S(1)}, s32[]{:S(2)}) async-start(s8[6291456]{0:T(1024)(128)(4,1)} %bitcast.175), calls=%async_computation.4 | async-start | bytes 4194304
  185.0 8.8 %slice-start.3 = ((s8[6291456]{0:T(1024)(128)(4,1)}), s8[2097152]{0:T(1024)(128)(4,1)S(1)}, s32[]{:S(2)}) async-start(s8[6291456]{0:T(1024)(128)(4,1)} %bitcast.177), calls=%async_computation.6 | async-start | bytes 4194304
  193.9 6.4 %copy-start.14 = (f32[2,128,8,64]{1,3,2,0:T(8,128)S(1)}, f32[2,128,8,64]{1,3,2,0:T(8,128)}, u32[]{:S(2)}) copy-start(f32[2,128,8,64]{1,3,2,0:T(8,128)} %fusion.24) | copy-start | bytes 1572868
  199.6 1.4 copy-start.5
Sparse Core Ops, SparseCore 0:
  10.4 66.5 all-gather.3
  79.4 58.9 all-gather.5
  140.7 42.6 all-gather.7

commit v4 on v3

--- a/solution.py
+++ b/solution.py
@@ -72,6 +72,10 @@
     out_full = jnp.einsum("bhqk,bkhd->bqhd", w_loc, v_tile, preferred_element_type=f32)
     out_full = out_full + jnp.einsum("bhqr,rbqhd->bqhd", w_pair, v_pair, preferred_element_type=f32)
     delta = jnp.transpose(jnp.sum(g4.astype(f32) * out_full, -1), (0, 2, 1))
+
+    stats = jnp.stack([top, total, delta], 1).reshape(blocks_dev * 3 * HEADS, BLOCK)
+    stats_cluster = lax.all_gather(stats, "blk", axis=0, tiled=True)
+    stats_cluster, delta = lax.optimization_barrier((stats_cluster, delta))
     d_loc = jnp.einsum("bqhd,bkhd->bhqk", g4, v_tile, preferred_element_type=f32)
     d_pair = jnp.einsum("bqhd,rbqhd->bhqr", g4, v_pair, preferred_element_type=f32)
     z_loc = (p_loc * (d_loc - delta[..., None])).astype(bf16)
@@ -93,12 +97,6 @@
     returned = jnp.sum(returned.astype(f32), 0)
     returned, qg_cluster = lax.optimization_barrier((returned, qg_cluster))
 
-    stats = jnp.stack([top, total, delta], 1).reshape(blocks_dev * 3 * HEADS, BLOCK)
-    rows = stats.shape[0]
-    stats = jnp.pad(stats, ((0, nodes - rows), (0, 0)))
-    stats_cluster = lax.all_gather(stats, "blk", axis=0, tiled=True)
-    stats_cluster = stats_cluster.reshape(team, nodes, BLOCK)[:, :rows]
-
     qg_tiles = qg_cluster.reshape(cluster_blocks, BLOCK, 2 * width)[tiles].reshape(
         blocks_dev, keys_tile, 2 * width
     )
@@ -111,7 +109,6 @@
     v4 = value.reshape(heads4)
     s_key = jnp.einsum("bkhd,bqhd->bhkq", k4, q_tile, preferred_element_type=f32) * scale
     d_key = jnp.einsum("bkhd,bqhd->bhkq", v4, g_tile, preferred_element_type=f32)
-    s_key, d_key = lax.optimization_barrier((s_key, d_key))
     s_key = jnp.where(tile_live[:, None, None, :], s_key, NEG_BIG)
     p_key = jnp.exp(s_key - top_t[:, :, None, :]) / total_t[:, :, None, :]
     w_key = p_key.astype(bf16)

time: 209 us -> 213 us (1.019)
  the two profiles are of different devices: /device:TPU:2 before, /device:TPU:24 now
where the time goes in v4:
time: 213 us; the launch traced here: 212 us
  local copies, waits for them, and re-layouts  54.3 us (25%)
  starting transfers between devices  43.6 us (20%)
  matrix products  29.8 us (14%)
  blocking collectives  27.3 us (13%)
  waiting for transfers between devices  23.2 us (11%)
  other arithmetic  19.1 us (9%)
  between operations  14.7 us (7%)
    ppermute x8, starting transfers between devices, passed_along(): return lax.ppermute(x, axis, [(i, (i + by) % size) for i in range(size)])  43.6 us
    all_gather x1, blocking collectives, shards(): stats_cluster = lax.all_gather(stats, 'blk', axis=0, tiled=True)  27.3 us
    all_gather x1, waiting for transfers between devices, shards(): kv_cluster = lax.all_gather(both, 'blk', axis=0, tiled=True)  23.1 us
    unnamed x45, local copies, waits for them, and re-layouts  11.1 us
    gather x8, local copies, waits for them, and re-layouts, fetch_partners(): return jnp.concatenate([ahead[slots[:half]], behind[slots[half:]]], 0)  7.59 us
    dot_general x1, matrix products, shards(): jnp.einsum('bhqk,bkhd->bqhd', z_loc, k_tile, preferred_element_type=f32)  7.18 us
    dot_general x1, matrix products, shards(): jnp.einsum('bhkq,bqhd->bkhd', z_key, q_tile, preferred_element_type=f32)  6.53 us
    dot_general x1, matrix products, shards(): jnp.einsum('bhqk,bkhd->bqhd', w_loc, v_tile, preferred_element_type=f32)  6.34 us
  transfers between devices with their start and end apart: 10, of which 1 were waited for; matrix products, arithmetic and copies ran while one was open for 30% of the time, Pallas kernels for 0%

profile of v4, /device:TPU:24, one launch (start us, length us, event | category | flops | bytes accessed | tf_op | source)
XLA Modules:
  0.0 212.0 jit_solution(15688780610944311057)
XLA Ops:
  7.3 1.0 constant_dynamic-update-slice_fusion.1
  8.3 1.0 constant_dynamic-update-slice_fusion
  9.3 0.8 copy-done.6
  10.1 1.9 fusion.70
  12.0 3.4 %collective-permute-start.3 = (bf16[128,1024]{1,0:T(8,128)(2,1)}, bf16[128,1024]{1,0:T(8,128)(2,1)S(1)}, u32[]{:S(2)}, u32[]{:S(2)}) collective-permute-start(bf16[128,1024]{1,0:T(8,128)(2,1)} %get-tuple-element.43), channel_id=1, source_target_pairs={{0,16},{8,24},{16,32},{24,40},{32,48},{40,56},{48,64},{56,72},{64,... | collective-permute-start | bytes 786440 | tf_op jit(solution)/shard_map/ppermute | solution.py:17
  15.4 1.9 collective-permute-start.1
  17.3 15.3 %collective-permute-start.2 = (bf16[128,1024]{1,0:T(8,128)(2,1)}, bf16[128,1024]{1,0:T(8,128)(2,1)S(1)}, u32[]{:S(2)}, u32[]{:S(2)}) collective-permute-start(bf16[128,1024]{1,0:T(8,128)(2,1)} %get-tuple-element.42), channel_id=1, source_target_pairs={{0,752},{8,760},{16,0},{24,8},{32,16},{40,24},{48,32},{56,40},{64,... | collective-permute-start | bytes 786440 | tf_op jit(solution)/shard_map/ppermute | solution.py:17
  32.6 3.4 %collective-permute-start = (bf16[128,1024]{1,0:T(8,128)(2,1)}, bf16[128,1024]{1,0:T(8,128)(2,1)S(1)}, u32[]{:S(2)}, u32[]{:S(2)}) collective-permute-start(bf16[128,1024]{1,0:T(8,128)(2,1)} %get-tuple-element.42), channel_id=1, source_target_pairs={{0,760},{8,0},{16,8},{24,16},{32,24},{40,32},{48,40},{56,48},{64,5... | collective-permute-start | bytes 786440 | tf_op jit(solution)/shard_map/ppermute | solution.py:17
  36.0 1.9 pad_maximum_fusion.1
  38.8 1.2 fusion.71
  40.1 1.1 reshape.382
  41.2 2.1 reshape.383
  43.3 1.2 copy.101
  44.5 0.9 gather_fusion.4
  45.4 1.6 gather_fusion.3
  46.9 0.9 gather_fusion.2
  47.8 1.0 maximum_bitcast_fusion.1
  48.8 0.9 gather_fusion.1
  49.7 0.9 pad_maximum_fusion
  51.0 0.6 multiply_reduce_fusion.3
  51.5 1.3 copy.92
  52.9 0.6 multiply_reduce_fusion.1
  53.5 23.1 %all-gather.3.cloned.1.call-done = bf16[2048,1024]{1,0:T(8,128)(2,1)} async-done(((bf16[256,1024]{1,0:T(8,128)(2,1)}), bf16[2048,1024]{1,0:T(8,128)(2,1)}) %all-gather.3.cloned.1.call-update) | async-done | bytes 4194320 | tf_op jit(solution)/shard_map/all_gather | solution.py:40
  76.6 2.9 %gather_fusion = bf16[12,128,1024]{2,1,0:T(8,128)(2,1)S(1)} fusion(bf16[16,128,1024]{2,1,0:T(8,128)(2,1)} %bitcast.171, s32[1024]{0:T(1024)S(1)} %pad_clamp_fusion.4), kind=kCustom, calls=%fused_computation | custom fusion | bytes 6291504 | tf_op jit(solution)/shard_map/gather | solution.py:50
  79.6 2.0 fusion.69
  81.6 1.7 copy.83
  83.3 2.8 %bitcast_reduce_fusion = (f32[2,8,128]{2,1,0:T(8,128)S(1)}, f32[2,8,768,128]{3,2,1,0:T(8,128)S(1)}) fusion(pred[2,768]{1,0:T(4,128)(4,1)S(1)} %bitcast.180, bf16[2,768,8,64]{1,3,2,0:T(8,128)(2,1)S(1)} %bitcast.166, bf16[2,128,8,64]{1,0,3,2:T(2,128)(2,1)} %copy-done.7), kind=kOutput, calls=%fused_computation.14 | convolution fusion | flops 206043136 | bytes 8136192 | tf_op jit(solution)/shard_map/bqhd,bkhd->bhqk/dot_general | solution.py:61
  86.2 2.6 %copy-done = f32[2,8,768,128]{3,2,1,0:T(8,128)} copy-done((f32[2,8,768,128]{3,2,1,0:T(8,128)}, f32[2,8,768,128]{3,2,1,0:T(8,128)S(1)}, u32[]{:S(2)}) %copy-start) | copy-done | bytes 6291480
  88.8 1.4 fusion.3
  90.3 1.6 copy.82
  91.9 2.0 multiply_reduce_fusion.2
  93.9 6.3 %multiply_reduce_fusion.4 = (f32[2,128,8]{1,2,0:T(8,128)S(1)}, bf16[2,128,8,64]{1,3,2,0:T(8,128)(2,1)}) fusion(bf16[2,128,8,64]{1,0,3,2:T(2,128)(2,1)S(1)} %reshape.262, f32[2,128,8,64]{1,0,3,2:T(2,128)S(1)} %multiply_reduce_fusion.2, bf16[2,768,8,64]{1,3,2,0:T(8,128)(2,1)} %bitcast.172, f32[2,8,128]{2,1,0:T(8,128)S(1)} %copy_add_fusion, ...), kind=kOutput, calls=%fused_computation.68 | convolution fusion | flops 209844224 | bytes 8939008 | tf_op jit(solution)/shard_map/bhqk,bkhd->bqhd/dot_general | solution.py:72
  100.3 27.3 %all_gather.10 = f32[384,128]{1,0:T(8,128)} all-gather(f32[48,128]{1,0:T(8,128)S(1)} %bitcast.178), channel_id=1, replica_groups=mesh['grp'=96,'blk'=8] {'blk'}, dimensions={0}, use_global_device_ids=true | all-gather | bytes 221184 | tf_op jit(solution)/shard_map/all_gather | solution.py:77
  127.7 1.3 fusion.42
  129.0 1.4 reshape.264
  130.4 1.0 copy.102
  132.4 2.1 %fusion.51 = (bf16[128,1024]{1,0:T(8,128)(2,1)}, bf16[128,1024]{1,0:T(8,128)(2,1)}, bf16[128,1024]{1,0:T(8,128)(2,1)}, bf16[128,1024]{1,0:T(8,128)(2,1)}) fusion(bf16[2,256,512]{2,1,0:T(8,128)(2,1)} %copy.102, bf16[2,256,512]{2,1,0:T(8,128)(2,1)S(1)} %copy.103), kind=kLoop, calls=%fused_computation.72 | loop fusion | flops 2097152 | bytes 2097152 | tf_op jit(solution)/shard_map/slice | solution.py:22
  134.6 3.4 %collective-permute-start.7 = (bf16[128,1024]{1,0:T(8,128)(2,1)}, bf16[128,1024]{1,0:T(8,128)(2,1)S(1)}, u32[]{:S(2)}, u32[]{:S(2)}) collective-permute-start(bf16[128,1024]{1,0:T(8,128)(2,1)} %get-tuple-element.36), channel_id=1, source_target_pairs={{0,16},{8,24},{16,32},{24,40},{32,48},{40,56},{48,64},{56,72},{64,... | collective-permute-start | bytes 786440 | tf_op jit(solution)/shard_map/ppermute | solution.py:17
  137.9 7.4 %collective-permute-start.6 = (bf16[128,1024]{1,0:T(8,128)(2,1)}, bf16[128,1024]{1,0:T(8,128)(2,1)S(1)}, u32[]{:S(2)}, u32[]{:S(2)}) collective-permute-start(bf16[128,1024]{1,0:T(8,128)(2,1)} %get-tuple-element.37), channel_id=1, source_target_pairs={{0,752},{8,760},{16,0},{24,8},{32,16},{40,24},{48,32},{56,40},{64,... | collective-permute-start | bytes 786440 | tf_op jit(solution)/shard_map/ppermute | solution.py:17
  145.3 1.9 collective-permute-start.5
  147.2 7.0 %collective-permute-start.4 = (bf16[128,1024]{1,0:T(8,128)(2,1)}, bf16[128,1024]{1,0:T(8,128)(2,1)S(1)}, u32[]{:S(2)}, u32[]{:S(2)}) collective-permute-start(bf16[128,1024]{1,0:T(8,128)(2,1)} %get-tuple-element.34), channel_id=1, source_target_pairs={{0,760},{8,0},{16,8},{24,16},{32,24},{40,32},{48,40},{56,48},{64,5... | collective-permute-start | bytes 786440 | tf_op jit(solution)/shard_map/ppermute | solution.py:17
  154.2 1.6 multiply_reduce_fusion
  155.8 7.2 %fusion.37 = bf16[2,128,8,64]{1,3,2,0:T(8,128)(2,1)} fusion(bf16[2,768,8,64]{1,3,2,0:T(8,128)(2,1)S(1)} %bitcast.167, f32[2,8,128]{2,1,0:T(8,128)S(1)} %bitcast.187, bf16[2,768,8,64]{1,3,2,0:T(8,128)(2,1)} %bitcast.173, f32[2,8,768,128]{3,2,1,0:T(8,128)} %copy-done, f32[2,8,128]{2,1,0:T(8,128)S(1)} %copy_add_fusion, f32[2,8,128]{2,1,0:T(8,128)S(1)} %copy_maximum_fusion, ...), kind=kOutput, calls=%fused_computation.46 | convolution fusion | flops 414056448 | bytes 10511872 | tf_op jit(solution)/shard_map/bhqk,bkhd->bqhd/dot_general | solution.py:83
  163.3 1.0 reshape.380
  164.3 1.2 copy.150
  165.6 1.0 reshape.381
  166.6 0.6 gather_fusion.10
  167.2 0.9 gather_fusion.8
  168.1 0.9 gather_fusion.7
  169.0 0.9 gather_fusion.6
  169.8 0.9 gather_fusion.5
  170.8 1.2 convert_reduce_fusion
  172.0 2.9 %gather_fusion.9 = bf16[12,128,1024]{2,1,0:T(8,128)(2,1)S(1)} fusion(bf16[16,128,1024]{2,1,0:T(8,128)(2,1)} %bitcast.170, s32[1024]{0:T(1024)S(1)} %pad_clamp_fusion.4), kind=kCustom, calls=%fused_computation.9 | custom fusion | bytes 6291504 | tf_op jit(solution)/shard_map/gather | solution.py:100
  174.9 2.0 fusion.68
  176.9 1.7 copy.108
  178.6 1.7 copy.104
  180.3 5.5 %exponential_divide_fusion = f32[2,8,768,128]{3,2,1,0:T(8,128)S(1)} fusion(f32[2,8,768]{2,1,0:T(8,128)S(1)} %get-tuple-element.47, f32[2,8,768]{2,1,0:T(8,128)S(1)} %get-tuple-element.48, pred[2,768]{1,0:T(4,128)(4,1)S(1)} %bitcast.184, bf16[2,768,8,64]{1,3,2,0:T(8,128)(2,1)S(1)} %bitcast.168, bf16[2,128,8,64]{3,2,1,0:T(8,128)(2,1)} %reshape.382), kind=kOutput, calls=%fused_computation.17 | convolution fusion | flops 207618048 | bytes 8226304 | tf_op jit(solution)/shard_map/bkhd,bqhd->bhkq/dot_general | solution.py:110
  185.8 2.7 %copy-done.1 = f32[2,8,768,128]{3,2,1,0:T(8,128)} copy-done((f32[2,8,768,128]{3,2,1,0:T(8,128)}, f32[2,8,768,128]{3,2,1,0:T(8,128)S(1)}, u32[]{:S(2)}) %copy-start.1) | copy-done | bytes 6291480
  188.4 1.5 fusion.23
  189.9 2.4 %copy.156 = f32[2,128,8,64]{3,2,1,0:T(8,128)} copy(f32[2,128,8,64]{1,3,2,0:T(8,128)} %fusion.23) | data formatting | bytes 1048576 | tf_op jit(solution)/shard_map/reshape | solution.py:122
  192.3 2.3 %reshape.385 = f32[256,512]{1,0:T(8,128)} reshape(f32[2,128,8,64]{3,2,1,0:T(8,128)} %copy.156) | data formatting | bytes 1048576 | tf_op jit(solution)/shard_map/reshape | solution.py:122
  194.6 6.5 %fusion.36 = f32[2,128,8,64]{1,3,2,0:T(8,128)} fusion(bf16[2,768,8,64]{1,3,2,0:T(8,128)(2,1)S(1)} %bitcast.169, f32[2,8,768,128]{3,2,1,0:T(8,128)} %copy-done.1, f32[2,8,768]{2,1,0:T(8,128)S(1)} %get-tuple-element.46, bf16[2,768,8,64]{1,3,2,0:T(8,128)(2,1)S(1)} %bitcast.163, bf16[2,128,8,64]{3,2,1,0:T(8,128)(2,1)} %reshape.383), kind=kOutput, calls=%fused_computation.45 | convolution fusion | flops 407502848 | bytes 10272768 | tf_op jit(solution)/shard_map/bhkq,bqhd->bkhd/dot_general | solution.py:116
  201.1 1.4 copy.155
  202.8 2.3 %add_convert_fusion = (bf16[256,512]{1,0:T(8,128)(2,1)}, bf16[256,512]{1,0:T(8,128)(2,1)}) fusion(f32[256,512]{1,0:T(8,128)} %reshape.385, f32[256,1024]{1,0:T(8,128)} %convert_reduce_fusion, f32[256,512]{1,0:T(8,128)S(1)} %reshape.384), kind=kLoop, calls=%fused_computation.66 | loop fusion | flops 524288 | bytes 2621440 | tf_op jit(solution)/shard_map/convert_element_type | solution.py:122
  (87 shorter events, 3.4 us)
Async XLA Ops:
  7.2 30.7 %copy-start.11 = (bf16[256,512]{1,0:T(8,128)(2,1)S(1)}, bf16[256,512]{1,0:T(8,128)(2,1)}, u32[]{:S(2)}) copy-start(bf16[256,512]{1,0:T(8,128)(2,1)} %param.10) | copy-start | bytes 786436
  7.2 30.9 %copy-start.12 = (bf16[256,512]{1,0:T(8,128)(2,1)S(1)}, bf16[256,512]{1,0:T(8,128)(2,1)}, u32[]{:S(2)}) copy-start(bf16[256,512]{1,0:T(8,128)(2,1)} %param.7) | copy-start | bytes 786436
  7.2 31.3 %copy-start.17 = (s32[2]{0:T(128)S(1)}, s32[2]{0:T(128)}, u32[]{:S(2)}) copy-start(s32[2]{0:T(128)} %param.13) | copy-start | bytes 28
  7.2 31.5 %copy-start.16 = (s32[2,6]{1,0:T(2,128)S(1)}, s32[2,6]{1,0:T(2,128)}, u32[]{:S(2)}) copy-start(s32[2,6]{1,0:T(2,128)} %param.12) | copy-start | bytes 148
  7.2 69.4 %all-gather.3.cloned.1.call-start = ((), (), s32[]{:S(2)}) async-start(), calls=%async_computation | async-start | bytes 4718592 | tf_op jit(solution)/shard_map/all_gather | solution.py:40
  9.3 0.8 copy-start.6
  9.3 30.7 %copy-start.15 = (s32[2,256]{1,0:T(2,128)S(1)}, s32[2,256]{1,0:T(2,128)}, u32[]{:S(2)}) copy-start(s32[2,256]{1,0:T(2,128)} %param.11) | copy-start | bytes 6148
  9.3 30.8 %copy-start.10 = (bf16[256,512]{1,0:T(8,128)(2,1)S(1)}, bf16[256,512]{1,0:T(8,128)(2,1)}, u32[]{:S(2)}) copy-start(bf16[256,512]{1,0:T(8,128)(2,1)} %param.8) | copy-start | bytes 786436
  10.1 161.9 %all-gather.5.cloned.1.call-start = ((), (), s32[]{:S(2)}) async-start(), calls=%async_computation.1 | async-start | bytes 4718592 | tf_op jit(solution)/shard_map/all_gather | solution.py:41
  12.0 32.5 %collective-permute-start.3 = (bf16[128,1024]{1,0:T(8,128)(2,1)}, bf16[128,1024]{1,0:T(8,128)(2,1)S(1)}, u32[]{:S(2)}, u32[]{:S(2)}) collective-permute-start(bf16[128,1024]{1,0:T(8,128)(2,1)} %get-tuple-element.43), channel_id=1, source_target_pairs={{0,16},{8,24},{16,32},{24,40},{32,48},{40,56},{48,64},{56,72},{64,... | collective-permute-start | bytes 786440 | tf_op jit(solution)/shard_map/ppermute | solution.py:17
  15.4 31.5 %collective-permute-start.1 = (bf16[128,1024]{1,0:T(8,128)(2,1)}, bf16[128,1024]{1,0:T(8,128)(2,1)S(1)}, u32[]{:S(2)}, u32[]{:S(2)}) collective-permute-start(bf16[128,1024]{1,0:T(8,128)(2,1)} %get-tuple-element.43), channel_id=1, source_target_pairs={{0,8},{8,16},{16,24},{24,32},{32,40},{40,48},{48,56},{56,64},{64,7... | collective-permute-start | bytes 786440 | tf_op jit(solution)/shard_map/ppermute | solution.py:17
  17.3 28.0 %collective-permute-start.2 = (bf16[128,1024]{1,0:T(8,128)(2,1)}, bf16[128,1024]{1,0:T(8,128)(2,1)S(1)}, u32[]{:S(2)}, u32[]{:S(2)}) collective-permute-start(bf16[128,1024]{1,0:T(8,128)(2,1)} %get-tuple-element.42), channel_id=1, source_target_pairs={{0,752},{8,760},{16,0},{24,8},{32,16},{40,24},{48,32},{56,40},{64,... | collective-permute-start | bytes 786440 | tf_op jit(solution)/shard_map/ppermute | solution.py:17
  32.6 16.2 %collective-permute-start = (bf16[128,1024]{1,0:T(8,128)(2,1)}, bf16[128,1024]{1,0:T(8,128)(2,1)S(1)}, u32[]{:S(2)}, u32[]{:S(2)}) collective-permute-start(bf16[128,1024]{1,0:T(8,128)(2,1)} %get-tuple-element.42), channel_id=1, source_target_pairs={{0,760},{8,0},{16,8},{24,16},{32,24},{40,32},{48,40},{56,48},{64,5... | collective-permute-start | bytes 786440 | tf_op jit(solution)/shard_map/ppermute | solution.py:17
  38.8 8.2 %copy-start.7 = (bf16[2,128,8,64]{1,0,3,2:T(2,128)(2,1)}, bf16[2,128,8,64]{1,0,3,2:T(2,128)(2,1)S(1)}, u32[]{:S(2)}) copy-start(bf16[2,128,8,64]{1,0,3,2:T(2,128)(2,1)S(1)} %reshape.259) | copy-start | bytes 786436
  51.0 25.7 %copy-start.3 = (bf16[2,2,128,8,64]{2,1,4,3,0:T(2,128)(2,1)}, bf16[2,2,128,8,64]{2,1,4,3,0:T(2,128)(2,1)S(1)}, u32[]{:S(2)}) copy-start(bf16[2,2,128,8,64]{2,1,4,3,0:T(2,128)(2,1)S(1)} %reshape.260) | copy-start | bytes 1572868
  52.9 23.7 %copy-start.5 = (bf16[2,2,128,8,64]{2,1,4,3,0:T(2,128)(2,1)}, bf16[2,2,128,8,64]{2,1,4,3,0:T(2,128)(2,1)S(1)}, u32[]{:S(2)}) copy-start(bf16[2,2,128,8,64]{2,1,4,3,0:T(2,128)(2,1)S(1)} %reshape.261) | copy-start | bytes 1572868
  86.1 2.7 %copy-start = (f32[2,8,768,128]{3,2,1,0:T(8,128)}, f32[2,8,768,128]{3,2,1,0:T(8,128)S(1)}, u32[]{:S(2)}) copy-start(f32[2,8,768,128]{3,2,1,0:T(8,128)S(1)} %get-tuple-element.54) | copy-start | bytes 18874372
  86.1 4.1 %copy-start.2 = (bf16[2,768,512]{2,1,0:T(8,128)(2,1)S(1)}, bf16[2,768,512]{2,1,0:T(8,128)(2,1)}, u32[]{:S(2)}) copy-start(bf16[2,768,512]{2,1,0:T(8,128)(2,1)} %get-tuple-element.31) | copy-start | bytes 4718596
  93.9 33.7 %copy-start.8 = (f32[2,128,8,64]{1,0,3,2:T(2,128)S(1)}, f32[2,128,8,64]{1,0,3,2:T(2,128)}, u32[]{:S(2)}) copy-start(f32[2,128,8,64]{1,0,3,2:T(2,128)} %get-tuple-element.44) | copy-start | bytes 1572868
  93.9 37.5 %copy-start.9 = (f32[2,128,8,64]{1,0,3,2:T(2,128)S(1)}, f32[2,128,8,64]{1,0,3,2:T(2,128)}, u32[]{:S(2)}) copy-start(f32[2,128,8,64]{1,0,3,2:T(2,128)} %copy.101) | copy-start | bytes 1572868
  127.7 26.6 %copy-start.4 = (bf16[2,2,128,8,64]{2,1,4,3,0:T(2,128)(2,1)S(1)}, bf16[2,2,128,8,64]{2,1,4,3,0:T(2,128)(2,1)}, u32[]{:S(2)}) copy-start(bf16[2,2,128,8,64]{2,1,4,3,0:T(2,128)(2,1)} %copy-done.3) | copy-start | bytes 1572868
  134.6 32.6 %collective-permute-start.7 = (bf16[128,1024]{1,0:T(8,128)(2,1)}, bf16[128,1024]{1,0:T(8,128)(2,1)S(1)}, u32[]{:S(2)}, u32[]{:S(2)}) collective-permute-start(bf16[128,1024]{1,0:T(8,128)(2,1)} %get-tuple-element.36), channel_id=1, source_target_pairs={{0,16},{8,24},{16,32},{24,40},{32,48},{40,56},{48,64},{56,72},{64,... | collective-permute-start | bytes 786440 | tf_op jit(solution)/shard_map/ppermute | solution.py:17
  137.9 30.1 %collective-permute-start.6 = (bf16[128,1024]{1,0:T(8,128)(2,1)}, bf16[128,1024]{1,0:T(8,128)(2,1)S(1)}, u32[]{:S(2)}, u32[]{:S(2)}) collective-permute-start(bf16[128,1024]{1,0:T(8,128)(2,1)} %get-tuple-element.37), channel_id=1, source_target_pairs={{0,752},{8,760},{16,0},{24,8},{32,16},{40,24},{48,32},{56,40},{64,... | collective-permute-start | bytes 786440 | tf_op jit(solution)/shard_map/ppermute | solution.py:17
  145.3 23.7 %collective-permute-start.5 = (bf16[128,1024]{1,0:T(8,128)(2,1)}, bf16[128,1024]{1,0:T(8,128)(2,1)S(1)}, u32[]{:S(2)}, u32[]{:S(2)}) collective-permute-start(bf16[128,1024]{1,0:T(8,128)(2,1)} %get-tuple-element.35), channel_id=1, source_target_pairs={{0,8},{8,16},{16,24},{24,32},{32,40},{40,48},{48,56},{56,64},{64,7... | collective-permute-start | bytes 786440 | tf_op jit(solution)/shard_map/ppermute | solution.py:17
  147.2 22.6 %collective-permute-start.4 = (bf16[128,1024]{1,0:T(8,128)(2,1)}, bf16[128,1024]{1,0:T(8,128)(2,1)S(1)}, u32[]{:S(2)}, u32[]{:S(2)}) collective-permute-start(bf16[128,1024]{1,0:T(8,128)(2,1)} %get-tuple-element.34), channel_id=1, source_target_pairs={{0,760},{8,0},{16,8},{24,16},{32,24},{40,32},{48,40},{56,48},{64,5... | collective-permute-start | bytes 786440 | tf_op jit(solution)/shard_map/ppermute | solution.py:17
  155.8 7.2 %copy-start.14 = (bf16[2,128,8,64]{1,3,2,0:T(8,128)(2,1)S(1)}, bf16[2,128,8,64]{1,3,2,0:T(8,128)(2,1)}, u32[]{:S(2)}) copy-start(bf16[2,128,8,64]{1,3,2,0:T(8,128)(2,1)} %get-tuple-element.41) | copy-start | bytes 786436
  155.8 10.8 %copy-start.13 = (f32[384,128]{1,0:T(8,128)S(1)}, f32[384,128]{1,0:T(8,128)}, u32[]{:S(2)}) copy-start(f32[384,128]{1,0:T(8,128)} %all_gather.10) | copy-start | bytes 589828
  185.8 2.7 %copy-start.1 = (f32[2,8,768,128]{3,2,1,0:T(8,128)}, f32[2,8,768,128]{3,2,1,0:T(8,128)S(1)}, u32[]{:S(2)}) copy-start(f32[2,8,768,128]{3,2,1,0:T(8,128)S(1)} %exponential_divide_fusion) | copy-start | bytes 18874372
Sparse Core Ops, SparseCore 0:
  10.4 66.1 all-gather.2
  79.0 60.7 all-gather.4

commit v5 on v4

--- a/solution.py
+++ b/solution.py
@@ -1,6 +1,10 @@
+import functools
+
 import jax
 import jax.numpy as jnp
 from jax import lax
+from jax.experimental import pallas as pl
+from jax.experimental.pallas import tpu as pltpu
 from jax.sharding import PartitionSpec as P
 
 HEADS = 8
@@ -22,6 +26,71 @@
     ahead = passed_along(load[half:], "grp", -offset)
     behind = passed_along(load[:half], "grp", offset)
     return jnp.concatenate([ahead[slots[:half]], behind[slots[half:]]], 0)
+
+
+def key_side_kernel(count_ref, qg_ref, st_ref, k_ref, v_ref, ks_ref, vs_ref, *, scale):
+    b = pl.program_id(0)
+    width = k_ref.shape[-1]
+    keys = qg_ref.shape[1]
+    pair = 2 * (width // HEADS)
+    half = pair // 2
+    live = (lax.broadcasted_iota(jnp.int32, (1, keys), 1) // BLOCK) < count_ref[b]
+    low = lax.broadcasted_iota(jnp.int32, (1, pair), 1) < half
+    nt = (((1,), (1,)), ((), ()))
+    for pr in range(width // pair):
+        cols = pl.ds(pr * pair, pair)
+        kp = k_ref[0, :, cols]
+        vp = v_ref[0, :, cols]
+        qp = qg_ref[0, :, cols]
+        gp = qg_ref[0, :, pl.ds(width + pr * pair, pair)]
+        zero = jnp.zeros_like(kp)
+        k_out = []
+        v_out = []
+        for side in range(2):
+            mine = low if side == 0 else jnp.logical_not(low)
+            h = 2 * pr + side
+            kh = jnp.where(mine, kp, zero)
+            vh = jnp.where(mine, vp, zero)
+            s = lax.dot_general(kh, qp, nt, preferred_element_type=jnp.float32) * scale
+            d = lax.dot_general(vh, gp, nt, preferred_element_type=jnp.float32)
+            top = st_ref[0, 0, pl.ds(h, 1), :]
+            total = st_ref[0, 1, pl.ds(h, 1), :]
+            delta = st_ref[0, 2, pl.ds(h, 1), :]
+            p = jnp.where(live, jnp.exp(s - top) / total, 0.0)
+            w = p.astype(jnp.bfloat16)
+            z = (p * (d - delta)).astype(jnp.bfloat16)
+            k_out.append(jnp.dot(z, qp, preferred_element_type=jnp.float32))
+            v_out.append(jnp.dot(w, gp, preferred_element_type=jnp.float32))
+        ks_ref[0, :, cols] = jnp.where(low, k_out[0], k_out[1]) * scale
+        vs_ref[0, :, cols] = jnp.where(low, v_out[0], v_out[1])
+
+
+def key_side(tile_count, qg_tiles, st, k3, v3, scale):
+    blocks, keys, width2 = qg_tiles.shape
+    width = width2 // 2
+    grid_spec = pltpu.PrefetchScalarGridSpec(
+        num_scalar_prefetch=1,
+        grid=(blocks,),
+        in_specs=[
+            pl.BlockSpec((1, keys, width2), lambda b, c: (b, 0, 0)),
+            pl.BlockSpec((1, 3, HEADS, keys), lambda b, c: (b, 0, 0, 0)),
+            pl.BlockSpec((1, BLOCK, width), lambda b, c: (b, 0, 0)),
+            pl.BlockSpec((1, BLOCK, width), lambda b, c: (b, 0, 0)),
+        ],
+        out_specs=[
+            pl.BlockSpec((1, BLOCK, width), lambda b, c: (b, 0, 0)),
+            pl.BlockSpec((1, BLOCK, width), lambda b, c: (b, 0, 0)),
+        ],
+    )
+    flops = blocks * (width // 128) * 2 * 4 * 2 * BLOCK * 128 * keys
+    cost = pl.CostEstimate(flops=flops, transcendentals=blocks * HEADS * BLOCK * keys,
+                           bytes_accessed=qg_tiles.size * 2 + st.size * 4 + 6 * blocks * BLOCK * width * 4)
+    return pl.pallas_call(
+        functools.partial(key_side_kernel, scale=scale),
+        grid_spec=grid_spec,
+        out_shape=[jax.ShapeDtypeStruct((blocks, BLOCK, width), jnp.float32)] * 2,
+        cost_estimate=cost,
+    )(tile_count, qg_tiles, st, k3, v3)
 
 
 def shards(query, key, value, out_grad, partner, tiles, tile_count):
@@ -100,21 +169,16 @@
     qg_tiles = qg_cluster.reshape(cluster_blocks, BLOCK, 2 * width)[tiles].reshape(
         blocks_dev, keys_tile, 2 * width
     )
-    q_tile = qg_tiles[..., :width].reshape(blocks_dev, keys_tile, HEADS, head_dim)
-    g_tile = qg_tiles[..., width:].reshape(blocks_dev, keys_tile, HEADS, head_dim)
     st = stats_cluster.reshape(cluster_blocks, 3, HEADS, BLOCK)[tiles]
     st = jnp.transpose(st, (0, 2, 3, 1, 4)).reshape(blocks_dev, 3, HEADS, keys_tile)
-    top_t, total_t, delta_t = st[:, 0], st[:, 1], st[:, 2]
-    k4 = key.reshape(heads4)
-    v4 = value.reshape(heads4)
-    s_key = jnp.einsum("bkhd,bqhd->bhkq", k4, q_tile, preferred_element_type=f32) * scale
-    d_key = jnp.einsum("bkhd,bqhd->bhkq", v4, g_tile, preferred_element_type=f32)
-    s_key = jnp.where(tile_live[:, None, None, :], s_key, NEG_BIG)
-    p_key = jnp.exp(s_key - top_t[:, :, None, :]) / total_t[:, :, None, :]
-    w_key = p_key.astype(bf16)
-    z_key = (p_key * (d_key - delta_t[:, :, None, :])).astype(bf16)
-    k_sum = jnp.einsum("bhkq,bqhd->bkhd", z_key, q_tile, preferred_element_type=f32) * scale
-    v_sum = jnp.einsum("bhkq,bqhd->bkhd", w_key, g_tile, preferred_element_type=f32)
+    k_sum, v_sum = key_side(
+        tile_count,
+        qg_tiles,
+        st,
+        key.reshape(blocks_dev, BLOCK, width),
+        value.reshape(blocks_dev, BLOCK, width),
+        scale,
+    )
 
     attended = out_full.reshape(nodes, width).astype(bf16)
     query_grad = q_grad.reshape(nodes, width).astype(bf16)

time: 213 us -> 194 us (0.911)
  local copies, waits for them, and re-layouts: 54.3 us -> 38.6 us
  matrix products: 29.8 us -> 16.3 us
  Pallas kernels: 0 us -> 8.13 us
  waiting for transfers between devices: 23.2 us -> 27.8 us
    dot_general x3 -> x0, matrix products: 13.5 us -> none  [the longest x1 6.53 us: shards(): jnp.einsum('bhkq,bqhd->bkhd', z_key, q_tile, preferred_element_type=f32)]
    reshape x6 -> x0, local copies, waits for them, and re-layouts: 9.55 us -> none  [the longest x2 4.68 us: shards(): v_sum.reshape(nodes, width) + returned[:, width:]]
    pallas_call x0 -> x1, Pallas kernels: none -> 8.13 us  [key_side(): pl.pallas_call(functools.partial(key_side_kernel, scale=scale), grid_spec...]
    slice x3 -> x0, local copies, waits for them, and re-layouts: 5.37 us -> none  [the longest x2 3.66 us: shards(): qg_tiles[..., width:].reshape(blocks_dev, keys_tile, HEADS, head_dim)]
    all_gather x1, waiting for transfers between devices: 23.1 us -> 27.7 us  [shards(): kv_cluster = lax.all_gather(both, 'blk', axis=0, tiled=True)]
    unnamed x45 -> x41, local copies, waits for them, and re-layouts: 11.1 us -> 8.41 us
  transfers between devices with their start and end apart: 10 -> 10, of which waited for: 1 -> 1; matrix products, arithmetic and copies ran while one was open for 30% -> 31% of each run, Pallas kernels for 0% -> 0%
where the time goes in v5:
time: 194 us; the launch traced here: 193 us
  starting transfers between devices  43.5 us (22%)
  local copies, waits for them, and re-layouts  38.6 us (20%)
  waiting for transfers between devices  27.8 us (14%)
  blocking collectives  27.4 us (14%)
  other arithmetic  17 us (9%)
  matrix products  16.3 us (8%)
  between operations  14.6 us (8%)
  Pallas kernels  8.13 us (4%)
    ppermute x8, starting transfers between devices, passed_along(): return lax.ppermute(x, axis, [(i, (i + by) % size) for i in range(size)])  43.4 us
    all_gather x1, waiting for transfers between devices, shards(): kv_cluster = lax.all_gather(both, 'blk', axis=0, tiled=True)  27.7 us
    all_gather x1, blocking collectives, shards(): stats_cluster = lax.all_gather(stats, 'blk', axis=0, tiled=True)  27.4 us
    unnamed x41, local copies, waits for them, and re-layouts  8.41 us
    pallas_call x1, Pallas kernels, key_side(): pl.pallas_call(functools.partial(key_side_kernel, scale=scale), grid_spec...  8.13 us
    dot_general x1, matrix products, shards(): jnp.einsum('bhqk,bkhd->bqhd', z_loc, k_tile, preferred_element_type=f32)  7.19 us
    gather x8, local copies, waits for them, and re-layouts, fetch_partners(): return jnp.concatenate([ahead[slots[:half]], behind[slots[half:]]], 0)  6.89 us
    dot_general x1, matrix products, shards(): jnp.einsum('bhqk,bkhd->bqhd', w_loc, v_tile, preferred_element_type=f32)  6.34 us
  transfers between devices with their start and end apart: 10, of which 1 were waited for; matrix products, arithmetic and copies ran while one was open for 31% of the time, Pallas kernels for 0%

profile of v5, /device:TPU:24, one launch (start us, length us, event | category | flops | bytes accessed | tf_op | source)
XLA Modules:
  0.0 193.3 jit_solution(15990854988170218408)
XLA Ops:
  7.3 1.0 constant_dynamic-update-slice_fusion.1
  8.3 1.0 constant_dynamic-update-slice_fusion
  9.3 0.8 copy-done.5
  10.1 1.9 fusion.57
  12.0 3.4 %collective-permute-start.3 = (bf16[128,1024]{1,0:T(8,128)(2,1)}, bf16[128,1024]{1,0:T(8,128)(2,1)S(1)}, u32[]{:S(2)}, u32[]{:S(2)}) collective-permute-start(bf16[128,1024]{1,0:T(8,128)(2,1)} %get-tuple-element.45), channel_id=1, source_target_pairs={{0,16},{8,24},{16,32},{24,40},{32,48},{40,56},{48,64},{56,72},{64,... | collective-permute-start | bytes 786440 | tf_op jit(solution)/shard_map/ppermute | solution.py:21
  15.4 1.9 collective-permute-start.1
  17.3 15.3 %collective-permute-start.2 = (bf16[128,1024]{1,0:T(8,128)(2,1)}, bf16[128,1024]{1,0:T(8,128)(2,1)S(1)}, u32[]{:S(2)}, u32[]{:S(2)}) collective-permute-start(bf16[128,1024]{1,0:T(8,128)(2,1)} %get-tuple-element.44), channel_id=1, source_target_pairs={{0,752},{8,760},{16,0},{24,8},{32,16},{40,24},{48,32},{56,40},{64,... | collective-permute-start | bytes 786440 | tf_op jit(solution)/shard_map/ppermute | solution.py:21
  32.6 3.4 %collective-permute-start = (bf16[128,1024]{1,0:T(8,128)(2,1)}, bf16[128,1024]{1,0:T(8,128)(2,1)S(1)}, u32[]{:S(2)}, u32[]{:S(2)}) collective-permute-start(bf16[128,1024]{1,0:T(8,128)(2,1)} %get-tuple-element.44), channel_id=1, source_target_pairs={{0,760},{8,0},{16,8},{24,16},{32,24},{40,32},{48,40},{56,48},{64,5... | collective-permute-start | bytes 786440 | tf_op jit(solution)/shard_map/ppermute | solution.py:21
  36.0 1.9 pad_maximum_fusion.1
  37.9 0.1 copy.74
  38.1 0.1 copy.64
  38.3 0.2 bitcast_convert_fusion
  38.8 1.2 fusion.58
  40.0 0.1 reshape.267
  40.1 1.2 copy.81
  41.3 0.9 gather_fusion.4
  42.2 0.9 gather_fusion.3
  43.1 0.9 gather_fusion.2
  44.0 0.9 gather_fusion.1
  44.9 0.9 pad_maximum_fusion
  45.8 0.2 copy.66
  46.0 0.1 reshape.251
  46.2 1.4 copy.72
  47.6 0.1 reshape.252
  47.7 0.6 multiply_reduce_fusion.3
  48.3 0.6 multiply_reduce_fusion.1
  48.9 27.7 %all-gather.3.cloned.1.call-done = bf16[2048,1024]{1,0:T(8,128)(2,1)} async-done(((bf16[256,1024]{1,0:T(8,128)(2,1)}), bf16[2048,1024]{1,0:T(8,128)(2,1)}) %all-gather.3.cloned.1.call-update) | async-done | bytes 4194320 | tf_op jit(solution)/shard_map/all_gather | solution.py:109
  76.6 2.9 %gather_fusion = bf16[12,128,1024]{2,1,0:T(8,128)(2,1)S(1)} fusion(bf16[16,128,1024]{2,1,0:T(8,128)(2,1)} %bitcast.157, s32[1024]{0:T(1024)S(1)} %pad_clamp_fusion.4), kind=kCustom, calls=%fused_computation | custom fusion | bytes 6291504 | tf_op jit(solution)/shard_map/gather | solution.py:119
  79.6 2.0 %fusion.56 = (bf16[2,768,512]{2,1,0:T(8,128)(2,1)}, bf16[2,768,512]{2,1,0:T(8,128)(2,1)}) fusion(bf16[2,768,1024]{2,1,0:T(8,128)(2,1)S(1)} %bitcast.152), kind=kLoop, calls=%fused_computation.109 | loop fusion | bytes 6291456 | tf_op jit(solution)/shard_map/slice | solution.py:122
  81.6 1.7 copy.63
  83.3 2.8 %bitcast_reduce_fusion = (f32[2,8,128]{2,1,0:T(8,128)S(1)}, f32[2,8,768,128]{3,2,1,0:T(8,128)S(1)}) fusion(pred[2,768]{1,0:T(4,128)(4,1)S(1)} %bitcast.168, bf16[2,768,8,64]{1,3,2,0:T(8,128)(2,1)S(1)} %bitcast.153, bf16[2,128,8,64]{1,0,3,2:T(2,128)(2,1)} %copy-done.6), kind=kOutput, calls=%fused_computation.14 | convolution fusion | flops 206043136 | bytes 8136192 | tf_op jit(solution)/shard_map/bqhd,bkhd->bhqk/dot_general | solution.py:130
  86.2 2.6 %copy-done = f32[2,8,768,128]{3,2,1,0:T(8,128)} copy-done((f32[2,8,768,128]{3,2,1,0:T(8,128)}, f32[2,8,768,128]{3,2,1,0:T(8,128)S(1)}, u32[]{:S(2)}) %copy-start) | copy-done | bytes 6291480
  88.8 1.4 fusion.3
  90.2 1.6 copy.62
  91.8 2.0 %multiply_reduce_fusion.2 = f32[2,128,8,64]{1,0,3,2:T(2,128)S(1)} fusion(f32[2,128,8,2]{1,0,2,3:T(2,128)S(1)} %bitcast_convert_fusion.3, bf16[2,2,128,8,64]{2,1,4,3,0:T(2,128)(2,1)} %copy-done.4), kind=kLoop, calls=%fused_computation.41 | loop fusion | flops 655360 | bytes 1064960
  93.9 6.3 %multiply_reduce_fusion.4 = (f32[2,128,8]{1,2,0:T(8,128)S(1)}, bf16[2,128,8,64]{1,3,2,0:T(8,128)(2,1)}) fusion(bf16[2,128,8,64]{1,0,3,2:T(2,128)(2,1)S(1)} %reshape.253, f32[2,128,8,64]{1,0,3,2:T(2,128)S(1)} %multiply_reduce_fusion.2, bf16[2,768,8,64]{1,3,2,0:T(8,128)(2,1)} %bitcast.158, f32[2,8,128]{2,1,0:T(8,128)S(1)} %copy_add_fusion, ...), kind=kOutput, calls=%fused_computation.58 | convolution fusion | flops 209844224 | bytes 8939008 | tf_op jit(solution)/shard_map/bhqk,bkhd->bqhd/dot_general | solution.py:141
  100.2 27.4 %all_gather.10 = f32[384,128]{1,0:T(8,128)} all-gather(f32[48,128]{1,0:T(8,128)S(1)} %bitcast.166), channel_id=1, replica_groups=mesh['grp'=96,'blk'=8] {'blk'}, dimensions={0}, use_global_device_ids=true | all-gather | bytes 221184 | tf_op jit(solution)/shard_map/all_gather | solution.py:146
  127.7 1.3 fusion.31
  129.0 1.4 reshape.255
  130.4 1.0 copy.82
  131.5 0.5 fusion.32
  131.9 0.3 reshape.256
  132.3 0.2 copy.83
  132.5 2.1 %fusion.39 = (bf16[128,1024]{1,0:T(8,128)(2,1)}, bf16[128,1024]{1,0:T(8,128)(2,1)}, bf16[128,1024]{1,0:T(8,128)(2,1)}, bf16[128,1024]{1,0:T(8,128)(2,1)}) fusion(bf16[2,256,512]{2,1,0:T(8,128)(2,1)} %copy.82, bf16[2,256,512]{2,1,0:T(8,128)(2,1)S(1)} %copy.83), kind=kLoop, calls=%fused_computation.62 | loop fusion | flops 2097152 | bytes 2097152 | tf_op jit(solution)/shard_map/slice | solution.py:26
  134.6 3.3 %collective-permute-start.7 = (bf16[128,1024]{1,0:T(8,128)(2,1)}, bf16[128,1024]{1,0:T(8,128)(2,1)S(1)}, u32[]{:S(2)}, u32[]{:S(2)}) collective-permute-start(bf16[128,1024]{1,0:T(8,128)(2,1)} %get-tuple-element.38), channel_id=1, source_target_pairs={{0,16},{8,24},{16,32},{24,40},{32,48},{40,56},{48,64},{56,72},{64,... | collective-permute-start | bytes 786440 | tf_op jit(solution)/shard_map/ppermute | solution.py:21
  137.9 7.3 %collective-permute-start.6 = (bf16[128,1024]{1,0:T(8,128)(2,1)}, bf16[128,1024]{1,0:T(8,128)(2,1)S(1)}, u32[]{:S(2)}, u32[]{:S(2)}) collective-permute-start(bf16[128,1024]{1,0:T(8,128)(2,1)} %get-tuple-element.39), channel_id=1, source_target_pairs={{0,752},{8,760},{16,0},{24,8},{32,16},{40,24},{48,32},{56,40},{64,... | collective-permute-start | bytes 786440 | tf_op jit(solution)/shard_map/ppermute | solution.py:21
  145.2 1.9 collective-permute-start.5
  147.1 7.0 %collective-permute-start.4 = (bf16[128,1024]{1,0:T(8,128)(2,1)}, bf16[128,1024]{1,0:T(8,128)(2,1)S(1)}, u32[]{:S(2)}, u32[]{:S(2)}) collective-permute-start(bf16[128,1024]{1,0:T(8,128)(2,1)} %get-tuple-element.36), channel_id=1, source_target_pairs={{0,760},{8,0},{16,8},{24,16},{32,24},{40,32},{48,40},{56,48},{64,5... | collective-permute-start | bytes 786440 | tf_op jit(solution)/shard_map/ppermute | solution.py:21
  154.1 1.6 multiply_reduce_fusion
  155.7 7.2 %fusion.26 = bf16[2,128,8,64]{1,3,2,0:T(8,128)(2,1)} fusion(bf16[2,768,8,64]{1,3,2,0:T(8,128)(2,1)S(1)} %bitcast.154, f32[2,8,128]{2,1,0:T(8,128)S(1)} %bitcast.174, bf16[2,768,8,64]{1,3,2,0:T(8,128)(2,1)} %bitcast.159, f32[2,8,768,128]{3,2,1,0:T(8,128)} %copy-done, f32[2,8,128]{2,1,0:T(8,128)S(1)} %copy_add_fusion, f32[2,8,128]{2,1,0:T(8,128)S(1)} %copy_maximum_fusion, ...), kind=kOutput, calls=%fused_computation.36 | convolution fusion | flops 414056448 | bytes 10511872 | tf_op jit(solution)/shard_map/bhqk,bkhd->bqhd/dot_general | solution.py:152
  162.9 0.3 copy.119
  163.2 1.0 reshape.369
  164.2 1.2 copy.120
  165.5 1.0 reshape.370
  166.5 0.6 gather_fusion.10
  167.1 0.7 copy.144
  167.7 0.9 gather_fusion.8
  168.6 0.9 gather_fusion.7
  169.5 0.9 gather_fusion.6
  170.3 0.9 gather_fusion.5
  171.3 0.2 convert_reduce_fusion
  171.5 4.7 %gather_fusion.9 = bf16[12,128,1024]{2,1,0:T(8,128)(2,1)} fusion(bf16[16,128,1024]{2,1,0:T(8,128)(2,1)} %bitcast.156, s32[1024]{0:T(1024)S(1)} %pad_clamp_fusion.4), kind=kCustom, calls=%fused_computation.9 | custom fusion | bytes 6291504 | tf_op jit(solution)/shard_map/gather | solution.py:169
  176.2 8.1 %shard_map.102 = (f32[2,128,512]{2,1,0:T(8,128)}, f32[2,128,512]{2,1,0:T(8,128)}) custom-call(s32[2]{0:T(128)} %count_ref.1, bf16[2,768,1024]{2,1,0:T(8,128)(2,1)} %bitcast.155, f32[2,3,8,768]{3,2,1,0:T(8,128)} %bitcast.164, bf16[2,128,512]{2,1,0:T(8,128)(2,1)} %bitcast.162, bf16[2,128,512]{2,1,0:T(8,128)(2,1)} %bitcast.163), custom_call_target="tpu_custom_call" | custom-call | flops 1610612736 | bytes 6438912 | tf_op jit(solution)/shard_map/pallas_call | solution.py:88
  184.3 2.1 %fusion.34 = (bf16[256,512]{1,0:T(8,128)(2,1)}, bf16[256,512]{1,0:T(8,128)(2,1)}) fusion(f32[2,128,512]{2,1,0:T(8,128)} %get-tuple-element.15, f32[256,1024]{1,0:T(8,128)S(1)} %convert_reduce_fusion, f32[2,128,512]{2,1,0:T(8,128)} %get-tuple-element.13), kind=kLoop, calls=%fused_computation.55 | loop fusion | flops 524288 | bytes 2621440 | tf_op jit(solution)/shard_map/convert_element_type | solution.py:186
  (71 shorter events, 0.9 us)
Async XLA Ops:
  7.2 30.7 %copy-start.9 = (bf16[256,512]{1,0:T(8,128)(2,1)S(1)}, bf16[256,512]{1,0:T(8,128)(2,1)}, u32[]{:S(2)}) copy-start(bf16[256,512]{1,0:T(8,128)(2,1)} %param.10) | copy-start | bytes 786436
  7.2 30.9 %copy-start.10 = (bf16[256,512]{1,0:T(8,128)(2,1)S(1)}, bf16[256,512]{1,0:T(8,128)(2,1)}, u32[]{:S(2)}) copy-start(bf16[256,512]{1,0:T(8,128)(2,1)} %param.7) | copy-start | bytes 786436
  7.2 31.3 %copy-start.15 = (s32[2]{0:T(128)S(1)}, s32[2]{0:T(128)}, u32[]{:S(2)}) copy-start(s32[2]{0:T(128)} %count_ref.1) | copy-start | bytes 28
  7.2 31.5 %copy-start.14 = (s32[2,6]{1,0:T(2,128)S(1)}, s32[2,6]{1,0:T(2,128)}, u32[]{:S(2)}) copy-start(s32[2,6]{1,0:T(2,128)} %param.12) | copy-start | bytes 148
  7.2 69.4 %all-gather.3.cloned.1.call-start = ((), (), s32[]{:S(2)}) async-start(), calls=%async_computation | async-start | bytes 4718592 | tf_op jit(solution)/shard_map/all_gather | solution.py:109
  9.3 0.8 copy-start.5
  9.3 30.7 %copy-start.13 = (s32[2,256]{1,0:T(2,128)S(1)}, s32[2,256]{1,0:T(2,128)}, u32[]{:S(2)}) copy-start(s32[2,256]{1,0:T(2,128)} %param.11) | copy-start | bytes 6148
  10.1 161.4 %all-gather.5.cloned.1.call-start = ((), (), s32[]{:S(2)}) async-start(), calls=%async_computation.1 | async-start | bytes 4718592 | tf_op jit(solution)/shard_map/all_gather | solution.py:110
  12.0 29.3 %collective-permute-start.3 = (bf16[128,1024]{1,0:T(8,128)(2,1)}, bf16[128,1024]{1,0:T(8,128)(2,1)S(1)}, u32[]{:S(2)}, u32[]{:S(2)}) collective-permute-start(bf16[128,1024]{1,0:T(8,128)(2,1)} %get-tuple-element.45), channel_id=1, source_target_pairs={{0,16},{8,24},{16,32},{24,40},{32,48},{40,56},{48,64},{56,72},{64,... | collective-permute-start | bytes 786440 | tf_op jit(solution)/shard_map/ppermute | solution.py:21
  15.4 27.7 %collective-permute-start.1 = (bf16[128,1024]{1,0:T(8,128)(2,1)}, bf16[128,1024]{1,0:T(8,128)(2,1)S(1)}, u32[]{:S(2)}, u32[]{:S(2)}) collective-permute-start(bf16[128,1024]{1,0:T(8,128)(2,1)} %get-tuple-element.45), channel_id=1, source_target_pairs={{0,8},{8,16},{16,24},{24,32},{32,40},{40,48},{48,56},{56,64},{64,7... | collective-permute-start | bytes 786440 | tf_op jit(solution)/shard_map/ppermute | solution.py:21
  17.3 24.9 %collective-permute-start.2 = (bf16[128,1024]{1,0:T(8,128)(2,1)}, bf16[128,1024]{1,0:T(8,128)(2,1)S(1)}, u32[]{:S(2)}, u32[]{:S(2)}) collective-permute-start(bf16[128,1024]{1,0:T(8,128)(2,1)} %get-tuple-element.44), channel_id=1, source_target_pairs={{0,752},{8,760},{16,0},{24,8},{32,16},{40,24},{48,32},{56,40},{64,... | collective-permute-start | bytes 786440 | tf_op jit(solution)/shard_map/ppermute | solution.py:21
  32.6 11.4 %collective-permute-start = (bf16[128,1024]{1,0:T(8,128)(2,1)}, bf16[128,1024]{1,0:T(8,128)(2,1)S(1)}, u32[]{:S(2)}, u32[]{:S(2)}) collective-permute-start(bf16[128,1024]{1,0:T(8,128)(2,1)} %get-tuple-element.44), channel_id=1, source_target_pairs={{0,760},{8,0},{16,8},{24,16},{32,24},{40,32},{48,40},{56,48},{64,5... | collective-permute-start | bytes 786440 | tf_op jit(solution)/shard_map/ppermute | solution.py:21
  38.8 5.2 %copy-start.6 = (bf16[2,128,8,64]{1,0,3,2:T(2,128)(2,1)}, bf16[2,128,8,64]{1,0,3,2:T(2,128)(2,1)S(1)}, u32[]{:S(2)}) copy-start(bf16[2,128,8,64]{1,0,3,2:T(2,128)(2,1)S(1)} %reshape.250) | copy-start | bytes 786436
  46.1 30.5 %copy-start.2 = (bf16[2,2,128,8,64]{2,1,4,3,0:T(2,128)(2,1)}, bf16[2,2,128,8,64]{2,1,4,3,0:T(2,128)(2,1)S(1)}, u32[]{:S(2)}) copy-start(bf16[2,2,128,8,64]{2,1,4,3,0:T(2,128)(2,1)S(1)} %reshape.251) | copy-start | bytes 1572868
  47.7 28.9 %copy-start.4 = (bf16[2,2,128,8,64]{2,1,4,3,0:T(2,128)(2,1)}, bf16[2,2,128,8,64]{2,1,4,3,0:T(2,128)(2,1)S(1)}, u32[]{:S(2)}) copy-start(bf16[2,2,128,8,64]{2,1,4,3,0:T(2,128)(2,1)S(1)} %reshape.252) | copy-start | bytes 1572868
  86.1 2.7 %copy-start = (f32[2,8,768,128]{3,2,1,0:T(8,128)}, f32[2,8,768,128]{3,2,1,0:T(8,128)S(1)}, u32[]{:S(2)}) copy-start(f32[2,8,768,128]{3,2,1,0:T(8,128)S(1)} %get-tuple-element.53) | copy-start | bytes 18874372
  86.1 4.1 %copy-start.1 = (bf16[2,768,512]{2,1,0:T(8,128)(2,1)S(1)}, bf16[2,768,512]{2,1,0:T(8,128)(2,1)}, u32[]{:S(2)}) copy-start(bf16[2,768,512]{2,1,0:T(8,128)(2,1)} %get-tuple-element.33) | copy-start | bytes 4718596
  93.9 33.8 %copy-start.7 = (f32[2,128,8,64]{1,0,3,2:T(2,128)S(1)}, f32[2,128,8,64]{1,0,3,2:T(2,128)}, u32[]{:S(2)}) copy-start(f32[2,128,8,64]{1,0,3,2:T(2,128)} %get-tuple-element.46) | copy-start | bytes 1572868
  93.9 37.6 %copy-start.8 = (f32[2,128,8,64]{1,0,3,2:T(2,128)S(1)}, f32[2,128,8,64]{1,0,3,2:T(2,128)}, u32[]{:S(2)}) copy-start(f32[2,128,8,64]{1,0,3,2:T(2,128)} %copy.81) | copy-start | bytes 1572868
  127.7 26.4 %copy-start.3 = (bf16[2,2,128,8,64]{2,1,4,3,0:T(2,128)(2,1)S(1)}, bf16[2,2,128,8,64]{2,1,4,3,0:T(2,128)(2,1)}, u32[]{:S(2)}) copy-start(bf16[2,2,128,8,64]{2,1,4,3,0:T(2,128)(2,1)} %copy-done.2) | copy-start | bytes 1572868
  134.6 33.1 %collective-permute-start.7 = (bf16[128,1024]{1,0:T(8,128)(2,1)}, bf16[128,1024]{1,0:T(8,128)(2,1)S(1)}, u32[]{:S(2)}, u32[]{:S(2)}) collective-permute-start(bf16[128,1024]{1,0:T(8,128)(2,1)} %get-tuple-element.38), channel_id=1, source_target_pairs={{0,16},{8,24},{16,32},{24,40},{32,48},{40,56},{48,64},{56,72},{64,... | collective-permute-start | bytes 786440 | tf_op jit(solution)/shard_map/ppermute | solution.py:21
  137.9 30.7 %collective-permute-start.6 = (bf16[128,1024]{1,0:T(8,128)(2,1)}, bf16[128,1024]{1,0:T(8,128)(2,1)S(1)}, u32[]{:S(2)}, u32[]{:S(2)}) collective-permute-start(bf16[128,1024]{1,0:T(8,128)(2,1)} %get-tuple-element.39), channel_id=1, source_target_pairs={{0,752},{8,760},{16,0},{24,8},{32,16},{40,24},{48,32},{56,40},{64,... | collective-permute-start | bytes 786440 | tf_op jit(solution)/shard_map/ppermute | solution.py:21
  145.2 24.3 %collective-permute-start.5 = (bf16[128,1024]{1,0:T(8,128)(2,1)}, bf16[128,1024]{1,0:T(8,128)(2,1)S(1)}, u32[]{:S(2)}, u32[]{:S(2)}) collective-permute-start(bf16[128,1024]{1,0:T(8,128)(2,1)} %get-tuple-element.37), channel_id=1, source_target_pairs={{0,8},{8,16},{16,24},{24,32},{32,40},{40,48},{48,56},{56,64},{64,7... | collective-permute-start | bytes 786440 | tf_op jit(solution)/shard_map/ppermute | solution.py:21
  147.1 23.2 %collective-permute-start.4 = (bf16[128,1024]{1,0:T(8,128)(2,1)}, bf16[128,1024]{1,0:T(8,128)(2,1)S(1)}, u32[]{:S(2)}, u32[]{:S(2)}) collective-permute-start(bf16[128,1024]{1,0:T(8,128)(2,1)} %get-tuple-element.36), channel_id=1, source_target_pairs={{0,760},{8,0},{16,8},{24,16},{32,24},{40,32},{48,40},{56,48},{64,5... | collective-permute-start | bytes 786440 | tf_op jit(solution)/shard_map/ppermute | solution.py:21
  155.7 7.2 %copy-start.12 = (bf16[2,128,8,64]{1,3,2,0:T(8,128)(2,1)S(1)}, bf16[2,128,8,64]{1,3,2,0:T(8,128)(2,1)}, u32[]{:S(2)}) copy-start(bf16[2,128,8,64]{1,3,2,0:T(8,128)(2,1)} %get-tuple-element.43) | copy-start | bytes 786436
  155.7 10.8 %copy-start.11 = (f32[384,128]{1,0:T(8,128)S(1)}, f32[384,128]{1,0:T(8,128)}, u32[]{:S(2)}) copy-start(f32[384,128]{1,0:T(8,128)} %all_gather.10) | copy-start | bytes 589828
Sparse Core Ops, SparseCore 0:
  10.4 66.1 all-gather.2
  79.0 60.7 all-gather.4

commit v6 on v5

--- a/solution.py
+++ b/solution.py
@@ -26,6 +26,114 @@
     ahead = passed_along(load[half:], "grp", -offset)
     behind = passed_along(load[:half], "grp", offset)
     return jnp.concatenate([ahead[slots[:half]], behind[slots[half:]]], 0)
+
+
+def query_side_kernel(count_ref, kv_ref, q_ref, g_ref, pair_ref, out_ref, qgrad_ref, term_ref, st_ref, *, scale):
+    b = pl.program_id(0)
+    width = q_ref.shape[-1]
+    keys = kv_ref.shape[1]
+    pair = 2 * (width // HEADS)
+    half = pair // 2
+    f32, bf16 = jnp.float32, jnp.bfloat16
+    live = (lax.broadcasted_iota(jnp.int32, (1, keys), 1) // BLOCK) < count_ref[b]
+    low = lax.broadcasted_iota(jnp.int32, (1, pair), 1) < half
+    lane = lax.broadcasted_iota(jnp.int32, (1, pair), 1)
+    nt = (((1,), (1,)), ((), ()))
+    stats = jnp.zeros((BLOCK, pair), f32)
+    for pr in range(width // pair):
+        cols = pl.ds(pr * pair, pair)
+        qp = q_ref[0, :, cols]
+        gp = g_ref[0, :, cols]
+        kp = kv_ref[0, :, cols]
+        vp = kv_ref[0, :, pl.ds(width + pr * pair, pair)]
+        kr = [pair_ref[r, 0, :, cols].astype(f32) for r in range(ROUNDS)]
+        vr = [pair_ref[r, 0, :, pl.ds(width + pr * pair, pair)].astype(f32) for r in range(ROUNDS)]
+        qf = qp.astype(f32)
+        gf = gp.astype(f32)
+        outs, grads = [], []
+        tk = [[] for _ in range(ROUNDS)]
+        tv = [[] for _ in range(ROUNDS)]
+        for side in range(2):
+            mine = low if side == 0 else jnp.logical_not(low)
+            h = 2 * pr + side
+            qh = jnp.where(mine, qp, jnp.zeros_like(qp))
+            gh = jnp.where(mine, gp, jnp.zeros_like(gp))
+            qhf = jnp.where(mine, qf, 0.0)
+            ghf = jnp.where(mine, gf, 0.0)
+            s_loc = lax.dot_general(qh, kp, nt, preferred_element_type=f32) * scale
+            s_loc = jnp.where(live, s_loc, NEG_BIG)
+            s_pair = [jnp.sum(qhf * kr[r], -1, keepdims=True) * scale for r in range(ROUNDS)]
+            top = jnp.max(s_loc, -1, keepdims=True)
+            for r in range(ROUNDS):
+                top = jnp.maximum(top, s_pair[r])
+            e_loc = jnp.exp(s_loc - top)
+            e_pair = [jnp.exp(s_pair[r] - top) for r in range(ROUNDS)]
+            total = jnp.sum(e_loc, -1, keepdims=True)
+            for r in range(ROUNDS):
+                total = total + e_pair[r]
+            p_loc = e_loc / total
+            p_pair = [e_pair[r] / total for r in range(ROUNDS)]
+            w_loc = p_loc.astype(bf16)
+            w_pair = [p_pair[r].astype(bf16).astype(f32) for r in range(ROUNDS)]
+            out = jnp.dot(w_loc, vp, preferred_element_type=f32)
+            for r in range(ROUNDS):
+                out = out + w_pair[r] * vr[r]
+            delta = jnp.sum(jnp.where(mine, gf * out, 0.0), -1, keepdims=True)
+            d_loc = lax.dot_general(gh, vp, nt, preferred_element_type=f32)
+            d_pair = [jnp.sum(ghf * vr[r], -1, keepdims=True) for r in range(ROUNDS)]
+            z_loc = (p_loc * (d_loc - delta)).astype(bf16)
+            z_pair = [(p_pair[r] * (d_pair[r] - delta)).astype(bf16).astype(f32) for r in range(ROUNDS)]
+            grad = jnp.dot(z_loc, kp, preferred_element_type=f32)
+            for r in range(ROUNDS):
+                grad = grad + z_pair[r] * kr[r]
+            outs.append(out)
+            grads.append(grad * scale)
+            for r in range(ROUNDS):
+                tk[r].append(z_pair[r] * qf * scale)
+                tv[r].append(w_pair[r] * gf)
+            for i, value in enumerate((top, total, delta)):
+                stats = jnp.where(lane == i * HEADS + h, value, stats)
+        out_ref[0, :, cols] = jnp.where(low, outs[0], outs[1])
+        qgrad_ref[0, :, cols] = jnp.where(low, grads[0], grads[1]).astype(bf16)
+        for r in range(ROUNDS):
+            term_ref[r, 0, :, cols] = jnp.where(low, tk[r][0], tk[r][1]).astype(bf16)
+            term_ref[r, 0, :, pl.ds(width + pr * pair, pair)] = jnp.where(low, tv[r][0], tv[r][1]).astype(bf16)
+    st_ref[0] = stats
+
+
+def query_side(tile_count, kv_tiles, q3, g3, pair_rows, scale):
+    blocks, keys, width2 = kv_tiles.shape
+    width = width2 // 2
+    grid_spec = pltpu.PrefetchScalarGridSpec(
+        num_scalar_prefetch=1,
+        grid=(blocks,),
+        in_specs=[
+            pl.BlockSpec((1, keys, width2), lambda b, c: (b, 0, 0)),
+            pl.BlockSpec((1, BLOCK, width), lambda b, c: (b, 0, 0)),
+            pl.BlockSpec((1, BLOCK, width), lambda b, c: (b, 0, 0)),
+            pl.BlockSpec((ROUNDS, 1, BLOCK, width2), lambda b, c: (0, b, 0, 0)),
+        ],
+        out_specs=[
+            pl.BlockSpec((1, BLOCK, width), lambda b, c: (b, 0, 0)),
+            pl.BlockSpec((1, BLOCK, width), lambda b, c: (b, 0, 0)),
+            pl.BlockSpec((ROUNDS, 1, BLOCK, width2), lambda b, c: (0, b, 0, 0)),
+            pl.BlockSpec((1, BLOCK, 2 * (width // HEADS)), lambda b, c: (b, 0, 0)),
+        ],
+    )
+    flops = blocks * (width // 128) * 2 * 4 * 2 * BLOCK * 128 * keys
+    cost = pl.CostEstimate(flops=flops, transcendentals=blocks * HEADS * BLOCK * keys,
+                           bytes_accessed=kv_tiles.size * 2 + pair_rows.size * 2 + 8 * blocks * BLOCK * width * 4)
+    return pl.pallas_call(
+        functools.partial(query_side_kernel, scale=scale),
+        grid_spec=grid_spec,
+        out_shape=[
+            jax.ShapeDtypeStruct((blocks, BLOCK, width), jnp.float32),
+            jax.ShapeDtypeStruct((blocks, BLOCK, width), jnp.bfloat16),
+            jax.ShapeDtypeStruct((ROUNDS, blocks, BLOCK, width2), jnp.bfloat16),
+            jax.ShapeDtypeStruct((blocks, BLOCK, 2 * (width // HEADS)), jnp.float32),
+        ],
+        cost_estimate=cost,
+    )(tile_count, kv_tiles, q3, g3, pair_rows)
 
 
 def key_side_kernel(count_ref, qg_ref, st_ref, k_ref, v_ref, ks_ref, vs_ref, *, scale):
@@ -103,7 +211,6 @@
     team = lax.axis_size("blk")
     cluster_blocks = blocks_dev * team
     keys_tile = TMAX * BLOCK
-    heads4 = (blocks_dev, BLOCK, HEADS, head_dim)
 
     both = jnp.concatenate([key, value], 1)
     kv_cluster = lax.all_gather(both, "blk", axis=0, tiled=True)
@@ -111,60 +218,31 @@
     partner_rows = jnp.stack(
         [fetch_partners(both, partner[step], step + 1) for step in range(ROUNDS)]
     )
-    live = jnp.arange(TMAX, dtype=jnp.int32)[None, :] < tile_count[:, None]
-    tile_live = jnp.broadcast_to(live[:, :, None], (blocks_dev, TMAX, BLOCK)).reshape(
-        blocks_dev, keys_tile
-    )
 
     kv_tiles = kv_cluster.reshape(cluster_blocks, BLOCK, 2 * width)[tiles].reshape(
         blocks_dev, keys_tile, 2 * width
     )
-    k_tile = kv_tiles[..., :width].reshape(blocks_dev, keys_tile, HEADS, head_dim)
-    v_tile = kv_tiles[..., width:].reshape(blocks_dev, keys_tile, HEADS, head_dim)
-    pair_shape = (ROUNDS,) + heads4
-    k_pair = partner_rows[..., :width].reshape(pair_shape)
-    v_pair = partner_rows[..., width:].reshape(pair_shape)
-    q4 = query.reshape(heads4)
-    g4 = out_grad.reshape(heads4)
-
-    s_loc = jnp.einsum("bqhd,bkhd->bhqk", q4, k_tile, preferred_element_type=f32) * scale
-    s_loc = jnp.where(tile_live[:, None, None, :], s_loc, NEG_BIG)
-    s_pair = jnp.einsum("bqhd,rbqhd->bhqr", q4, k_pair, preferred_element_type=f32) * scale
-    top = jnp.maximum(jnp.max(s_loc, -1), jnp.max(s_pair, -1))
-    e_loc = jnp.exp(s_loc - top[..., None])
-    e_pair = jnp.exp(s_pair - top[..., None])
-    total = jnp.sum(e_loc, -1) + jnp.sum(e_pair, -1)
-    p_loc = e_loc / total[..., None]
-    p_pair = e_pair / total[..., None]
-    w_loc = p_loc.astype(bf16)
-    w_pair = p_pair.astype(bf16)
-    out_full = jnp.einsum("bhqk,bkhd->bqhd", w_loc, v_tile, preferred_element_type=f32)
-    out_full = out_full + jnp.einsum("bhqr,rbqhd->bqhd", w_pair, v_pair, preferred_element_type=f32)
-    delta = jnp.transpose(jnp.sum(g4.astype(f32) * out_full, -1), (0, 2, 1))
-
-    stats = jnp.stack([top, total, delta], 1).reshape(blocks_dev * 3 * HEADS, BLOCK)
+    out_full, query_grad, terms, stats = query_side(
+        tile_count,
+        kv_tiles,
+        query.reshape(blocks_dev, BLOCK, width),
+        out_grad.reshape(blocks_dev, BLOCK, width),
+        partner_rows.reshape(ROUNDS, blocks_dev, BLOCK, 2 * width),
+        scale,
+    )
+
+    stats = stats[..., : 3 * HEADS].reshape(blocks_dev, BLOCK, 3, HEADS)
+    stats = jnp.transpose(stats, (0, 2, 3, 1)).reshape(blocks_dev * 3 * HEADS, BLOCK)
     stats_cluster = lax.all_gather(stats, "blk", axis=0, tiled=True)
-    stats_cluster, delta = lax.optimization_barrier((stats_cluster, delta))
-    d_loc = jnp.einsum("bqhd,bkhd->bhqk", g4, v_tile, preferred_element_type=f32)
-    d_pair = jnp.einsum("bqhd,rbqhd->bhqr", g4, v_pair, preferred_element_type=f32)
-    z_loc = (p_loc * (d_loc - delta[..., None])).astype(bf16)
-    z_pair = (p_pair * (d_pair - delta[..., None])).astype(bf16)
-    q_grad = jnp.einsum("bhqk,bkhd->bqhd", z_loc, k_tile, preferred_element_type=f32)
-    q_grad = (
-        q_grad + jnp.einsum("bhqr,rbqhd->bqhd", z_pair, k_pair, preferred_element_type=f32)
-    ) * scale
-    t_key = (
-        jnp.einsum("bhqr,bqhd->rbqhd", z_pair, q4, preferred_element_type=f32) * scale
-    ).astype(bf16)
-    t_val = jnp.einsum("bhqr,bqhd->rbqhd", w_pair, g4, preferred_element_type=f32).astype(bf16)
-    terms = jnp.concatenate(
-        [t_key.reshape(ROUNDS, nodes, width), t_val.reshape(ROUNDS, nodes, width)], 2
-    )
+
+    terms = terms.reshape(ROUNDS, nodes, 2 * width)
     returned = jnp.stack(
         [fetch_partners(terms[step], partner[step], step + 1) for step in range(ROUNDS)]
     )
     returned = jnp.sum(returned.astype(f32), 0)
-    returned, qg_cluster = lax.optimization_barrier((returned, qg_cluster))
+    returned, stats_cluster, qg_cluster = lax.optimization_barrier(
+        (returned, stats_cluster, qg_cluster)
+    )
 
     qg_tiles = qg_cluster.reshape(cluster_blocks, BLOCK, 2 * width)[tiles].reshape(
         blocks_dev, keys_tile, 2 * width
@@ -181,7 +259,7 @@
     )
 
     attended = out_full.reshape(nodes, width).astype(bf16)
-    query_grad = q_grad.reshape(nodes, width).astype(bf16)
+    query_grad = query_grad.reshape(nodes, width)
     key_grad = (k_sum.reshape(nodes, width) + returned[:, :width]).astype(bf16)
     value_grad = (v_sum.reshape(nodes, width) + returned[:, width:]).astype(bf16)
     return (attended, query_grad, key_grad, value_grad)

time: 194 us -> 173 us (0.89)
  matrix products: 16.3 us -> 0 us
  local copies, waits for them, and re-layouts: 38.6 us -> 23.8 us
  Pallas kernels: 8.13 us -> 22.9 us
  other arithmetic: 17 us -> 7.33 us
  waiting for transfers between devices: 27.8 us -> 34.7 us
  blocking collectives: 27.4 us -> 25.4 us
    dot_general x3 -> x0, matrix products: 16.3 us -> none  [the longest x1 7.19 us: shards(): jnp.einsum('bhqk,bkhd->bqhd', z_loc, k_tile, preferred_element_type=f32)]
    pallas_call x0 -> x1, Pallas kernels: none -> 14.7 us  [query_side(): pl.pallas_call(functools.partial(query_side_kernel, scale=scale), grid_sp...]
    unnamed x41 -> x7, local copies, waits for them, and re-layouts: 8.41 us -> 1.84 us
    slice x5 -> x1, local copies, waits for them, and re-layouts: 6.92 us -> 0.97 us  [shards(): stats = stats[..., :3 * HEADS].reshape(blocks_dev, BLOCK, 3, HEADS)]
    all_gather x1, waiting for transfers between devices: 27.7 us -> 32.4 us  [shards(): kv_cluster = lax.all_gather(both, 'blk', axis=0, tiled=True)]
    unnamed x5 -> x0, other arithmetic: 3.79 us -> none
    reshape x8 -> x0, local copies, waits for them, and re-layouts: 3.34 us -> none  [the longest x2 2.41 us: shards(): t_key.reshape(ROUNDS, nodes, width)]
    ppermute x8, waiting for transfers between devices: 0.02 us -> 2.24 us  [passed_along(): return lax.ppermute(x, axis, [(i, (i + by) % size) for i in range(size)])]
  transfers between devices with their start and end apart: 10 -> 10, of which waited for: 1 -> 3; matrix products, arithmetic and copies ran while one was open for 31% -> 12% of each run, Pallas kernels for 0% -> 9%
where the time goes in v6:
time: 173 us; the launch traced here: 172 us
  starting transfers between devices  43.6 us (25%)
  waiting for transfers between devices  34.7 us (20%)
  blocking collectives  25.4 us (15%)
  local copies, waits for them, and re-layouts  23.8 us (14%)
  Pallas kernels  22.9 us (13%)
  between operations  14.3 us (8%)
  other arithmetic  7.33 us (4%)
    ppermute x8, starting transfers between devices, passed_along(): return lax.ppermute(x, axis, [(i, (i + by) % size) for i in range(size)])  43.5 us
    all_gather x1, waiting for transfers between devices, shards(): kv_cluster = lax.all_gather(both, 'blk', axis=0, tiled=True)  32.4 us
    all_gather x1, blocking collectives, shards(): stats_cluster = lax.all_gather(stats, 'blk', axis=0, tiled=True)  25.4 us
    pallas_call x1, Pallas kernels, query_side(): pl.pallas_call(functools.partial(query_side_kernel, scale=scale), grid_sp...  14.7 us
    pallas_call x1, Pallas kernels, key_side(): pl.pallas_call(functools.partial(key_side_kernel, scale=scale), grid_spec...  8.14 us
    gather x8, local copies, waits for them, and re-layouts, fetch_partners(): return jnp.concatenate([ahead[slots[:half]], behind[slots[half:]]], 0)  6.89 us
    gather x1, local copies, waits for them, and re-layouts, shards(): kv_cluster.reshape(cluster_blocks, BLOCK, 2 * width)[tiles]  4.74 us
    gather x1, local copies, waits for them, and re-layouts, shards(): qg_cluster.reshape(cluster_blocks, BLOCK, 2 * width)[tiles]  4.73 us
  transfers between devices with their start and end apart: 10, of which 3 were waited for; matrix products, arithmetic and copies ran while one was open for 12% of the time, Pallas kernels for 9%

profile of v6, /device:TPU:24, one launch (start us, length us, event | category | flops | bytes accessed | tf_op | source)
XLA Modules:
  0.0 171.9 jit_solution(3139056897277205082)
XLA Ops:
  7.2 0.0 copy-start.2
  7.2 0.0 copy-start.1
  7.2 0.0 all-gather.3.cloned.1.call-start
  7.2 1.0 constant_dynamic-update-slice_fusion.1
  8.2 1.0 constant_dynamic-update-slice_fusion
  9.2 0.0 copy-start
  9.2 0.9 copy-done
  10.1 0.0 all-gather.3.cloned.1.call-update
  10.1 0.0 all-gather.5.cloned.1.call-start
  10.1 1.9 %pad_maximum_fusion.3 = bf16[256,1024]{1,0:T(8,128)(2,1)} fusion(bf16[256,512]{1,0:T(8,128)(2,1)} %param.10, bf16[256,512]{1,0:T(8,128)(2,1)} %param.7), kind=kLoop, calls=%fused_computation.17 | loop fusion | flops 1048576 | bytes 1048576 | tf_op jit(solution)/shard_map/concatenate | solution.py:217
  12.1 0.0 all-gather.5.cloned.1.call-update
  12.1 1.1 fusion.6
  13.2 3.4 %collective-permute-start.3 = (bf16[128,1024]{1,0:T(8,128)(2,1)S(1)}, bf16[128,1024]{1,0:T(8,128)(2,1)S(1)}, u32[]{:S(2)}, u32[]{:S(2)}) collective-permute-start(bf16[128,1024]{1,0:T(8,128)(2,1)S(1)} %get-tuple-element.29), channel_id=1, source_target_pairs={{0,16},{8,24},{16,32},{24,40},{32,48},{40,56},{48,64},{56,72},{64,... | collective-permute-start | bytes 786440 | tf_op jit(solution)/shard_map/ppermute | solution.py:21
  16.6 1.9 %collective-permute-start.1 = (bf16[128,1024]{1,0:T(8,128)(2,1)S(1)}, bf16[128,1024]{1,0:T(8,128)(2,1)S(1)}, u32[]{:S(2)}, u32[]{:S(2)}) collective-permute-start(bf16[128,1024]{1,0:T(8,128)(2,1)S(1)} %get-tuple-element.29), channel_id=1, source_target_pairs={{0,8},{8,16},{16,24},{24,32},{32,40},{40,48},{48,56},{56,64},{64,7... | collective-permute-start | bytes 786440 | tf_op jit(solution)/shard_map/ppermute | solution.py:21
  18.5 15.3 %collective-permute-start.2 = (bf16[128,1024]{1,0:T(8,128)(2,1)S(1)}, bf16[128,1024]{1,0:T(8,128)(2,1)S(1)}, u32[]{:S(2)}, u32[]{:S(2)}) collective-permute-start(bf16[128,1024]{1,0:T(8,128)(2,1)S(1)} %get-tuple-element.28), channel_id=1, source_target_pairs={{0,752},{8,760},{16,0},{24,8},{32,16},{40,24},{48,32},{56,40},{64,... | collective-permute-start | bytes 786440 | tf_op jit(solution)/shard_map/ppermute | solution.py:21
  33.8 3.4 %collective-permute-start = (bf16[128,1024]{1,0:T(8,128)(2,1)S(1)}, bf16[128,1024]{1,0:T(8,128)(2,1)S(1)}, u32[]{:S(2)}, u32[]{:S(2)}) collective-permute-start(bf16[128,1024]{1,0:T(8,128)(2,1)S(1)} %get-tuple-element.28), channel_id=1, source_target_pairs={{0,760},{8,0},{16,8},{24,16},{32,24},{40,32},{48,40},{56,48},{64,5... | collective-permute-start | bytes 786440 | tf_op jit(solution)/shard_map/ppermute | solution.py:21
  37.2 0.0 copy-done.2
  37.2 0.1 reshape.202
  37.3 0.0 copy-done.1
  37.3 0.0 collective-permute-done.3
  37.3 0.9 gather_fusion.4
  38.2 1.1 collective-permute-done.2
  39.4 0.9 gather_fusion.3
  40.2 0.0 collective-permute-done.1
  40.2 0.9 gather_fusion.2
  41.1 1.1 collective-permute-done
  42.2 0.9 gather_fusion.1
  43.1 1.1 pad_maximum_fusion.pair_ref
  44.2 32.4 %all-gather.3.cloned.1.call-done = bf16[2048,1024]{1,0:T(8,128)(2,1)} async-done(((bf16[256,1024]{1,0:T(8,128)(2,1)}), bf16[2048,1024]{1,0:T(8,128)(2,1)}) %all-gather.3.cloned.1.call-update) | async-done | bytes 4194320 | tf_op jit(solution)/shard_map/all_gather | solution.py:216
  76.6 4.7 %gather_fusion = bf16[12,128,1024]{2,1,0:T(8,128)(2,1)} fusion(bf16[16,128,1024]{2,1,0:T(8,128)(2,1)} %bitcast.64, s32[1024]{0:T(1024)S(1)} %pad_clamp_fusion.4), kind=kCustom, calls=%fused_computation | custom fusion | bytes 6291504 | tf_op jit(solution)/shard_map/gather | solution.py:222
  81.3 14.7 %shard_map.102 = (f32[2,128,512]{2,1,0:T(8,128)}, bf16[2,128,512]{2,1,0:T(8,128)(2,1)}, bf16[2,2,128,1024]{3,2,1,0:T(8,128)(2,1)}, f32[2,128,128]{2,1,0:T(8,128)}) custom-call(s32[2]{0:T(128)} %count_ref.3, bf16[2,768,1024]{2,1,0:T(8,128)(2,1)} %bitcast.62, bf16[2,128,512]{2,1,0:T(8,128)(2,1)} %bitcast.72, bf16[2,128,512]{2,1,0:T(8,128)(2,1)} %bitcast.73, ...), custom_call_target="tpu_custom_call" | custom-call | flops 1610612736 | bytes 8388608 | tf_op jit(solution)/shard_map/pallas_call | solution.py:126
  96.1 1.3 slice_bitcast_fusion.3
  97.3 3.4 %collective-permute-start.7 = (bf16[128,1024]{1,0:T(8,128)(2,1)S(1)}, bf16[128,1024]{1,0:T(8,128)(2,1)S(1)}, u32[]{:S(2)}, u32[]{:S(2)}) collective-permute-start(bf16[128,1024]{1,0:T(8,128)(2,1)S(1)} %get-tuple-element.25), channel_id=1, source_target_pairs={{0,16},{8,24},{16,32},{24,40},{32,48},{40,56},{48,64},{56,72},{64,... | collective-permute-start | bytes 786440 | tf_op jit(solution)/shard_map/ppermute | solution.py:21
  100.7 7.3 %collective-permute-start.6 = (bf16[128,1024]{1,0:T(8,128)(2,1)S(1)}, bf16[128,1024]{1,0:T(8,128)(2,1)S(1)}, u32[]{:S(2)}, u32[]{:S(2)}) collective-permute-start(bf16[128,1024]{1,0:T(8,128)(2,1)S(1)} %get-tuple-element.26), channel_id=1, source_target_pairs={{0,752},{8,760},{16,0},{24,8},{32,16},{40,24},{48,32},{56,40},{64,... | collective-permute-start | bytes 786440 | tf_op jit(solution)/shard_map/ppermute | solution.py:21
  108.0 1.9 %collective-permute-start.5 = (bf16[128,1024]{1,0:T(8,128)(2,1)S(1)}, bf16[128,1024]{1,0:T(8,128)(2,1)S(1)}, u32[]{:S(2)}, u32[]{:S(2)}) collective-permute-start(bf16[128,1024]{1,0:T(8,128)(2,1)S(1)} %get-tuple-element.27), channel_id=1, source_target_pairs={{0,8},{8,16},{16,24},{24,32},{32,40},{40,48},{48,56},{56,64},{64,7... | collective-permute-start | bytes 786440 | tf_op jit(solution)/shard_map/ppermute | solution.py:21
  109.9 7.0 %collective-permute-start.4 = (bf16[128,1024]{1,0:T(8,128)(2,1)S(1)}, bf16[128,1024]{1,0:T(8,128)(2,1)S(1)}, u32[]{:S(2)}, u32[]{:S(2)}) collective-permute-start(bf16[128,1024]{1,0:T(8,128)(2,1)S(1)} %get-tuple-element.24), channel_id=1, source_target_pairs={{0,760},{8,0},{16,8},{24,16},{32,24},{40,32},{48,40},{56,48},{64,5... | collective-permute-start | bytes 786440 | tf_op jit(solution)/shard_map/ppermute | solution.py:21
  116.9 1.8 %convert_element_type.15 = bf16[2,128,512]{2,1,0:T(8,128)(2,1)} convert(f32[2,128,512]{2,1,0:T(8,128)} %get-tuple-element.13) | non-fusion elementwise | flops 131072 | bytes 786432 | tf_op jit(solution)/shard_map/convert_element_type | solution.py:261
  118.6 1.0 copy.11
  119.6 25.4 %all_gather.10 = f32[384,128]{1,0:T(8,128)S(1)} all-gather(f32[48,128]{1,0:T(8,128)S(1)} %bitcast.76), channel_id=1, replica_groups=mesh['grp'=96,'blk'=8] {'blk'}, dimensions={0}, use_global_device_ids=true | all-gather | bytes 221184 | tf_op jit(solution)/shard_map/all_gather | solution.py:236
  145.0 0.0 collective-permute-done.7
  145.0 0.9 gather_fusion.8
  145.8 0.0 collective-permute-done.6
  145.9 0.9 gather_fusion.7
  146.7 0.0 collective-permute-done.5
  146.7 0.9 gather_fusion.6
  147.6 0.0 collective-permute-done.4
  147.6 0.9 gather_fusion.5
  148.5 0.2 convert_reduce_fusion
  148.8 0.0 all-gather.5.cloned.1.call-done
  148.8 4.7 %gather_fusion.9 = bf16[12,128,1024]{2,1,0:T(8,128)(2,1)} fusion(bf16[16,128,1024]{2,1,0:T(8,128)(2,1)} %bitcast.63, s32[1024]{0:T(1024)S(1)} %pad_clamp_fusion.4), kind=kCustom, calls=%fused_computation.9 | custom fusion | bytes 6291504 | tf_op jit(solution)/shard_map/gather | solution.py:247
  153.5 0.6 gather_fusion.10
  154.1 0.7 copy.14
  154.8 8.1 %shard_map.103 = (f32[2,128,512]{2,1,0:T(8,128)}, f32[2,128,512]{2,1,0:T(8,128)}) custom-call(s32[2]{0:T(128)} %count_ref.3, bf16[2,768,1024]{2,1,0:T(8,128)(2,1)} %bitcast.61, f32[2,3,8,768]{3,2,1,0:T(8,128)} %bitcast.74, bf16[2,128,512]{2,1,0:T(8,128)(2,1)} %bitcast.70, bf16[2,128,512]{2,1,0:T(8,128)(2,1)} %bitcast.71), custom_call_target="tpu_custom_call" | custom-call | flops 1610612736 | bytes 6438912 | tf_op jit(solution)/shard_map/pallas_call | solution.py:196
  162.9 2.1 %fusion = (bf16[256,512]{1,0:T(8,128)(2,1)}, bf16[256,512]{1,0:T(8,128)(2,1)}) fusion(f32[2,128,512]{2,1,0:T(8,128)} %get-tuple-element.21, f32[256,1024]{1,0:T(8,128)S(1)} %convert_reduce_fusion, f32[2,128,512]{2,1,0:T(8,128)} %get-tuple-element.19), kind=kLoop, calls=%fused_computation.19 | loop fusion | flops 524288 | bytes 2621440 | tf_op jit(solution)/shard_map/convert_element_type | solution.py:264
  (9 shorter events, 0.2 us)
Async XLA Ops:
  7.2 30.0 %copy-start.2 = (s32[2,6]{1,0:T(2,128)S(1)}, s32[2,6]{1,0:T(2,128)}, u32[]{:S(2)}) copy-start(s32[2,6]{1,0:T(2,128)} %param.12) | copy-start | bytes 148
  7.2 30.1 %copy-start.1 = (s32[2,256]{1,0:T(2,128)S(1)}, s32[2,256]{1,0:T(2,128)}, u32[]{:S(2)}) copy-start(s32[2,256]{1,0:T(2,128)} %param.11) | copy-start | bytes 6148
  7.2 69.4 %all-gather.3.cloned.1.call-start = ((), (), s32[]{:S(2)}) async-start(), calls=%async_computation | async-start | bytes 4718592 | tf_op jit(solution)/shard_map/all_gather | solution.py:216
  9.2 0.9 copy-start
  10.1 138.7 %all-gather.5.cloned.1.call-start = ((), (), s32[]{:S(2)}) async-start(), calls=%async_computation.1 | async-start | bytes 4718592 | tf_op jit(solution)/shard_map/all_gather | solution.py:217
  13.2 24.2 %collective-permute-start.3 = (bf16[128,1024]{1,0:T(8,128)(2,1)S(1)}, bf16[128,1024]{1,0:T(8,128)(2,1)S(1)}, u32[]{:S(2)}, u32[]{:S(2)}) collective-permute-start(bf16[128,1024]{1,0:T(8,128)(2,1)S(1)} %get-tuple-element.29), channel_id=1, source_target_pairs={{0,16},{8,24},{16,32},{24,40},{32,48},{40,56},{48,64},{56,72},{64,... | collective-permute-start | bytes 786440 | tf_op jit(solution)/shard_map/ppermute | solution.py:21
  16.6 23.6 %collective-permute-start.1 = (bf16[128,1024]{1,0:T(8,128)(2,1)S(1)}, bf16[128,1024]{1,0:T(8,128)(2,1)S(1)}, u32[]{:S(2)}, u32[]{:S(2)}) collective-permute-start(bf16[128,1024]{1,0:T(8,128)(2,1)S(1)} %get-tuple-element.29), channel_id=1, source_target_pairs={{0,8},{8,16},{16,24},{24,32},{32,40},{40,48},{48,56},{56,64},{64,7... | collective-permute-start | bytes 786440 | tf_op jit(solution)/shard_map/ppermute | solution.py:21
  18.5 20.9 %collective-permute-start.2 = (bf16[128,1024]{1,0:T(8,128)(2,1)S(1)}, bf16[128,1024]{1,0:T(8,128)(2,1)S(1)}, u32[]{:S(2)}, u32[]{:S(2)}) collective-permute-start(bf16[128,1024]{1,0:T(8,128)(2,1)S(1)} %get-tuple-element.28), channel_id=1, source_target_pairs={{0,752},{8,760},{16,0},{24,8},{32,16},{40,24},{48,32},{56,40},{64,... | collective-permute-start | bytes 786440 | tf_op jit(solution)/shard_map/ppermute | solution.py:21
  33.8 8.4 %collective-permute-start = (bf16[128,1024]{1,0:T(8,128)(2,1)S(1)}, bf16[128,1024]{1,0:T(8,128)(2,1)S(1)}, u32[]{:S(2)}, u32[]{:S(2)}) collective-permute-start(bf16[128,1024]{1,0:T(8,128)(2,1)S(1)} %get-tuple-element.28), channel_id=1, source_target_pairs={{0,760},{8,0},{16,8},{24,16},{32,24},{40,32},{48,40},{56,48},{64,5... | collective-permute-start | bytes 786440 | tf_op jit(solution)/shard_map/ppermute | solution.py:21
  97.3 47.7 %collective-permute-start.7 = (bf16[128,1024]{1,0:T(8,128)(2,1)S(1)}, bf16[128,1024]{1,0:T(8,128)(2,1)S(1)}, u32[]{:S(2)}, u32[]{:S(2)}) collective-permute-start(bf16[128,1024]{1,0:T(8,128)(2,1)S(1)} %get-tuple-element.25), channel_id=1, source_target_pairs={{0,16},{8,24},{16,32},{24,40},{32,48},{40,56},{48,64},{56,72},{64,... | collective-permute-start | bytes 786440 | tf_op jit(solution)/shard_map/ppermute | solution.py:21
  100.7 45.2 %collective-permute-start.6 = (bf16[128,1024]{1,0:T(8,128)(2,1)S(1)}, bf16[128,1024]{1,0:T(8,128)(2,1)S(1)}, u32[]{:S(2)}, u32[]{:S(2)}) collective-permute-start(bf16[128,1024]{1,0:T(8,128)(2,1)S(1)} %get-tuple-element.26), channel_id=1, source_target_pairs={{0,752},{8,760},{16,0},{24,8},{32,16},{40,24},{48,32},{56,40},{64,... | collective-permute-start | bytes 786440 | tf_op jit(solution)/shard_map/ppermute | solution.py:21
  108.0 38.8 %collective-permute-start.5 = (bf16[128,1024]{1,0:T(8,128)(2,1)S(1)}, bf16[128,1024]{1,0:T(8,128)(2,1)S(1)}, u32[]{:S(2)}, u32[]{:S(2)}) collective-permute-start(bf16[128,1024]{1,0:T(8,128)(2,1)S(1)} %get-tuple-element.27), channel_id=1, source_target_pairs={{0,8},{8,16},{16,24},{24,32},{32,40},{40,48},{48,56},{56,64},{64,7... | collective-permute-start | bytes 786440 | tf_op jit(solution)/shard_map/ppermute | solution.py:21
  109.9 37.7 %collective-permute-start.4 = (bf16[128,1024]{1,0:T(8,128)(2,1)S(1)}, bf16[128,1024]{1,0:T(8,128)(2,1)S(1)}, u32[]{:S(2)}, u32[]{:S(2)}) collective-permute-start(bf16[128,1024]{1,0:T(8,128)(2,1)S(1)} %get-tuple-element.24), channel_id=1, source_target_pairs={{0,760},{8,0},{16,8},{24,16},{32,24},{40,32},{48,40},{56,48},{64,5... | collective-permute-start | bytes 786440 | tf_op jit(solution)/shard_map/ppermute | solution.py:21
Sparse Core Ops, SparseCore 0:
  10.4 66.1 all-gather.2
  78.9 60.5 all-gather.4

commit v7 on v6

--- a/solution.py
+++ b/solution.py
@@ -28,10 +28,14 @@
     return jnp.concatenate([ahead[slots[:half]], behind[slots[half:]]], 0)
 
 
-def query_side_kernel(count_ref, kv_ref, q_ref, g_ref, pair_ref, out_ref, qgrad_ref, term_ref, st_ref, *, scale):
+def query_side_kernel(
+    count_ref, tiles_ref, kv_ref, q_ref, g_ref, pair_ref, out_ref, qgrad_ref, term_ref, st_ref, *, scale
+):
     b = pl.program_id(0)
     width = q_ref.shape[-1]
-    keys = kv_ref.shape[1]
+    slots = tiles_ref.shape[1]
+    keys = slots * BLOCK
+    ids = [tiles_ref[b, t] for t in range(slots)]
     pair = 2 * (width // HEADS)
     half = pair // 2
     f32, bf16 = jnp.float32, jnp.bfloat16
@@ -44,8 +48,8 @@
         cols = pl.ds(pr * pair, pair)
         qp = q_ref[0, :, cols]
         gp = g_ref[0, :, cols]
-        kp = kv_ref[0, :, cols]
-        vp = kv_ref[0, :, pl.ds(width + pr * pair, pair)]
+        kp = jnp.concatenate([kv_ref[i, :, cols] for i in ids], 0)
+        vp = jnp.concatenate([kv_ref[i, :, pl.ds(width + pr * pair, pair)] for i in ids], 0)
         kr = [pair_ref[r, 0, :, cols].astype(f32) for r in range(ROUNDS)]
         vr = [pair_ref[r, 0, :, pl.ds(width + pr * pair, pair)].astype(f32) for r in range(ROUNDS)]
         qf = qp.astype(f32)
@@ -101,28 +105,30 @@
     st_ref[0] = stats
 
 
-def query_side(tile_count, kv_tiles, q3, g3, pair_rows, scale):
-    blocks, keys, width2 = kv_tiles.shape
+def query_side(tile_count, tiles, kv_blocks, q3, g3, pair_rows, scale):
+    blocks, slots = tiles.shape
+    keys = slots * BLOCK
+    width2 = kv_blocks.shape[-1]
     width = width2 // 2
     grid_spec = pltpu.PrefetchScalarGridSpec(
-        num_scalar_prefetch=1,
+        num_scalar_prefetch=2,
         grid=(blocks,),
         in_specs=[
-            pl.BlockSpec((1, keys, width2), lambda b, c: (b, 0, 0)),
-            pl.BlockSpec((1, BLOCK, width), lambda b, c: (b, 0, 0)),
-            pl.BlockSpec((1, BLOCK, width), lambda b, c: (b, 0, 0)),
-            pl.BlockSpec((ROUNDS, 1, BLOCK, width2), lambda b, c: (0, b, 0, 0)),
+            pl.BlockSpec(memory_space=pltpu.VMEM),
+            pl.BlockSpec((1, BLOCK, width), lambda b, c, t: (b, 0, 0)),
+            pl.BlockSpec((1, BLOCK, width), lambda b, c, t: (b, 0, 0)),
+            pl.BlockSpec((ROUNDS, 1, BLOCK, width2), lambda b, c, t: (0, b, 0, 0)),
         ],
         out_specs=[
-            pl.BlockSpec((1, BLOCK, width), lambda b, c: (b, 0, 0)),
-            pl.BlockSpec((1, BLOCK, width), lambda b, c: (b, 0, 0)),
-            pl.BlockSpec((ROUNDS, 1, BLOCK, width2), lambda b, c: (0, b, 0, 0)),
-            pl.BlockSpec((1, BLOCK, 2 * (width // HEADS)), lambda b, c: (b, 0, 0)),
+            pl.BlockSpec((1, BLOCK, width), lambda b, c, t: (b, 0, 0)),
+            pl.BlockSpec((1, BLOCK, width), lambda b, c, t: (b, 0, 0)),
+            pl.BlockSpec((ROUNDS, 1, BLOCK, width2), lambda b, c, t: (0, b, 0, 0)),
+            pl.BlockSpec((1, BLOCK, 2 * (width // HEADS)), lambda b, c, t: (b, 0, 0)),
         ],
     )
     flops = blocks * (width // 128) * 2 * 4 * 2 * BLOCK * 128 * keys
     cost = pl.CostEstimate(flops=flops, transcendentals=blocks * HEADS * BLOCK * keys,
-                           bytes_accessed=kv_tiles.size * 2 + pair_rows.size * 2 + 8 * blocks * BLOCK * width * 4)
+                           bytes_accessed=kv_blocks.size * 2 + pair_rows.size * 2 + 8 * blocks * BLOCK * width * 4)
     return pl.pallas_call(
         functools.partial(query_side_kernel, scale=scale),
         grid_spec=grid_spec,
@@ -133,13 +139,15 @@
             jax.ShapeDtypeStruct((blocks, BLOCK, 2 * (width // HEADS)), jnp.float32),
         ],
         cost_estimate=cost,
-    )(tile_count, kv_tiles, q3, g3, pair_rows)
-
-
-def key_side_kernel(count_ref, qg_ref, st_ref, k_ref, v_ref, ks_ref, vs_ref, *, scale):
+    )(tile_count, tiles, kv_blocks, q3, g3, pair_rows)
+
+
+def key_side_kernel(count_ref, tiles_ref, qg_ref, st_ref, k_ref, v_ref, ks_ref, vs_ref, *, scale):
     b = pl.program_id(0)
     width = k_ref.shape[-1]
-    keys = qg_ref.shape[1]
+    slots = tiles_ref.shape[1]
+    keys = slots * BLOCK
+    ids = [tiles_ref[b, t] for t in range(slots)]
     pair = 2 * (width // HEADS)
     half = pair // 2
     live = (lax.broadcasted_iota(jnp.int32, (1, keys), 1) // BLOCK) < count_ref[b]
@@ -149,8 +157,8 @@
         cols = pl.ds(pr * pair, pair)
         kp = k_ref[0, :, cols]
         vp = v_ref[0, :, cols]
-        qp = qg_ref[0, :, cols]
-        gp = qg_ref[0, :, pl.ds(width + pr * pair, pair)]
+        qp = jnp.concatenate([qg_ref[i, :, cols] for i in ids], 0)
+        gp = jnp.concatenate([qg_ref[i, :, pl.ds(width + pr * pair, pair)] for i in ids], 0)
         zero = jnp.zeros_like(kp)
         k_out = []
         v_out = []
@@ -161,9 +169,9 @@
             vh = jnp.where(mine, vp, zero)
             s = lax.dot_general(kh, qp, nt, preferred_element_type=jnp.float32) * scale
             d = lax.dot_general(vh, gp, nt, preferred_element_type=jnp.float32)
-            top = st_ref[0, 0, pl.ds(h, 1), :]
-            total = st_ref[0, 1, pl.ds(h, 1), :]
-            delta = st_ref[0, 2, pl.ds(h, 1), :]
+            top, total, delta = [
+                jnp.concatenate([st_ref[i, j, pl.ds(h, 1), :] for i in ids], 1) for j in range(3)
+            ]
             p = jnp.where(live, jnp.exp(s - top) / total, 0.0)
             w = p.astype(jnp.bfloat16)
             z = (p * (d - delta)).astype(jnp.bfloat16)
@@ -173,32 +181,33 @@
         vs_ref[0, :, cols] = jnp.where(low, v_out[0], v_out[1])
 
 
-def key_side(tile_count, qg_tiles, st, k3, v3, scale):
-    blocks, keys, width2 = qg_tiles.shape
-    width = width2 // 2
+def key_side(tile_count, tiles, qg_blocks, st, k3, v3, scale):
+    blocks, slots = tiles.shape
+    keys = slots * BLOCK
+    width = k3.shape[-1]
     grid_spec = pltpu.PrefetchScalarGridSpec(
-        num_scalar_prefetch=1,
+        num_scalar_prefetch=2,
         grid=(blocks,),
         in_specs=[
-            pl.BlockSpec((1, keys, width2), lambda b, c: (b, 0, 0)),
-            pl.BlockSpec((1, 3, HEADS, keys), lambda b, c: (b, 0, 0, 0)),
-            pl.BlockSpec((1, BLOCK, width), lambda b, c: (b, 0, 0)),
-            pl.BlockSpec((1, BLOCK, width), lambda b, c: (b, 0, 0)),
+            pl.BlockSpec(memory_space=pltpu.VMEM),
+            pl.BlockSpec(memory_space=pltpu.VMEM),
+            pl.BlockSpec((1, BLOCK, width), lambda b, c, t: (b, 0, 0)),
+            pl.BlockSpec((1, BLOCK, width), lambda b, c, t: (b, 0, 0)),
         ],
         out_specs=[
-            pl.BlockSpec((1, BLOCK, width), lambda b, c: (b, 0, 0)),
-            pl.BlockSpec((1, BLOCK, width), lambda b, c: (b, 0, 0)),
+            pl.BlockSpec((1, BLOCK, width), lambda b, c, t: (b, 0, 0)),
+            pl.BlockSpec((1, BLOCK, width), lambda b, c, t: (b, 0, 0)),
         ],
     )
     flops = blocks * (width // 128) * 2 * 4 * 2 * BLOCK * 128 * keys
     cost = pl.CostEstimate(flops=flops, transcendentals=blocks * HEADS * BLOCK * keys,
-                           bytes_accessed=qg_tiles.size * 2 + st.size * 4 + 6 * blocks * BLOCK * width * 4)
+                           bytes_accessed=qg_blocks.size * 2 + st.size * 4 + 6 * blocks * BLOCK * width * 4)
     return pl.pallas_call(
         functools.partial(key_side_kernel, scale=scale),
         grid_spec=grid_spec,
         out_shape=[jax.ShapeDtypeStruct((blocks, BLOCK, width), jnp.float32)] * 2,
         cost_estimate=cost,
-    )(tile_count, qg_tiles, st, k3, v3)
+    )(tile_count, tiles, qg_blocks, st, k3, v3)
 
 
 def shards(query, key, value, out_grad, partner, tiles, tile_count):
@@ -210,7 +219,6 @@
     blocks_dev = nodes // BLOCK
     team = lax.axis_size("blk")
     cluster_blocks = blocks_dev * team
-    keys_tile = TMAX * BLOCK
 
     both = jnp.concatenate([key, value], 1)
     kv_cluster = lax.all_gather(both, "blk", axis=0, tiled=True)
@@ -219,12 +227,10 @@
         [fetch_partners(both, partner[step], step + 1) for step in range(ROUNDS)]
     )
 
-    kv_tiles = kv_cluster.reshape(cluster_blocks, BLOCK, 2 * width)[tiles].reshape(
-        blocks_dev, keys_tile, 2 * width
-    )
     out_full, query_grad, terms, stats = query_side(
         tile_count,
-        kv_tiles,
+        tiles,
+        kv_cluster.reshape(cluster_blocks, BLOCK, 2 * width),
         query.reshape(blocks_dev, BLOCK, width),
         out_grad.reshape(blocks_dev, BLOCK, width),
         partner_rows.reshape(ROUNDS, blocks_dev, BLOCK, 2 * width),
@@ -244,15 +250,11 @@
         (returned, stats_cluster, qg_cluster)
     )
 
-    qg_tiles = qg_cluster.reshape(cluster_blocks, BLOCK, 2 * width)[tiles].reshape(
-        blocks_dev, keys_tile, 2 * width
-    )
-    st = stats_cluster.reshape(cluster_blocks, 3, HEADS, BLOCK)[tiles]
-    st = jnp.transpose(st, (0, 2, 3, 1, 4)).reshape(blocks_dev, 3, HEADS, keys_tile)
     k_sum, v_sum = key_side(
         tile_count,
-        qg_tiles,
-        st,
+        tiles,
+        qg_cluster.reshape(cluster_blocks, BLOCK, 2 * width),
+        stats_cluster.reshape(cluster_blocks, 3, HEADS, BLOCK),
         key.reshape(blocks_dev, BLOCK, width),
         value.reshape(blocks_dev, BLOCK, width),
         scale,

time: 173 us -> 165 us (0.954)
  local copies, waits for them, and re-layouts: 23.8 us -> 12.9 us
  blocking collectives: 25.4 us -> 27.2 us
    gather x3 -> x0, local copies, waits for them, and re-layouts: 10 us -> none  [the longest x1 4.74 us: shards(): kv_cluster.reshape(cluster_blocks, BLOCK, 2 * width)[tiles]]
    all_gather x1, blocking collectives: 25.4 us -> 27.2 us  [shards(): stats_cluster = lax.all_gather(stats, 'blk', axis=0, tiled=True)]
  transfers between devices with their start and end apart: 10 -> 10, of which waited for: 3 -> 3; matrix products, arithmetic and copies ran while one was open for 12% -> 9% of each run, Pallas kernels for 9% -> 9%
where the time goes in v7:
time: 165 us
  starting transfers between devices  43.6 us (26%)
  waiting for transfers between devices  34.8 us (21%)
  blocking collectives  27.2 us (16%)
  Pallas kernels  24.6 us (15%)
  between operations  14.2 us (9%)
  local copies, waits for them, and re-layouts  12.9 us (8%)
  other arithmetic  7.34 us (4%)
    ppermute x8, starting transfers between devices, passed_along(): return lax.ppermute(x, axis, [(i, (i + by) % size) for i in range(size)])  43.5 us
    all_gather x1, waiting for transfers between devices, shards(): kv_cluster = lax.all_gather(both, 'blk', axis=0, tiled=True)  32.4 us
    all_gather x1, blocking collectives, shards(): stats_cluster = lax.all_gather(stats, 'blk', axis=0, tiled=True)  27.2 us
    pallas_call x1, Pallas kernels, query_side(): pl.pallas_call(functools.partial(query_side_kernel, scale=scale), grid_sp...  15.6 us
    pallas_call x1, Pallas kernels, key_side(): pl.pallas_call(functools.partial(key_side_kernel, scale=scale), grid_spec...  9.04 us
    gather x8, local copies, waits for them, and re-layouts, fetch_partners(): return jnp.concatenate([ahead[slots[:half]], behind[slots[half:]]], 0)  6.89 us
  transfers between devices with their start and end apart: 10, of which 3 were waited for; matrix products, arithmetic and copies ran while one was open for 9% of the time, Pallas kernels for 9%

profile of v7, /device:TPU:24, one launch (start us, length us, event | category | flops | bytes accessed | tf_op | source)
XLA Modules:
  0.0 164.8 jit_solution(8542761012935246148)
XLA Ops:
  7.2 0.0 copy-start.1
  7.2 0.0 all-gather.3.cloned.1.call-start
  7.2 1.0 constant_dynamic-update-slice_fusion.1
  8.2 1.0 constant_dynamic-update-slice_fusion
  9.2 0.0 copy-start
  9.2 0.8 copy-done
  10.0 0.0 all-gather.3.cloned.1.call-update
  10.0 0.0 all-gather.5.cloned.1.call-start
  10.1 1.9 %pad_maximum_fusion.3 = bf16[256,1024]{1,0:T(8,128)(2,1)} fusion(bf16[256,512]{1,0:T(8,128)(2,1)} %param.10, bf16[256,512]{1,0:T(8,128)(2,1)} %param.7), kind=kLoop, calls=%fused_computation.14 | loop fusion | flops 1048576 | bytes 1048576 | tf_op jit(solution)/shard_map/concatenate | solution.py:225
  11.9 0.0 all-gather.5.cloned.1.call-update
  12.0 1.1 fusion.6
  13.0 3.4 %collective-permute-start.3 = (bf16[128,1024]{1,0:T(8,128)(2,1)S(1)}, bf16[128,1024]{1,0:T(8,128)(2,1)S(1)}, u32[]{:S(2)}, u32[]{:S(2)}) collective-permute-start(bf16[128,1024]{1,0:T(8,128)(2,1)S(1)} %get-tuple-element.29), channel_id=1, source_target_pairs={{0,16},{8,24},{16,32},{24,40},{32,48},{40,56},{48,64},{56,72},{64,... | collective-permute-start | bytes 786440 | tf_op jit(solution)/shard_map/ppermute | solution.py:21
  16.4 1.9 %collective-permute-start.1 = (bf16[128,1024]{1,0:T(8,128)(2,1)S(1)}, bf16[128,1024]{1,0:T(8,128)(2,1)S(1)}, u32[]{:S(2)}, u32[]{:S(2)}) collective-permute-start(bf16[128,1024]{1,0:T(8,128)(2,1)S(1)} %get-tuple-element.29), channel_id=1, source_target_pairs={{0,8},{8,16},{16,24},{24,32},{32,40},{40,48},{48,56},{56,64},{64,7... | collective-permute-start | bytes 786440 | tf_op jit(solution)/shard_map/ppermute | solution.py:21
  18.4 15.3 %collective-permute-start.2 = (bf16[128,1024]{1,0:T(8,128)(2,1)S(1)}, bf16[128,1024]{1,0:T(8,128)(2,1)S(1)}, u32[]{:S(2)}, u32[]{:S(2)}) collective-permute-start(bf16[128,1024]{1,0:T(8,128)(2,1)S(1)} %get-tuple-element.28), channel_id=1, source_target_pairs={{0,752},{8,760},{16,0},{24,8},{32,16},{40,24},{48,32},{56,40},{64,... | collective-permute-start | bytes 786440 | tf_op jit(solution)/shard_map/ppermute | solution.py:21
  33.7 3.4 %collective-permute-start = (bf16[128,1024]{1,0:T(8,128)(2,1)S(1)}, bf16[128,1024]{1,0:T(8,128)(2,1)S(1)}, u32[]{:S(2)}, u32[]{:S(2)}) collective-permute-start(bf16[128,1024]{1,0:T(8,128)(2,1)S(1)} %get-tuple-element.28), channel_id=1, source_target_pairs={{0,760},{8,0},{16,8},{24,16},{32,24},{40,32},{48,40},{56,48},{64,5... | collective-permute-start | bytes 786440 | tf_op jit(solution)/shard_map/ppermute | solution.py:21
  37.0 0.0 copy-done.1
  37.1 0.0 collective-permute-done.3
  37.1 0.9 gather_fusion.3
  38.0 1.2 collective-permute-done.2
  39.2 0.9 gather_fusion.2
  40.1 0.0 collective-permute-done.1
  40.1 0.9 gather_fusion.1
  41.0 1.1 collective-permute-done
  42.0 0.9 gather_fusion
  43.0 1.2 pad_maximum_fusion.pair_ref
  44.1 32.4 %all-gather.3.cloned.1.call-done = bf16[2048,1024]{1,0:T(8,128)(2,1)} async-done(((bf16[256,1024]{1,0:T(8,128)(2,1)}), bf16[2048,1024]{1,0:T(8,128)(2,1)}) %all-gather.3.cloned.1.call-update) | async-done | bytes 4194320 | tf_op jit(solution)/shard_map/all_gather | solution.py:224
  76.6 15.6 %shard_map.102 = (f32[2,128,512]{2,1,0:T(8,128)}, bf16[2,128,512]{2,1,0:T(8,128)(2,1)}, bf16[2,2,128,1024]{3,2,1,0:T(8,128)(2,1)}, f32[2,128,128]{2,1,0:T(8,128)}) custom-call(s32[2]{0:T(128)} %count_ref.3, s32[2,6]{1,0:T(2,128)} %tiles_ref.3, bf16[16,128,1024]{2,1,0:T(8,128)(2,1)} %bitcast.64, bf16[2,128,512]{2,1,0:T(8,128)(2,1)} %bitcast.58, ...), custom_call_target="tpu_custom_call" | custom-call | flops 1610612736 | bytes 9437184 | tf_op jit(solution)/shard_map/pallas_call | solution.py:132
  92.1 1.3 slice_bitcast_fusion.3
  93.4 3.4 %collective-permute-start.7 = (bf16[128,1024]{1,0:T(8,128)(2,1)S(1)}, bf16[128,1024]{1,0:T(8,128)(2,1)S(1)}, u32[]{:S(2)}, u32[]{:S(2)}) collective-permute-start(bf16[128,1024]{1,0:T(8,128)(2,1)S(1)} %get-tuple-element.25), channel_id=1, source_target_pairs={{0,16},{8,24},{16,32},{24,40},{32,48},{40,56},{48,64},{56,72},{64,... | collective-permute-start | bytes 786440 | tf_op jit(solution)/shard_map/ppermute | solution.py:21
  96.8 7.3 %collective-permute-start.6 = (bf16[128,1024]{1,0:T(8,128)(2,1)S(1)}, bf16[128,1024]{1,0:T(8,128)(2,1)S(1)}, u32[]{:S(2)}, u32[]{:S(2)}) collective-permute-start(bf16[128,1024]{1,0:T(8,128)(2,1)S(1)} %get-tuple-element.26), channel_id=1, source_target_pairs={{0,752},{8,760},{16,0},{24,8},{32,16},{40,24},{48,32},{56,40},{64,... | collective-permute-start | bytes 786440 | tf_op jit(solution)/shard_map/ppermute | solution.py:21
  104.0 1.9 %collective-permute-start.5 = (bf16[128,1024]{1,0:T(8,128)(2,1)S(1)}, bf16[128,1024]{1,0:T(8,128)(2,1)S(1)}, u32[]{:S(2)}, u32[]{:S(2)}) collective-permute-start(bf16[128,1024]{1,0:T(8,128)(2,1)S(1)} %get-tuple-element.27), channel_id=1, source_target_pairs={{0,8},{8,16},{16,24},{24,32},{32,40},{40,48},{48,56},{56,64},{64,7... | collective-permute-start | bytes 786440 | tf_op jit(solution)/shard_map/ppermute | solution.py:21
  106.0 7.0 %collective-permute-start.4 = (bf16[128,1024]{1,0:T(8,128)(2,1)S(1)}, bf16[128,1024]{1,0:T(8,128)(2,1)S(1)}, u32[]{:S(2)}, u32[]{:S(2)}) collective-permute-start(bf16[128,1024]{1,0:T(8,128)(2,1)S(1)} %get-tuple-element.24), channel_id=1, source_target_pairs={{0,760},{8,0},{16,8},{24,16},{32,24},{40,32},{48,40},{56,48},{64,5... | collective-permute-start | bytes 786440 | tf_op jit(solution)/shard_map/ppermute | solution.py:21
  112.9 1.8 %convert_element_type.15 = bf16[2,128,512]{2,1,0:T(8,128)(2,1)} convert(f32[2,128,512]{2,1,0:T(8,128)} %get-tuple-element.13) | non-fusion elementwise | flops 131072 | bytes 786432 | tf_op jit(solution)/shard_map/convert_element_type | solution.py:263
  114.7 1.0 copy.12
  115.7 27.2 %all_gather.10 = f32[384,128]{1,0:T(8,128)} all-gather(f32[48,128]{1,0:T(8,128)S(1)} %bitcast.62), channel_id=1, replica_groups=mesh['grp'=96,'blk'=8] {'blk'}, dimensions={0}, use_global_device_ids=true | all-gather | bytes 221184 | tf_op jit(solution)/shard_map/all_gather | solution.py:242
  142.9 0.0 collective-permute-done.7
  142.9 0.9 gather_fusion.7
  143.8 0.0 collective-permute-done.6
  143.8 0.9 gather_fusion.6
  144.7 0.0 collective-permute-done.5
  144.7 0.9 gather_fusion.5
  145.5 0.0 collective-permute-done.4
  145.6 0.9 gather_fusion.4
  146.5 0.2 convert_reduce_fusion
  146.7 0.0 all-gather.5.cloned.1.call-done
  146.7 9.0 %shard_map.103 = (f32[2,128,512]{2,1,0:T(8,128)}, f32[2,128,512]{2,1,0:T(8,128)}) custom-call(s32[2]{0:T(128)} %count_ref.3, s32[2,6]{1,0:T(2,128)} %tiles_ref.3, bf16[16,128,1024]{2,1,0:T(8,128)(2,1)} %bitcast.63, f32[16,3,8,128]{3,2,1,0:T(8,128)} %bitcast.60, bf16[2,128,512]{2,1,0:T(8,128)(2,1)} %bitcast.56, bf16[2,128,512]{2,1,0:T(8,128)(2,1)} %bitcast.57), custom_call_target="tpu_custom_call" | custom-call | flops 1610612736 | bytes 7536640 | tf_op jit(solution)/shard_map/pallas_call | solution.py:205
  155.8 2.1 %fusion = (bf16[256,512]{1,0:T(8,128)(2,1)}, bf16[256,512]{1,0:T(8,128)(2,1)}) fusion(f32[2,128,512]{2,1,0:T(8,128)} %get-tuple-element.21, f32[256,1024]{1,0:T(8,128)S(1)} %convert_reduce_fusion, f32[2,128,512]{2,1,0:T(8,128)} %get-tuple-element.19), kind=kLoop, calls=%fused_computation.16 | loop fusion | flops 524288 | bytes 2621440 | tf_op jit(solution)/shard_map/convert_element_type | solution.py:266
  (7 shorter events, 0.2 us)
Async XLA Ops:
  7.2 29.9 %copy-start.1 = (s32[2,256]{1,0:T(2,128)S(1)}, s32[2,256]{1,0:T(2,128)}, u32[]{:S(2)}) copy-start(s32[2,256]{1,0:T(2,128)} %param.11) | copy-start | bytes 6148
  7.2 69.4 %all-gather.3.cloned.1.call-start = ((), (), s32[]{:S(2)}) async-start(), calls=%async_computation | async-start | bytes 4718592 | tf_op jit(solution)/shard_map/all_gather | solution.py:224
  9.2 0.8 copy-start
  10.0 136.7 %all-gather.5.cloned.1.call-start = ((), (), s32[]{:S(2)}) async-start(), calls=%async_computation.1 | async-start | bytes 4718592 | tf_op jit(solution)/shard_map/all_gather | solution.py:225
  13.0 24.1 %collective-permute-start.3 = (bf16[128,1024]{1,0:T(8,128)(2,1)S(1)}, bf16[128,1024]{1,0:T(8,128)(2,1)S(1)}, u32[]{:S(2)}, u32[]{:S(2)}) collective-permute-start(bf16[128,1024]{1,0:T(8,128)(2,1)S(1)} %get-tuple-element.29), channel_id=1, source_target_pairs={{0,16},{8,24},{16,32},{24,40},{32,48},{40,56},{48,64},{56,72},{64,... | collective-permute-start | bytes 786440 | tf_op jit(solution)/shard_map/ppermute | solution.py:21
  16.4 23.6 %collective-permute-start.1 = (bf16[128,1024]{1,0:T(8,128)(2,1)S(1)}, bf16[128,1024]{1,0:T(8,128)(2,1)S(1)}, u32[]{:S(2)}, u32[]{:S(2)}) collective-permute-start(bf16[128,1024]{1,0:T(8,128)(2,1)S(1)} %get-tuple-element.29), channel_id=1, source_target_pairs={{0,8},{8,16},{16,24},{24,32},{32,40},{40,48},{48,56},{56,64},{64,7... | collective-permute-start | bytes 786440 | tf_op jit(solution)/shard_map/ppermute | solution.py:21
  18.4 20.9 %collective-permute-start.2 = (bf16[128,1024]{1,0:T(8,128)(2,1)S(1)}, bf16[128,1024]{1,0:T(8,128)(2,1)S(1)}, u32[]{:S(2)}, u32[]{:S(2)}) collective-permute-start(bf16[128,1024]{1,0:T(8,128)(2,1)S(1)} %get-tuple-element.28), channel_id=1, source_target_pairs={{0,752},{8,760},{16,0},{24,8},{32,16},{40,24},{48,32},{56,40},{64,... | collective-permute-start | bytes 786440 | tf_op jit(solution)/shard_map/ppermute | solution.py:21
  33.7 8.4 %collective-permute-start = (bf16[128,1024]{1,0:T(8,128)(2,1)S(1)}, bf16[128,1024]{1,0:T(8,128)(2,1)S(1)}, u32[]{:S(2)}, u32[]{:S(2)}) collective-permute-start(bf16[128,1024]{1,0:T(8,128)(2,1)S(1)} %get-tuple-element.28), channel_id=1, source_target_pairs={{0,760},{8,0},{16,8},{24,16},{32,24},{40,32},{48,40},{56,48},{64,5... | collective-permute-start | bytes 786440 | tf_op jit(solution)/shard_map/ppermute | solution.py:21
  93.4 49.6 %collective-permute-start.7 = (bf16[128,1024]{1,0:T(8,128)(2,1)S(1)}, bf16[128,1024]{1,0:T(8,128)(2,1)S(1)}, u32[]{:S(2)}, u32[]{:S(2)}) collective-permute-start(bf16[128,1024]{1,0:T(8,128)(2,1)S(1)} %get-tuple-element.25), channel_id=1, source_target_pairs={{0,16},{8,24},{16,32},{24,40},{32,48},{40,56},{48,64},{56,72},{64,... | collective-permute-start | bytes 786440 | tf_op jit(solution)/shard_map/ppermute | solution.py:21
  96.8 47.0 %collective-permute-start.6 = (bf16[128,1024]{1,0:T(8,128)(2,1)S(1)}, bf16[128,1024]{1,0:T(8,128)(2,1)S(1)}, u32[]{:S(2)}, u32[]{:S(2)}) collective-permute-start(bf16[128,1024]{1,0:T(8,128)(2,1)S(1)} %get-tuple-element.26), channel_id=1, source_target_pairs={{0,752},{8,760},{16,0},{24,8},{32,16},{40,24},{48,32},{56,40},{64,... | collective-permute-start | bytes 786440 | tf_op jit(solution)/shard_map/ppermute | solution.py:21
  104.0 40.6 %collective-permute-start.5 = (bf16[128,1024]{1,0:T(8,128)(2,1)S(1)}, bf16[128,1024]{1,0:T(8,128)(2,1)S(1)}, u32[]{:S(2)}, u32[]{:S(2)}) collective-permute-start(bf16[128,1024]{1,0:T(8,128)(2,1)S(1)} %get-tuple-element.27), channel_id=1, source_target_pairs={{0,8},{8,16},{16,24},{24,32},{32,40},{40,48},{48,56},{56,64},{64,7... | collective-permute-start | bytes 786440 | tf_op jit(solution)/shard_map/ppermute | solution.py:21
  106.0 39.6 %collective-permute-start.4 = (bf16[128,1024]{1,0:T(8,128)(2,1)S(1)}, bf16[128,1024]{1,0:T(8,128)(2,1)S(1)}, u32[]{:S(2)}, u32[]{:S(2)}) collective-permute-start(bf16[128,1024]{1,0:T(8,128)(2,1)S(1)} %get-tuple-element.24), channel_id=1, source_target_pairs={{0,760},{8,0},{16,8},{24,16},{32,24},{40,32},{48,40},{56,48},{64,5... | collective-permute-start | bytes 786440 | tf_op jit(solution)/shard_map/ppermute | solution.py:21
Sparse Core Ops, SparseCore 0:
  10.4 66.1 all-gather.2
  78.9 60.6 all-gather.4

commit v8 on v7

--- a/solution.py
+++ b/solution.py
@@ -210,6 +210,17 @@
     )(tile_count, tiles, qg_blocks, st, k3, v3)
 
 
+def doubling_gather(x, axis):
+    size = lax.axis_size(axis)
+    me = lax.axis_index(axis)
+    step = 1
+    while step < size:
+        other = lax.ppermute(x, axis, [(i, i ^ step) for i in range(size)])
+        x = jnp.where((me & step) == 0, jnp.concatenate([x, other], 0), jnp.concatenate([other, x], 0))
+        step *= 2
+    return x
+
+
 def shards(query, key, value, out_grad, partner, tiles, tile_count):
     f32 = jnp.float32
     bf16 = jnp.bfloat16
@@ -239,7 +250,7 @@
 
     stats = stats[..., : 3 * HEADS].reshape(blocks_dev, BLOCK, 3, HEADS)
     stats = jnp.transpose(stats, (0, 2, 3, 1)).reshape(blocks_dev * 3 * HEADS, BLOCK)
-    stats_cluster = lax.all_gather(stats, "blk", axis=0, tiled=True)
+    stats_cluster = doubling_gather(stats, "blk")
 
     terms = terms.reshape(ROUNDS, nodes, 2 * width)
     returned = jnp.stack(

time: 165 us -> 162 us (0.982)
  the two profiles are of different devices: /device:TPU:24 before, /device:TPU:1 now
where the time goes in v8:
time: 162 us
  waiting for transfers between devices  51.3 us (32%)
  starting transfers between devices  50.5 us (31%)
  Pallas kernels  24.7 us (15%)
  between operations  14.3 us (9%)
  local copies, waits for them, and re-layouts  12.9 us (8%)
  other arithmetic  8.03 us (5%)
    ppermute x8, starting transfers between devices, passed_along(): return lax.ppermute(x, axis, [(i, (i + by) % size) for i in range(size)])  39.9 us
    all_gather x1, waiting for transfers between devices, shards(): kv_cluster = lax.all_gather(both, 'blk', axis=0, tiled=True)  33.4 us
    pallas_call x1, Pallas kernels, query_side(): pl.pallas_call(functools.partial(query_side_kernel, scale=scale), grid_sp...  15.6 us
    ppermute x3, starting transfers between devices, doubling_gather(): other = lax.ppermute(x, axis, [(i, i ^ step) for i in range(size)])  10.5 us
    pallas_call x1, Pallas kernels, key_side(): pl.pallas_call(functools.partial(key_side_kernel, scale=scale), grid_spec...  9.11 us
    ppermute x3, waiting for transfers between devices, doubling_gather(): other = lax.ppermute(x, axis, [(i, i ^ step) for i in range(size)])  8.59 us
    gather x8, local copies, waits for them, and re-layouts, fetch_partners(): return jnp.concatenate([ahead[slots[:half]], behind[slots[half:]]], 0)  6.89 us
    all_gather x1, waiting for transfers between devices, shards(): lax.all_gather(jnp.concatenate([query, out_grad], 1), 'blk', axis=0, tile...  6.65 us
  transfers between devices with their start and end apart: 13, of which 6 were waited for; matrix products, arithmetic and copies ran while one was open for 10% of the time, Pallas kernels for 10%

profile of v8, /device:TPU:1, one launch (start us, length us, event | category | flops | bytes accessed | tf_op | source)
XLA Modules:
  0.0 161.7 jit_solution(15239986068463023416)
XLA Ops:
  7.2 0.0 copy-start.1
  7.2 0.0 all-gather.3.cloned.1.call-start
  7.2 1.0 constant_dynamic-update-slice_fusion.1
  8.2 1.0 constant_dynamic-update-slice_fusion
  9.2 0.0 copy-start
  9.2 0.8 copy-done
  10.0 0.0 all-gather.3.cloned.1.call-update
  10.0 0.0 all-gather.5.cloned.1.call-start
  10.1 1.9 %pad_maximum_fusion.3 = bf16[256,1024]{1,0:T(8,128)(2,1)} fusion(bf16[256,512]{1,0:T(8,128)(2,1)} %param.10, bf16[256,512]{1,0:T(8,128)(2,1)} %param.7), kind=kLoop, calls=%fused_computation.14 | loop fusion | flops 1048576 | bytes 1048576 | tf_op jit(solution)/shard_map/concatenate | solution.py:236
  11.9 0.0 all-gather.5.cloned.1.call-update
  12.0 1.1 fusion.6
  13.0 3.9 %collective-permute-start.3 = (bf16[128,1024]{1,0:T(8,128)(2,1)S(1)}, bf16[128,1024]{1,0:T(8,128)(2,1)S(1)}, u32[]{:S(2)}, u32[]{:S(2)}) collective-permute-start(bf16[128,1024]{1,0:T(8,128)(2,1)S(1)} %get-tuple-element.29), channel_id=1, source_target_pairs={{0,16},{8,24},{16,32},{24,40},{32,48},{40,56},{48,64},{56,72},{64,... | collective-permute-start | bytes 786440 | tf_op jit(solution)/shard_map/ppermute | solution.py:21
  17.0 4.0 %collective-permute-start.1 = (bf16[128,1024]{1,0:T(8,128)(2,1)S(1)}, bf16[128,1024]{1,0:T(8,128)(2,1)S(1)}, u32[]{:S(2)}, u32[]{:S(2)}) collective-permute-start(bf16[128,1024]{1,0:T(8,128)(2,1)S(1)} %get-tuple-element.29), channel_id=1, source_target_pairs={{0,8},{8,16},{16,24},{24,32},{32,40},{40,48},{48,56},{56,64},{64,7... | collective-permute-start | bytes 786440 | tf_op jit(solution)/shard_map/ppermute | solution.py:21
  21.0 13.3 %collective-permute-start.2 = (bf16[128,1024]{1,0:T(8,128)(2,1)S(1)}, bf16[128,1024]{1,0:T(8,128)(2,1)S(1)}, u32[]{:S(2)}, u32[]{:S(2)}) collective-permute-start(bf16[128,1024]{1,0:T(8,128)(2,1)S(1)} %get-tuple-element.28), channel_id=1, source_target_pairs={{0,752},{8,760},{16,0},{24,8},{32,16},{40,24},{48,32},{56,40},{64,... | collective-permute-start | bytes 786440 | tf_op jit(solution)/shard_map/ppermute | solution.py:21
  34.2 2.9 %collective-permute-start = (bf16[128,1024]{1,0:T(8,128)(2,1)S(1)}, bf16[128,1024]{1,0:T(8,128)(2,1)S(1)}, u32[]{:S(2)}, u32[]{:S(2)}) collective-permute-start(bf16[128,1024]{1,0:T(8,128)(2,1)S(1)} %get-tuple-element.28), channel_id=1, source_target_pairs={{0,760},{8,0},{16,8},{24,16},{32,24},{40,32},{48,40},{56,48},{64,5... | collective-permute-start | bytes 786440 | tf_op jit(solution)/shard_map/ppermute | solution.py:21
  37.1 0.0 copy-done.1
  37.2 0.0 collective-permute-done.3
  37.2 0.9 gather_fusion.3
  38.0 1.2 collective-permute-done.2
  39.2 0.9 gather_fusion.2
  40.0 0.0 collective-permute-done.1
  40.1 0.9 gather_fusion.1
  40.9 1.4 collective-permute-done
  42.3 0.9 gather_fusion
  43.3 1.1 pad_maximum_fusion.pair_ref
  44.4 33.4 %all-gather.3.cloned.1.call-done = bf16[2048,1024]{1,0:T(8,128)(2,1)} async-done(((bf16[256,1024]{1,0:T(8,128)(2,1)}), bf16[2048,1024]{1,0:T(8,128)(2,1)}) %all-gather.3.cloned.1.call-update) | async-done | bytes 4194320 | tf_op jit(solution)/shard_map/all_gather | solution.py:235
  77.8 15.6 %shard_map.102 = (f32[2,128,512]{2,1,0:T(8,128)}, bf16[2,128,512]{2,1,0:T(8,128)(2,1)}, bf16[2,2,128,1024]{3,2,1,0:T(8,128)(2,1)}, f32[2,128,128]{2,1,0:T(8,128)}) custom-call(s32[2]{0:T(128)} %count_ref.3, s32[2,6]{1,0:T(2,128)} %tiles_ref.3, bf16[16,128,1024]{2,1,0:T(8,128)(2,1)} %bitcast.65, bf16[2,128,512]{2,1,0:T(8,128)(2,1)} %bitcast.58, ...), custom_call_target="tpu_custom_call" | custom-call | flops 1610612736 | bytes 9437184 | tf_op jit(solution)/shard_map/pallas_call | solution.py:132
  93.4 1.0 copy.12
  94.4 1.9 %collective-permute-start.8 = (f32[48,128]{1,0:T(8,128)S(1)}, f32[48,128]{1,0:T(8,128)S(1)}, u32[]{:S(2)}, u32[]{:S(2)}) collective-permute-start(f32[48,128]{1,0:T(8,128)S(1)} %bitcast.62), channel_id=1, source_target_pairs={{0,1},{1,0},{2,3},{3,2},{4,5},{5,4},{6,7},{7,6},{8,9},{9,8},{10,11... | collective-permute-start | bytes 73736 | tf_op jit(solution)/shard_map/ppermute | solution.py:218
  96.3 3.2 %collective-permute-done.8 = f32[48,128]{1,0:T(8,128)S(1)} collective-permute-done((f32[48,128]{1,0:T(8,128)S(1)}, f32[48,128]{1,0:T(8,128)S(1)}, u32[]{:S(2)}, u32[]{:S(2)}) %collective-permute-start.8) | collective-permute-done | bytes 24608 | tf_op jit(solution)/shard_map/ppermute | solution.py:218
  99.5 3.8 %collective-permute-start.9 = (f32[96,128]{1,0:T(8,128)S(1)}, f32[96,128]{1,0:T(8,128)S(1)}, u32[]{:S(2)}, u32[]{:S(2)}) collective-permute-start(f32[96,128]{1,0:T(8,128)S(1)} %maximum_select_fusion.2), channel_id=1, source_target_pairs={{0,2},{1,3},{2,0},{3,1},{4,6},{5,7},{6,4},{7,5},{8,10},{9,11},{10,... | collective-permute-start | bytes 147464 | tf_op jit(solution)/shard_map/ppermute | solution.py:218
  103.3 1.3 slice_bitcast_fusion.3
  104.6 3.1 %collective-permute-start.7 = (bf16[128,1024]{1,0:T(8,128)(2,1)S(1)}, bf16[128,1024]{1,0:T(8,128)(2,1)S(1)}, u32[]{:S(2)}, u32[]{:S(2)}) collective-permute-start(bf16[128,1024]{1,0:T(8,128)(2,1)S(1)} %get-tuple-element.25), channel_id=1, source_target_pairs={{0,16},{8,24},{16,32},{24,40},{32,48},{40,56},{48,64},{56,72},{64,... | collective-permute-start | bytes 786440 | tf_op jit(solution)/shard_map/ppermute | solution.py:21
  107.7 7.3 %collective-permute-start.6 = (bf16[128,1024]{1,0:T(8,128)(2,1)S(1)}, bf16[128,1024]{1,0:T(8,128)(2,1)S(1)}, u32[]{:S(2)}, u32[]{:S(2)}) collective-permute-start(bf16[128,1024]{1,0:T(8,128)(2,1)S(1)} %get-tuple-element.26), channel_id=1, source_target_pairs={{0,752},{8,760},{16,0},{24,8},{32,16},{40,24},{48,32},{56,40},{64,... | collective-permute-start | bytes 786440 | tf_op jit(solution)/shard_map/ppermute | solution.py:21
  115.0 1.9 %collective-permute-start.5 = (bf16[128,1024]{1,0:T(8,128)(2,1)S(1)}, bf16[128,1024]{1,0:T(8,128)(2,1)S(1)}, u32[]{:S(2)}, u32[]{:S(2)}) collective-permute-start(bf16[128,1024]{1,0:T(8,128)(2,1)S(1)} %get-tuple-element.27), channel_id=1, source_target_pairs={{0,8},{8,16},{16,24},{24,32},{32,40},{40,48},{48,56},{56,64},{64,7... | collective-permute-start | bytes 786440 | tf_op jit(solution)/shard_map/ppermute | solution.py:21
  116.9 3.6 %collective-permute-start.4 = (bf16[128,1024]{1,0:T(8,128)(2,1)S(1)}, bf16[128,1024]{1,0:T(8,128)(2,1)S(1)}, u32[]{:S(2)}, u32[]{:S(2)}) collective-permute-start(bf16[128,1024]{1,0:T(8,128)(2,1)S(1)} %get-tuple-element.24), channel_id=1, source_target_pairs={{0,760},{8,0},{16,8},{24,16},{32,24},{40,32},{48,40},{56,48},{64,5... | collective-permute-start | bytes 786440 | tf_op jit(solution)/shard_map/ppermute | solution.py:21
  120.4 0.0 collective-permute-done.9
  120.5 4.8 %collective-permute-start.10 = (f32[192,128]{1,0:T(8,128)S(1)}, f32[192,128]{1,0:T(8,128)S(1)}, u32[]{:S(2)}, u32[]{:S(2)}) collective-permute-start(f32[192,128]{1,0:T(8,128)S(1)} %maximum_select_fusion.1), channel_id=1, source_target_pairs={{0,4},{1,5},{2,6},{3,7},{4,0},{5,1},{6,2},{7,3},{8,12},{9,13},{10,... | collective-permute-start | bytes 294920 | tf_op jit(solution)/shard_map/ppermute | solution.py:218
  125.3 1.8 %convert_element_type.15 = bf16[2,128,512]{2,1,0:T(8,128)(2,1)} convert(f32[2,128,512]{2,1,0:T(8,128)} %get-tuple-element.13) | non-fusion elementwise | flops 131072 | bytes 786432 | tf_op jit(solution)/shard_map/convert_element_type | solution.py:274
  127.1 5.4 %collective-permute-done.10 = f32[192,128]{1,0:T(8,128)S(1)} collective-permute-done((f32[192,128]{1,0:T(8,128)S(1)}, f32[192,128]{1,0:T(8,128)S(1)}, u32[]{:S(2)}, u32[]{:S(2)}) %collective-permute-start.10) | collective-permute-done | bytes 98336 | tf_op jit(solution)/shard_map/ppermute | solution.py:218
  132.5 0.7 maximum_select_fusion
  133.2 0.0 collective-permute-done.7
  133.2 0.9 gather_fusion.7
  134.0 0.0 collective-permute-done.6
  134.1 0.9 gather_fusion.6
  134.9 0.0 collective-permute-done.5
  134.9 0.9 gather_fusion.5
  135.8 0.0 collective-permute-done.4
  135.8 0.9 gather_fusion.4
  136.7 0.2 convert_reduce_fusion
  137.0 6.6 %all-gather.5.cloned.1.call-done = bf16[2048,1024]{1,0:T(8,128)(2,1)} async-done(((bf16[256,1024]{1,0:T(8,128)(2,1)}), bf16[2048,1024]{1,0:T(8,128)(2,1)}) %all-gather.5.cloned.1.call-update) | async-done | bytes 4194320 | tf_op jit(solution)/shard_map/all_gather | solution.py:236
  143.6 9.1 %shard_map.103 = (f32[2,128,512]{2,1,0:T(8,128)}, f32[2,128,512]{2,1,0:T(8,128)}) custom-call(s32[2]{0:T(128)} %count_ref.3, s32[2,6]{1,0:T(2,128)} %tiles_ref.3, bf16[16,128,1024]{2,1,0:T(8,128)(2,1)} %bitcast.64, f32[16,3,8,128]{3,2,1,0:T(8,128)} %bitcast.60, bf16[2,128,512]{2,1,0:T(8,128)(2,1)} %bitcast.56, bf16[2,128,512]{2,1,0:T(8,128)(2,1)} %bitcast.57), custom_call_target="tpu_custom_call" | custom-call | flops 1610612736 | bytes 7536640 | tf_op jit(solution)/shard_map/pallas_call | solution.py:205
  152.7 2.1 %fusion = (bf16[256,512]{1,0:T(8,128)(2,1)}, bf16[256,512]{1,0:T(8,128)(2,1)}) fusion(f32[2,128,512]{2,1,0:T(8,128)} %get-tuple-element.21, f32[256,1024]{1,0:T(8,128)S(1)} %convert_reduce_fusion, f32[2,128,512]{2,1,0:T(8,128)} %get-tuple-element.19), kind=kLoop, calls=%fused_computation.16 | loop fusion | flops 524288 | bytes 2621440 | tf_op jit(solution)/shard_map/convert_element_type | solution.py:277
  (9 shorter events, 0.2 us)
Async XLA Ops:
  7.2 29.9 %copy-start.1 = (s32[2,256]{1,0:T(2,128)S(1)}, s32[2,256]{1,0:T(2,128)}, u32[]{:S(2)}) copy-start(s32[2,256]{1,0:T(2,128)} %param.11) | copy-start | bytes 6148
  7.2 70.7 %all-gather.3.cloned.1.call-start = ((), (), s32[]{:S(2)}) async-start(), calls=%async_computation | async-start | bytes 4718592 | tf_op jit(solution)/shard_map/all_gather | solution.py:235
  9.2 0.8 copy-start
  10.0 133.6 %all-gather.5.cloned.1.call-start = ((), (), s32[]{:S(2)}) async-start(), calls=%async_computation.1 | async-start | bytes 4718592 | tf_op jit(solution)/shard_map/all_gather | solution.py:236
  13.0 24.1 %collective-permute-start.3 = (bf16[128,1024]{1,0:T(8,128)(2,1)S(1)}, bf16[128,1024]{1,0:T(8,128)(2,1)S(1)}, u32[]{:S(2)}, u32[]{:S(2)}) collective-permute-start(bf16[128,1024]{1,0:T(8,128)(2,1)S(1)} %get-tuple-element.29), channel_id=1, source_target_pairs={{0,16},{8,24},{16,32},{24,40},{32,48},{40,56},{48,64},{56,72},{64,... | collective-permute-start | bytes 786440 | tf_op jit(solution)/shard_map/ppermute | solution.py:21
  17.0 23.1 %collective-permute-start.1 = (bf16[128,1024]{1,0:T(8,128)(2,1)S(1)}, bf16[128,1024]{1,0:T(8,128)(2,1)S(1)}, u32[]{:S(2)}, u32[]{:S(2)}) collective-permute-start(bf16[128,1024]{1,0:T(8,128)(2,1)S(1)} %get-tuple-element.29), channel_id=1, source_target_pairs={{0,8},{8,16},{16,24},{24,32},{32,40},{40,48},{48,56},{56,64},{64,7... | collective-permute-start | bytes 786440 | tf_op jit(solution)/shard_map/ppermute | solution.py:21
  21.0 18.2 %collective-permute-start.2 = (bf16[128,1024]{1,0:T(8,128)(2,1)S(1)}, bf16[128,1024]{1,0:T(8,128)(2,1)S(1)}, u32[]{:S(2)}, u32[]{:S(2)}) collective-permute-start(bf16[128,1024]{1,0:T(8,128)(2,1)S(1)} %get-tuple-element.28), channel_id=1, source_target_pairs={{0,752},{8,760},{16,0},{24,8},{32,16},{40,24},{48,32},{56,40},{64,... | collective-permute-start | bytes 786440 | tf_op jit(solution)/shard_map/ppermute | solution.py:21
  34.2 8.1 %collective-permute-start = (bf16[128,1024]{1,0:T(8,128)(2,1)S(1)}, bf16[128,1024]{1,0:T(8,128)(2,1)S(1)}, u32[]{:S(2)}, u32[]{:S(2)}) collective-permute-start(bf16[128,1024]{1,0:T(8,128)(2,1)S(1)} %get-tuple-element.28), channel_id=1, source_target_pairs={{0,760},{8,0},{16,8},{24,16},{32,24},{40,32},{48,40},{56,48},{64,5... | collective-permute-start | bytes 786440 | tf_op jit(solution)/shard_map/ppermute | solution.py:21
  94.4 5.1 %collective-permute-start.8 = (f32[48,128]{1,0:T(8,128)S(1)}, f32[48,128]{1,0:T(8,128)S(1)}, u32[]{:S(2)}, u32[]{:S(2)}) collective-permute-start(f32[48,128]{1,0:T(8,128)S(1)} %bitcast.62), channel_id=1, source_target_pairs={{0,1},{1,0},{2,3},{3,2},{4,5},{5,4},{6,7},{7,6},{8,9},{9,8},{10,11... | collective-permute-start | bytes 73736 | tf_op jit(solution)/shard_map/ppermute | solution.py:218
  99.5 20.9 %collective-permute-start.9 = (f32[96,128]{1,0:T(8,128)S(1)}, f32[96,128]{1,0:T(8,128)S(1)}, u32[]{:S(2)}, u32[]{:S(2)}) collective-permute-start(f32[96,128]{1,0:T(8,128)S(1)} %maximum_select_fusion.2), channel_id=1, source_target_pairs={{0,2},{1,3},{2,0},{3,1},{4,6},{5,7},{6,4},{7,5},{8,10},{9,11},{10,... | collective-permute-start | bytes 147464 | tf_op jit(solution)/shard_map/ppermute | solution.py:218
  104.6 28.6 %collective-permute-start.7 = (bf16[128,1024]{1,0:T(8,128)(2,1)S(1)}, bf16[128,1024]{1,0:T(8,128)(2,1)S(1)}, u32[]{:S(2)}, u32[]{:S(2)}) collective-permute-start(bf16[128,1024]{1,0:T(8,128)(2,1)S(1)} %get-tuple-element.25), channel_id=1, source_target_pairs={{0,16},{8,24},{16,32},{24,40},{32,48},{40,56},{48,64},{56,72},{64,... | collective-permute-start | bytes 786440 | tf_op jit(solution)/shard_map/ppermute | solution.py:21
  107.7 26.4 %collective-permute-start.6 = (bf16[128,1024]{1,0:T(8,128)(2,1)S(1)}, bf16[128,1024]{1,0:T(8,128)(2,1)S(1)}, u32[]{:S(2)}, u32[]{:S(2)}) collective-permute-start(bf16[128,1024]{1,0:T(8,128)(2,1)S(1)} %get-tuple-element.26), channel_id=1, source_target_pairs={{0,752},{8,760},{16,0},{24,8},{32,16},{40,24},{48,32},{56,40},{64,... | collective-permute-start | bytes 786440 | tf_op jit(solution)/shard_map/ppermute | solution.py:21
  115.0 20.0 %collective-permute-start.5 = (bf16[128,1024]{1,0:T(8,128)(2,1)S(1)}, bf16[128,1024]{1,0:T(8,128)(2,1)S(1)}, u32[]{:S(2)}, u32[]{:S(2)}) collective-permute-start(bf16[128,1024]{1,0:T(8,128)(2,1)S(1)} %get-tuple-element.27), channel_id=1, source_target_pairs={{0,8},{8,16},{16,24},{24,32},{32,40},{40,48},{48,56},{56,64},{64,7... | collective-permute-start | bytes 786440 | tf_op jit(solution)/shard_map/ppermute | solution.py:21
  116.9 18.9 %collective-permute-start.4 = (bf16[128,1024]{1,0:T(8,128)(2,1)S(1)}, bf16[128,1024]{1,0:T(8,128)(2,1)S(1)}, u32[]{:S(2)}, u32[]{:S(2)}) collective-permute-start(bf16[128,1024]{1,0:T(8,128)(2,1)S(1)} %get-tuple-element.24), channel_id=1, source_target_pairs={{0,760},{8,0},{16,8},{24,16},{32,24},{40,32},{48,40},{56,48},{64,5... | collective-permute-start | bytes 786440 | tf_op jit(solution)/shard_map/ppermute | solution.py:21
  120.5 12.0 %collective-permute-start.10 = (f32[192,128]{1,0:T(8,128)S(1)}, f32[192,128]{1,0:T(8,128)S(1)}, u32[]{:S(2)}, u32[]{:S(2)}) collective-permute-start(f32[192,128]{1,0:T(8,128)S(1)} %maximum_select_fusion.1), channel_id=1, source_target_pairs={{0,4},{1,5},{2,6},{3,7},{4,0},{5,1},{6,2},{7,3},{8,12},{9,13},{10,... | collective-permute-start | bytes 294920 | tf_op jit(solution)/shard_map/ppermute | solution.py:218
Sparse Core Ops, SparseCore 0:
  10.4 67.4 all-gather.2
  80.2 63.3 all-gather.4

commit v9 on v8

--- a/solution.py
+++ b/solution.py
@@ -142,7 +142,7 @@
     )(tile_count, tiles, kv_blocks, q3, g3, pair_rows)
 
 
-def key_side_kernel(count_ref, tiles_ref, qg_ref, st_ref, k_ref, v_ref, ks_ref, vs_ref, *, scale):
+def key_side_kernel(count_ref, tiles_ref, qg_ref, st_ref, k_ref, v_ref, ret_ref, ks_ref, vs_ref, *, scale):
     b = pl.program_id(0)
     width = k_ref.shape[-1]
     slots = tiles_ref.shape[1]
@@ -177,11 +177,13 @@
             z = (p * (d - delta)).astype(jnp.bfloat16)
             k_out.append(jnp.dot(z, qp, preferred_element_type=jnp.float32))
             v_out.append(jnp.dot(w, gp, preferred_element_type=jnp.float32))
-        ks_ref[0, :, cols] = jnp.where(low, k_out[0], k_out[1]) * scale
-        vs_ref[0, :, cols] = jnp.where(low, v_out[0], v_out[1])
-
-
-def key_side(tile_count, tiles, qg_blocks, st, k3, v3, scale):
+        k_sum = jnp.where(low, k_out[0], k_out[1]) * scale
+        v_sum = jnp.where(low, v_out[0], v_out[1])
+        ks_ref[0, :, cols] = (k_sum + ret_ref[0, :, cols]).astype(ks_ref.dtype)
+        vs_ref[0, :, cols] = (v_sum + ret_ref[0, :, pl.ds(width + pr * pair, pair)]).astype(vs_ref.dtype)
+
+
+def key_side(tile_count, tiles, qg_blocks, st, k3, v3, returned, scale):
     blocks, slots = tiles.shape
     keys = slots * BLOCK
     width = k3.shape[-1]
@@ -193,6 +195,7 @@
             pl.BlockSpec(memory_space=pltpu.VMEM),
             pl.BlockSpec((1, BLOCK, width), lambda b, c, t: (b, 0, 0)),
             pl.BlockSpec((1, BLOCK, width), lambda b, c, t: (b, 0, 0)),
+            pl.BlockSpec((1, BLOCK, 2 * width), lambda b, c, t: (b, 0, 0)),
         ],
         out_specs=[
             pl.BlockSpec((1, BLOCK, width), lambda b, c, t: (b, 0, 0)),
@@ -205,9 +208,9 @@
     return pl.pallas_call(
         functools.partial(key_side_kernel, scale=scale),
         grid_spec=grid_spec,
-        out_shape=[jax.ShapeDtypeStruct((blocks, BLOCK, width), jnp.float32)] * 2,
+        out_shape=[jax.ShapeDtypeStruct((blocks, BLOCK, width), jnp.bfloat16)] * 2,
         cost_estimate=cost,
-    )(tile_count, tiles, qg_blocks, st, k3, v3)
+    )(tile_count, tiles, qg_blocks, st, k3, v3, returned)
 
 
 def doubling_gather(x, axis):
@@ -261,20 +264,21 @@
         (returned, stats_cluster, qg_cluster)
     )
 
-    k_sum, v_sum = key_side(
+    key_grad, value_grad = key_side(
         tile_count,
         tiles,
         qg_cluster.reshape(cluster_blocks, BLOCK, 2 * width),
         stats_cluster.reshape(cluster_blocks, 3, HEADS, BLOCK),
         key.reshape(blocks_dev, BLOCK, width),
         value.reshape(blocks_dev, BLOCK, width),
+        returned.reshape(blocks_dev, BLOCK, 2 * width),
         scale,
     )
 
     attended = out_full.reshape(nodes, width).astype(bf16)
     query_grad = query_grad.reshape(nodes, width)
-    key_grad = (k_sum.reshape(nodes, width) + returned[:, :width]).astype(bf16)
-    value_grad = (v_sum.reshape(nodes, width) + returned[:, width:]).astype(bf16)
+    key_grad = key_grad.reshape(nodes, width)
+    value_grad = value_grad.reshape(nodes, width)
     return (attended, query_grad, key_grad, value_grad)
 
 

time: 162 us -> 160 us (0.988)
  waiting for transfers between devices: 51.3 us -> 46.2 us
  starting transfers between devices: 50.5 us -> 54.6 us
    all_gather x1, waiting for transfers between devices: 33.4 us -> 26.2 us  [shards(): kv_cluster = lax.all_gather(both, 'blk', axis=0, tiled=True)]
    ppermute x8, waiting for transfers between devices: 2.58 us -> 8.7 us  [passed_along(): return lax.ppermute(x, axis, [(i, (i + by) % size) for i in range(size)])]
    all_gather x1, waiting for transfers between devices: 6.65 us -> 0.88 us  [shards(): lax.all_gather(jnp.concatenate([query, out_grad], 1), 'blk', axis=0, tile...]
    ppermute x8, starting transfers between devices: 39.9 us -> 44.4 us  [passed_along(): return lax.ppermute(x, axis, [(i, (i + by) % size) for i in range(size)])]
    convert_element_type x1 -> x0, other arithmetic: 2.14 us -> none  [shards(): (v_sum.reshape(nodes, width) + returned[:, width:]).astype(bf16)]
    ppermute x3, waiting for transfers between devices: 8.59 us -> 10.3 us  [doubling_gather(): other = lax.ppermute(x, axis, [(i, i ^ step) for i in range(size)])]
  transfers between devices with their start and end apart: 13 -> 13, of which waited for: 6 -> 6; matrix products, arithmetic and copies ran while one was open for 10% -> 11% of each run, Pallas kernels for 10% -> 10%
where the time goes in v9:
time: 160 us
  starting transfers between devices  54.6 us (34%)
  waiting for transfers between devices  46.2 us (29%)
  Pallas kernels  24.7 us (15%)
  between operations  14.3 us (9%)
  local copies, waits for them, and re-layouts  12.9 us (8%)
  other arithmetic  6.89 us (4%)
    ppermute x8, starting transfers between devices, passed_along(): return lax.ppermute(x, axis, [(i, (i + by) % size) for i in range(size)])  44.4 us
    all_gather x1, waiting for transfers between devices, shards(): kv_cluster = lax.all_gather(both, 'blk', axis=0, tiled=True)  26.2 us
    pallas_call x1, Pallas kernels, query_side(): pl.pallas_call(functools.partial(query_side_kernel, scale=scale), grid_sp...  15.6 us
    ppermute x3, waiting for transfers between devices, doubling_gather(): other = lax.ppermute(x, axis, [(i, i ^ step) for i in range(size)])  10.3 us
    ppermute x3, starting transfers between devices, doubling_gather(): other = lax.ppermute(x, axis, [(i, i ^ step) for i in range(size)])  10.2 us
    pallas_call x1, Pallas kernels, key_side(): pl.pallas_call(functools.partial(key_side_kernel, scale=scale), grid_spec...  9.14 us
    ppermute x8, waiting for transfers between devices, passed_along(): return lax.ppermute(x, axis, [(i, (i + by) % size) for i in range(size)])  8.7 us
    gather x8, local copies, waits for them, and re-layouts, fetch_partners(): return jnp.concatenate([ahead[slots[:half]], behind[slots[half:]]], 0)  6.89 us
  transfers between devices with their start and end apart: 13, of which 6 were waited for; matrix products, arithmetic and copies ran while one was open for 11% of the time, Pallas kernels for 10%

profile of v9, /device:TPU:1, one launch (start us, length us, event | category | flops | bytes accessed | tf_op | source)
XLA Modules:
  0.0 159.6 jit_solution(377695557854878185)
XLA Ops:
  7.2 0.0 copy-start.1
  7.2 0.0 all-gather.3.cloned.1.call-start
  7.2 1.0 constant_dynamic-update-slice_fusion.1
  8.2 1.0 constant_dynamic-update-slice_fusion
  9.2 0.0 copy-start
  9.2 0.8 copy-done
  10.0 0.0 all-gather.3.cloned.1.call-update
  10.0 0.0 all-gather.5.cloned.1.call-start
  10.1 1.9 %pad_maximum_fusion.3 = bf16[256,1024]{1,0:T(8,128)(2,1)} fusion(bf16[256,512]{1,0:T(8,128)(2,1)} %param.10, bf16[256,512]{1,0:T(8,128)(2,1)} %param.7), kind=kLoop, calls=%fused_computation.14 | loop fusion | flops 1048576 | bytes 1048576 | tf_op jit(solution)/shard_map/concatenate | solution.py:239
  11.9 0.0 all-gather.5.cloned.1.call-update
  12.0 1.1 fusion.4
  13.0 12.4 %collective-permute-start = (bf16[128,1024]{1,0:T(8,128)(2,1)S(1)}, bf16[128,1024]{1,0:T(8,128)(2,1)S(1)}, u32[]{:S(2)}, u32[]{:S(2)}) collective-permute-start(bf16[128,1024]{1,0:T(8,128)(2,1)S(1)} %get-tuple-element.26), channel_id=1, source_target_pairs={{0,760},{8,0},{16,8},{24,16},{32,24},{40,32},{48,40},{56,48},{64,5... | collective-permute-start | bytes 786440 | tf_op jit(solution)/shard_map/ppermute | solution.py:21
  25.5 7.5 %collective-permute-start.2 = (bf16[128,1024]{1,0:T(8,128)(2,1)S(1)}, bf16[128,1024]{1,0:T(8,128)(2,1)S(1)}, u32[]{:S(2)}, u32[]{:S(2)}) collective-permute-start(bf16[128,1024]{1,0:T(8,128)(2,1)S(1)} %get-tuple-element.26), channel_id=1, source_target_pairs={{0,752},{8,760},{16,0},{24,8},{32,16},{40,24},{48,32},{56,40},{64,... | collective-permute-start | bytes 786440 | tf_op jit(solution)/shard_map/ppermute | solution.py:21
  33.0 3.3 %collective-permute-start.1 = (bf16[128,1024]{1,0:T(8,128)(2,1)S(1)}, bf16[128,1024]{1,0:T(8,128)(2,1)S(1)}, u32[]{:S(2)}, u32[]{:S(2)}) collective-permute-start(bf16[128,1024]{1,0:T(8,128)(2,1)S(1)} %get-tuple-element.27), channel_id=1, source_target_pairs={{0,8},{8,16},{16,24},{24,32},{32,40},{40,48},{48,56},{56,64},{64,7... | collective-permute-start | bytes 786440 | tf_op jit(solution)/shard_map/ppermute | solution.py:21
  36.2 1.9 %collective-permute-start.3 = (bf16[128,1024]{1,0:T(8,128)(2,1)S(1)}, bf16[128,1024]{1,0:T(8,128)(2,1)S(1)}, u32[]{:S(2)}, u32[]{:S(2)}) collective-permute-start(bf16[128,1024]{1,0:T(8,128)(2,1)S(1)} %get-tuple-element.27), channel_id=1, source_target_pairs={{0,16},{8,24},{16,32},{24,40},{32,48},{40,56},{48,64},{56,72},{64,... | collective-permute-start | bytes 786440 | tf_op jit(solution)/shard_map/ppermute | solution.py:21
  38.2 0.0 copy-done.1
  38.2 0.0 collective-permute-done
  38.2 0.9 gather_fusion
  39.1 0.7 collective-permute-done.1
  39.8 0.9 gather_fusion.1
  40.6 0.0 collective-permute-done.2
  40.6 0.9 gather_fusion.2
  41.5 8.0 %collective-permute-done.3 = bf16[128,1024]{1,0:T(8,128)(2,1)S(1)} collective-permute-done((bf16[128,1024]{1,0:T(8,128)(2,1)S(1)}, bf16[128,1024]{1,0:T(8,128)(2,1)S(1)}, u32[]{:S(2)}, u32[]{:S(2)}) %collective-permute-start.3) | collective-permute-done | bytes 262176 | tf_op jit(solution)/shard_map/ppermute | solution.py:21
  49.5 0.9 gather_fusion.3
  50.5 1.1 pad_maximum_fusion.pair_ref
  51.6 26.2 %all-gather.3.cloned.1.call-done = bf16[2048,1024]{1,0:T(8,128)(2,1)} async-done(((bf16[256,1024]{1,0:T(8,128)(2,1)}), bf16[2048,1024]{1,0:T(8,128)(2,1)}) %all-gather.3.cloned.1.call-update) | async-done | bytes 4194320 | tf_op jit(solution)/shard_map/all_gather | solution.py:238
  77.8 15.6 %shard_map.102 = (f32[2,128,512]{2,1,0:T(8,128)}, bf16[2,128,512]{2,1,0:T(8,128)(2,1)}, bf16[2,2,128,1024]{3,2,1,0:T(8,128)(2,1)}, f32[2,128,128]{2,1,0:T(8,128)}) custom-call(s32[2]{0:T(128)} %count_ref.3, s32[2,6]{1,0:T(2,128)} %tiles_ref.3, bf16[16,128,1024]{2,1,0:T(8,128)(2,1)} %bitcast.61, bf16[2,128,512]{2,1,0:T(8,128)(2,1)} %bitcast.56, ...), custom_call_target="tpu_custom_call" | custom-call | flops 1610612736 | bytes 9437184 | tf_op jit(solution)/shard_map/pallas_call | solution.py:132
  93.4 1.0 copy.12
  94.4 1.9 %collective-permute-start.8 = (f32[48,128]{1,0:T(8,128)S(1)}, f32[48,128]{1,0:T(8,128)S(1)}, u32[]{:S(2)}, u32[]{:S(2)}) collective-permute-start(f32[48,128]{1,0:T(8,128)S(1)} %bitcast.59), channel_id=1, source_target_pairs={{0,1},{1,0},{2,3},{3,2},{4,5},{5,4},{6,7},{7,6},{8,9},{9,8},{10,11... | collective-permute-start | bytes 73736 | tf_op jit(solution)/shard_map/ppermute | solution.py:221
  96.3 3.2 %collective-permute-done.8 = f32[48,128]{1,0:T(8,128)S(1)} collective-permute-done((f32[48,128]{1,0:T(8,128)S(1)}, f32[48,128]{1,0:T(8,128)S(1)}, u32[]{:S(2)}, u32[]{:S(2)}) %collective-permute-start.8) | collective-permute-done | bytes 24608 | tf_op jit(solution)/shard_map/ppermute | solution.py:221
  99.5 3.8 %collective-permute-start.9 = (f32[96,128]{1,0:T(8,128)S(1)}, f32[96,128]{1,0:T(8,128)S(1)}, u32[]{:S(2)}, u32[]{:S(2)}) collective-permute-start(f32[96,128]{1,0:T(8,128)S(1)} %maximum_select_fusion.2), channel_id=1, source_target_pairs={{0,2},{1,3},{2,0},{3,1},{4,6},{5,7},{6,4},{7,5},{8,10},{9,11},{10,... | collective-permute-start | bytes 147464 | tf_op jit(solution)/shard_map/ppermute | solution.py:221
  103.3 1.3 slice_bitcast_fusion.3
  104.6 3.3 %collective-permute-start.4 = (bf16[128,1024]{1,0:T(8,128)(2,1)S(1)}, bf16[128,1024]{1,0:T(8,128)(2,1)S(1)}, u32[]{:S(2)}, u32[]{:S(2)}) collective-permute-start(bf16[128,1024]{1,0:T(8,128)(2,1)S(1)} %get-tuple-element.22), channel_id=1, source_target_pairs={{0,760},{8,0},{16,8},{24,16},{32,24},{40,32},{48,40},{56,48},{64,5... | collective-permute-start | bytes 786440 | tf_op jit(solution)/shard_map/ppermute | solution.py:21
  107.9 3.1 %collective-permute-start.5 = (bf16[128,1024]{1,0:T(8,128)(2,1)S(1)}, bf16[128,1024]{1,0:T(8,128)(2,1)S(1)}, u32[]{:S(2)}, u32[]{:S(2)}) collective-permute-start(bf16[128,1024]{1,0:T(8,128)(2,1)S(1)} %get-tuple-element.25), channel_id=1, source_target_pairs={{0,8},{8,16},{16,24},{24,32},{32,40},{40,48},{48,56},{56,64},{64,7... | collective-permute-start | bytes 786440 | tf_op jit(solution)/shard_map/ppermute | solution.py:21
  110.9 11.0 %collective-permute-start.6 = (bf16[128,1024]{1,0:T(8,128)(2,1)S(1)}, bf16[128,1024]{1,0:T(8,128)(2,1)S(1)}, u32[]{:S(2)}, u32[]{:S(2)}) collective-permute-start(bf16[128,1024]{1,0:T(8,128)(2,1)S(1)} %get-tuple-element.24), channel_id=1, source_target_pairs={{0,752},{8,760},{16,0},{24,8},{32,16},{40,24},{48,32},{56,40},{64,... | collective-permute-start | bytes 786440 | tf_op jit(solution)/shard_map/ppermute | solution.py:21
  121.9 1.9 %collective-permute-start.7 = (bf16[128,1024]{1,0:T(8,128)(2,1)S(1)}, bf16[128,1024]{1,0:T(8,128)(2,1)S(1)}, u32[]{:S(2)}, u32[]{:S(2)}) collective-permute-start(bf16[128,1024]{1,0:T(8,128)(2,1)S(1)} %get-tuple-element.23), channel_id=1, source_target_pairs={{0,16},{8,24},{16,32},{24,40},{32,48},{40,56},{48,64},{56,72},{64,... | collective-permute-start | bytes 786440 | tf_op jit(solution)/shard_map/ppermute | solution.py:21
  123.9 0.0 collective-permute-done.9
  123.9 4.5 %collective-permute-start.10 = (f32[192,128]{1,0:T(8,128)S(1)}, f32[192,128]{1,0:T(8,128)S(1)}, u32[]{:S(2)}, u32[]{:S(2)}) collective-permute-start(f32[192,128]{1,0:T(8,128)S(1)} %maximum_select_fusion.1), channel_id=1, source_target_pairs={{0,4},{1,5},{2,6},{3,7},{4,0},{5,1},{6,2},{7,3},{8,12},{9,13},{10,... | collective-permute-start | bytes 294920 | tf_op jit(solution)/shard_map/ppermute | solution.py:221
  128.4 1.8 %convert_element_type.9 = bf16[2,128,512]{2,1,0:T(8,128)(2,1)} convert(f32[2,128,512]{2,1,0:T(8,128)} %get-tuple-element.13) | non-fusion elementwise | flops 131072 | bytes 786432 | tf_op jit(solution)/shard_map/convert_element_type | solution.py:278
  130.2 7.1 %collective-permute-done.10 = f32[192,128]{1,0:T(8,128)S(1)} collective-permute-done((f32[192,128]{1,0:T(8,128)S(1)}, f32[192,128]{1,0:T(8,128)S(1)}, u32[]{:S(2)}, u32[]{:S(2)}) %collective-permute-start.10) | collective-permute-done | bytes 98336 | tf_op jit(solution)/shard_map/ppermute | solution.py:221
  137.3 0.7 maximum_select_fusion
  138.0 0.0 collective-permute-done.4
  138.0 0.9 gather_fusion.4
  138.8 0.0 collective-permute-done.5
  138.8 0.9 gather_fusion.5
  139.7 0.0 collective-permute-done.6
  139.7 0.9 gather_fusion.6
  140.6 0.0 collective-permute-done.7
  140.6 0.9 gather_fusion.7
  141.5 1.2 convert_reduce_fusion
  142.7 0.9 all-gather.5.cloned.1.call-done
  143.6 9.1 %shard_map.103 = (bf16[2,128,512]{2,1,0:T(8,128)(2,1)}, bf16[2,128,512]{2,1,0:T(8,128)(2,1)}) custom-call(s32[2]{0:T(128)} %count_ref.3, s32[2,6]{1,0:T(2,128)} %tiles_ref.3, bf16[16,128,1024]{2,1,0:T(8,128)(2,1)} %bitcast.48, f32[16,3,8,128]{3,2,1,0:T(8,128)} %bitcast.54, bf16[2,128,512]{2,1,0:T(8,128)(2,1)} %bitcast.52, bf16[2,128,512]{2,1,0:T(8,128)(2,1)} %bitcast.53, ...), custom_call_target="tpu_custom_call" | custom-call | flops 1610612736 | bytes 7536640 | tf_op jit(solution)/shard_map/pallas_call | solution.py:208
  (9 shorter events, 0.2 us)
Async XLA Ops:
  7.2 31.0 %copy-start.1 = (s32[2,256]{1,0:T(2,128)S(1)}, s32[2,256]{1,0:T(2,128)}, u32[]{:S(2)}) copy-start(s32[2,256]{1,0:T(2,128)} %param.11) | copy-start | bytes 6148
  7.2 70.7 %all-gather.3.cloned.1.call-start = ((), (), s32[]{:S(2)}) async-start(), calls=%async_computation | async-start | bytes 4718592 | tf_op jit(solution)/shard_map/all_gather | solution.py:238
  9.2 0.8 copy-start
  10.0 133.6 %all-gather.5.cloned.1.call-start = ((), (), s32[]{:S(2)}) async-start(), calls=%async_computation.1 | async-start | bytes 4718592 | tf_op jit(solution)/shard_map/all_gather | solution.py:239
  13.0 25.2 %collective-permute-start = (bf16[128,1024]{1,0:T(8,128)(2,1)S(1)}, bf16[128,1024]{1,0:T(8,128)(2,1)S(1)}, u32[]{:S(2)}, u32[]{:S(2)}) collective-permute-start(bf16[128,1024]{1,0:T(8,128)(2,1)S(1)} %get-tuple-element.26), channel_id=1, source_target_pairs={{0,760},{8,0},{16,8},{24,16},{32,24},{40,32},{48,40},{56,48},{64,5... | collective-permute-start | bytes 786440 | tf_op jit(solution)/shard_map/ppermute | solution.py:21
  25.5 15.2 %collective-permute-start.2 = (bf16[128,1024]{1,0:T(8,128)(2,1)S(1)}, bf16[128,1024]{1,0:T(8,128)(2,1)S(1)}, u32[]{:S(2)}, u32[]{:S(2)}) collective-permute-start(bf16[128,1024]{1,0:T(8,128)(2,1)S(1)} %get-tuple-element.26), channel_id=1, source_target_pairs={{0,752},{8,760},{16,0},{24,8},{32,16},{40,24},{48,32},{56,40},{64,... | collective-permute-start | bytes 786440 | tf_op jit(solution)/shard_map/ppermute | solution.py:21
  33.0 6.8 %collective-permute-start.1 = (bf16[128,1024]{1,0:T(8,128)(2,1)S(1)}, bf16[128,1024]{1,0:T(8,128)(2,1)S(1)}, u32[]{:S(2)}, u32[]{:S(2)}) collective-permute-start(bf16[128,1024]{1,0:T(8,128)(2,1)S(1)} %get-tuple-element.27), channel_id=1, source_target_pairs={{0,8},{8,16},{16,24},{24,32},{32,40},{40,48},{48,56},{56,64},{64,7... | collective-permute-start | bytes 786440 | tf_op jit(solution)/shard_map/ppermute | solution.py:21
  36.2 13.3 %collective-permute-start.3 = (bf16[128,1024]{1,0:T(8,128)(2,1)S(1)}, bf16[128,1024]{1,0:T(8,128)(2,1)S(1)}, u32[]{:S(2)}, u32[]{:S(2)}) collective-permute-start(bf16[128,1024]{1,0:T(8,128)(2,1)S(1)} %get-tuple-element.27), channel_id=1, source_target_pairs={{0,16},{8,24},{16,32},{24,40},{32,48},{40,56},{48,64},{56,72},{64,... | collective-permute-start | bytes 786440 | tf_op jit(solution)/shard_map/ppermute | solution.py:21
  94.4 5.1 %collective-permute-start.8 = (f32[48,128]{1,0:T(8,128)S(1)}, f32[48,128]{1,0:T(8,128)S(1)}, u32[]{:S(2)}, u32[]{:S(2)}) collective-permute-start(f32[48,128]{1,0:T(8,128)S(1)} %bitcast.59), channel_id=1, source_target_pairs={{0,1},{1,0},{2,3},{3,2},{4,5},{5,4},{6,7},{7,6},{8,9},{9,8},{10,11... | collective-permute-start | bytes 73736 | tf_op jit(solution)/shard_map/ppermute | solution.py:221
  99.5 24.3 %collective-permute-start.9 = (f32[96,128]{1,0:T(8,128)S(1)}, f32[96,128]{1,0:T(8,128)S(1)}, u32[]{:S(2)}, u32[]{:S(2)}) collective-permute-start(f32[96,128]{1,0:T(8,128)S(1)} %maximum_select_fusion.2), channel_id=1, source_target_pairs={{0,2},{1,3},{2,0},{3,1},{4,6},{5,7},{6,4},{7,5},{8,10},{9,11},{10,... | collective-permute-start | bytes 147464 | tf_op jit(solution)/shard_map/ppermute | solution.py:221
  104.6 33.4 %collective-permute-start.4 = (bf16[128,1024]{1,0:T(8,128)(2,1)S(1)}, bf16[128,1024]{1,0:T(8,128)(2,1)S(1)}, u32[]{:S(2)}, u32[]{:S(2)}) collective-permute-start(bf16[128,1024]{1,0:T(8,128)(2,1)S(1)} %get-tuple-element.22), channel_id=1, source_target_pairs={{0,760},{8,0},{16,8},{24,16},{32,24},{40,32},{48,40},{56,48},{64,5... | collective-permute-start | bytes 786440 | tf_op jit(solution)/shard_map/ppermute | solution.py:21
  107.9 31.0 %collective-permute-start.5 = (bf16[128,1024]{1,0:T(8,128)(2,1)S(1)}, bf16[128,1024]{1,0:T(8,128)(2,1)S(1)}, u32[]{:S(2)}, u32[]{:S(2)}) collective-permute-start(bf16[128,1024]{1,0:T(8,128)(2,1)S(1)} %get-tuple-element.25), channel_id=1, source_target_pairs={{0,8},{8,16},{16,24},{24,32},{32,40},{40,48},{48,56},{56,64},{64,7... | collective-permute-start | bytes 786440 | tf_op jit(solution)/shard_map/ppermute | solution.py:21
  110.9 28.8 %collective-permute-start.6 = (bf16[128,1024]{1,0:T(8,128)(2,1)S(1)}, bf16[128,1024]{1,0:T(8,128)(2,1)S(1)}, u32[]{:S(2)}, u32[]{:S(2)}) collective-permute-start(bf16[128,1024]{1,0:T(8,128)(2,1)S(1)} %get-tuple-element.24), channel_id=1, source_target_pairs={{0,752},{8,760},{16,0},{24,8},{32,16},{40,24},{48,32},{56,40},{64,... | collective-permute-start | bytes 786440 | tf_op jit(solution)/shard_map/ppermute | solution.py:21
  121.9 18.6 %collective-permute-start.7 = (bf16[128,1024]{1,0:T(8,128)(2,1)S(1)}, bf16[128,1024]{1,0:T(8,128)(2,1)S(1)}, u32[]{:S(2)}, u32[]{:S(2)}) collective-permute-start(bf16[128,1024]{1,0:T(8,128)(2,1)S(1)} %get-tuple-element.23), channel_id=1, source_target_pairs={{0,16},{8,24},{16,32},{24,40},{32,48},{40,56},{48,64},{56,72},{64,... | collective-permute-start | bytes 786440 | tf_op jit(solution)/shard_map/ppermute | solution.py:21
  123.9 13.4 %collective-permute-start.10 = (f32[192,128]{1,0:T(8,128)S(1)}, f32[192,128]{1,0:T(8,128)S(1)}, u32[]{:S(2)}, u32[]{:S(2)}) collective-permute-start(f32[192,128]{1,0:T(8,128)S(1)} %maximum_select_fusion.1), channel_id=1, source_target_pairs={{0,4},{1,5},{2,6},{3,7},{4,0},{5,1},{6,2},{7,3},{8,12},{9,13},{10,... | collective-permute-start | bytes 294920 | tf_op jit(solution)/shard_map/ppermute | solution.py:221
Sparse Core Ops, SparseCore 0:
  10.4 67.4 all-gather.2
  80.2 63.3 all-gather.4

commit v10 on v9

--- a/solution.py
+++ b/solution.py
@@ -216,12 +216,15 @@
 def doubling_gather(x, axis):
     size = lax.axis_size(axis)
     me = lax.axis_index(axis)
-    step = 1
-    while step < size:
+    bits = size.bit_length() - 1
+    step = size // 2
+    while step >= 1:
         other = lax.ppermute(x, axis, [(i, i ^ step) for i in range(size)])
         x = jnp.where((me & step) == 0, jnp.concatenate([x, other], 0), jnp.concatenate([other, x], 0))
-        step *= 2
-    return x
+        step //= 2
+    pieces = x.reshape((2,) * bits + (x.shape[0] // size,) + x.shape[1:])
+    order = tuple(reversed(range(bits))) + tuple(range(bits, pieces.ndim))
+    return jnp.transpose(pieces, order).reshape(x.shape)
 
 
 def shards(query, key, value, out_grad, partner, tiles, tile_count):

time: 160 us -> 158 us (0.988)
  waiting for transfers between devices: 46.2 us -> 42.2 us
  starting transfers between devices: 54.6 us -> 56.7 us
    ppermute x3, waiting for transfers between devices: 10.3 us -> 6.71 us  [doubling_gather(): other = lax.ppermute(x, axis, [(i, i ^ step) for i in range(size)])]
    ppermute x3, starting transfers between devices: 10.2 us -> 12.4 us  [doubling_gather(): other = lax.ppermute(x, axis, [(i, i ^ step) for i in range(size)])]
where the time goes in v10:
time: 158 us
  starting transfers between devices  56.7 us (36%)
  waiting for transfers between devices  42.2 us (27%)
  Pallas kernels  24.7 us (16%)
  between operations  14.3 us (9%)
  local copies, waits for them, and re-layouts  13.6 us (9%)
  other arithmetic  6.19 us (4%)
    ppermute x8, starting transfers between devices, passed_along(): return lax.ppermute(x, axis, [(i, (i + by) % size) for i in range(size)])  44.3 us
    all_gather x1, waiting for transfers between devices, shards(): kv_cluster = lax.all_gather(both, 'blk', axis=0, tiled=True)  26.2 us
    pallas_call x1, Pallas kernels, query_side(): pl.pallas_call(functools.partial(query_side_kernel, scale=scale), grid_sp...  15.6 us
    ppermute x3, starting transfers between devices, doubling_gather(): other = lax.ppermute(x, axis, [(i, i ^ step) for i in range(size)])  12.4 us
    pallas_call x1, Pallas kernels, key_side(): pl.pallas_call(functools.partial(key_side_kernel, scale=scale), grid_spec...  9.15 us
    ppermute x8, waiting for transfers between devices, passed_along(): return lax.ppermute(x, axis, [(i, (i + by) % size) for i in range(size)])  8.7 us
    gather x8, local copies, waits for them, and re-layouts, fetch_partners(): return jnp.concatenate([ahead[slots[:half]], behind[slots[half:]]], 0)  6.89 us
    ppermute x3, waiting for transfers between devices, doubling_gather(): other = lax.ppermute(x, axis, [(i, i ^ step) for i in range(size)])  6.71 us
  transfers between devices with their start and end apart: 13, of which 6 were waited for; matrix products, arithmetic and copies ran while one was open for 11% of the time, Pallas kernels for 10%

profile of v10, /device:TPU:1, one launch (start us, length us, event | category | flops | bytes accessed | tf_op | source)
XLA Modules:
  0.0 157.8 jit_solution(3978187915657984692)
XLA Ops:
  7.2 0.0 copy-start.1
  7.2 0.0 all-gather.3.cloned.1.call-start
  7.2 1.0 constant_dynamic-update-slice_fusion.1
  8.2 1.0 constant_dynamic-update-slice_fusion
  9.2 0.0 copy-start
  9.2 0.8 copy-done
  10.0 0.0 all-gather.3.cloned.1.call-update
  10.0 0.0 all-gather.5.cloned.1.call-start
  10.1 1.9 %pad_maximum_fusion.3 = bf16[256,1024]{1,0:T(8,128)(2,1)} fusion(bf16[256,512]{1,0:T(8,128)(2,1)} %param.10, bf16[256,512]{1,0:T(8,128)(2,1)} %param.7), kind=kLoop, calls=%fused_computation.14 | loop fusion | flops 1048576 | bytes 1048576 | tf_op jit(solution)/shard_map/concatenate | solution.py:242
  11.9 0.0 all-gather.5.cloned.1.call-update
  12.0 1.1 fusion.4
  13.0 12.4 %collective-permute-start = (bf16[128,1024]{1,0:T(8,128)(2,1)S(1)}, bf16[128,1024]{1,0:T(8,128)(2,1)S(1)}, u32[]{:S(2)}, u32[]{:S(2)}) collective-permute-start(bf16[128,1024]{1,0:T(8,128)(2,1)S(1)} %get-tuple-element.26), channel_id=1, source_target_pairs={{0,760},{8,0},{16,8},{24,16},{32,24},{40,32},{48,40},{56,48},{64,5... | collective-permute-start | bytes 786440 | tf_op jit(solution)/shard_map/ppermute | solution.py:21
  25.5 7.5 %collective-permute-start.2 = (bf16[128,1024]{1,0:T(8,128)(2,1)S(1)}, bf16[128,1024]{1,0:T(8,128)(2,1)S(1)}, u32[]{:S(2)}, u32[]{:S(2)}) collective-permute-start(bf16[128,1024]{1,0:T(8,128)(2,1)S(1)} %get-tuple-element.26), channel_id=1, source_target_pairs={{0,752},{8,760},{16,0},{24,8},{32,16},{40,24},{48,32},{56,40},{64,... | collective-permute-start | bytes 786440 | tf_op jit(solution)/shard_map/ppermute | solution.py:21
  33.0 3.3 %collective-permute-start.1 = (bf16[128,1024]{1,0:T(8,128)(2,1)S(1)}, bf16[128,1024]{1,0:T(8,128)(2,1)S(1)}, u32[]{:S(2)}, u32[]{:S(2)}) collective-permute-start(bf16[128,1024]{1,0:T(8,128)(2,1)S(1)} %get-tuple-element.27), channel_id=1, source_target_pairs={{0,8},{8,16},{16,24},{24,32},{32,40},{40,48},{48,56},{56,64},{64,7... | collective-permute-start | bytes 786440 | tf_op jit(solution)/shard_map/ppermute | solution.py:21
  36.2 1.9 %collective-permute-start.3 = (bf16[128,1024]{1,0:T(8,128)(2,1)S(1)}, bf16[128,1024]{1,0:T(8,128)(2,1)S(1)}, u32[]{:S(2)}, u32[]{:S(2)}) collective-permute-start(bf16[128,1024]{1,0:T(8,128)(2,1)S(1)} %get-tuple-element.27), channel_id=1, source_target_pairs={{0,16},{8,24},{16,32},{24,40},{32,48},{40,56},{48,64},{56,72},{64,... | collective-permute-start | bytes 786440 | tf_op jit(solution)/shard_map/ppermute | solution.py:21
  38.2 0.0 copy-done.1
  38.2 0.0 collective-permute-done
  38.2 0.9 gather_fusion
  39.1 0.7 collective-permute-done.1
  39.8 0.9 gather_fusion.1
  40.6 0.0 collective-permute-done.2
  40.6 0.9 gather_fusion.2
  41.5 8.0 %collective-permute-done.3 = bf16[128,1024]{1,0:T(8,128)(2,1)S(1)} collective-permute-done((bf16[128,1024]{1,0:T(8,128)(2,1)S(1)}, bf16[128,1024]{1,0:T(8,128)(2,1)S(1)}, u32[]{:S(2)}, u32[]{:S(2)}) %collective-permute-start.3) | collective-permute-done | bytes 262176 | tf_op jit(solution)/shard_map/ppermute | solution.py:21
  49.5 0.9 gather_fusion.3
  50.5 1.1 pad_maximum_fusion.pair_ref
  51.6 26.2 %all-gather.3.cloned.1.call-done = bf16[2048,1024]{1,0:T(8,128)(2,1)} async-done(((bf16[256,1024]{1,0:T(8,128)(2,1)}), bf16[2048,1024]{1,0:T(8,128)(2,1)}) %all-gather.3.cloned.1.call-update) | async-done | bytes 4194320 | tf_op jit(solution)/shard_map/all_gather | solution.py:241
  77.8 15.6 %shard_map.102 = (f32[2,128,512]{2,1,0:T(8,128)}, bf16[2,128,512]{2,1,0:T(8,128)(2,1)}, bf16[2,2,128,1024]{3,2,1,0:T(8,128)(2,1)}, f32[2,128,128]{2,1,0:T(8,128)}) custom-call(s32[2]{0:T(128)} %count_ref.3, s32[2,6]{1,0:T(2,128)} %tiles_ref.3, bf16[16,128,1024]{2,1,0:T(8,128)(2,1)} %bitcast.66, bf16[2,128,512]{2,1,0:T(8,128)(2,1)} %bitcast.61, ...), custom_call_target="tpu_custom_call" | custom-call | flops 1610612736 | bytes 9437184 | tf_op jit(solution)/shard_map/pallas_call | solution.py:132
  93.4 1.0 copy.12
  94.4 4.8 %collective-permute-start.8 = (f32[48,128]{1,0:T(8,128)S(1)}, f32[48,128]{1,0:T(8,128)S(1)}, u32[]{:S(2)}, u32[]{:S(2)}) collective-permute-start(f32[48,128]{1,0:T(8,128)S(1)} %bitcast.64), channel_id=1, source_target_pairs={{0,4},{1,5},{2,6},{3,7},{4,0},{5,1},{6,2},{7,3},{8,12},{9,13},{10,... | collective-permute-start | bytes 73736 | tf_op jit(solution)/shard_map/ppermute | solution.py:222
  99.2 3.8 %collective-permute-done.8 = f32[48,128]{1,0:T(8,128)S(1)} collective-permute-done((f32[48,128]{1,0:T(8,128)S(1)}, f32[48,128]{1,0:T(8,128)S(1)}, u32[]{:S(2)}, u32[]{:S(2)}) %collective-permute-start.8) | collective-permute-done | bytes 24608 | tf_op jit(solution)/shard_map/ppermute | solution.py:222
  103.0 2.5 %collective-permute-start.9 = (f32[96,128]{1,0:T(8,128)S(1)}, f32[96,128]{1,0:T(8,128)S(1)}, u32[]{:S(2)}, u32[]{:S(2)}) collective-permute-start(f32[96,128]{1,0:T(8,128)S(1)} %maximum_select_fusion.2), channel_id=1, source_target_pairs={{0,2},{1,3},{2,0},{3,1},{4,6},{5,7},{6,4},{7,5},{8,10},{9,11},{10,... | collective-permute-start | bytes 147464 | tf_op jit(solution)/shard_map/ppermute | solution.py:222
  105.5 1.3 slice_bitcast_fusion.3
  106.8 4.8 %collective-permute-start.4 = (bf16[128,1024]{1,0:T(8,128)(2,1)S(1)}, bf16[128,1024]{1,0:T(8,128)(2,1)S(1)}, u32[]{:S(2)}, u32[]{:S(2)}) collective-permute-start(bf16[128,1024]{1,0:T(8,128)(2,1)S(1)} %get-tuple-element.22), channel_id=1, source_target_pairs={{0,760},{8,0},{16,8},{24,16},{32,24},{40,32},{48,40},{56,48},{64,5... | collective-permute-start | bytes 786440 | tf_op jit(solution)/shard_map/ppermute | solution.py:21
  111.6 3.0 %collective-permute-start.5 = (bf16[128,1024]{1,0:T(8,128)(2,1)S(1)}, bf16[128,1024]{1,0:T(8,128)(2,1)S(1)}, u32[]{:S(2)}, u32[]{:S(2)}) collective-permute-start(bf16[128,1024]{1,0:T(8,128)(2,1)S(1)} %get-tuple-element.25), channel_id=1, source_target_pairs={{0,8},{8,16},{16,24},{24,32},{32,40},{40,48},{48,56},{56,64},{64,7... | collective-permute-start | bytes 786440 | tf_op jit(solution)/shard_map/ppermute | solution.py:21
  114.5 9.5 %collective-permute-start.6 = (bf16[128,1024]{1,0:T(8,128)(2,1)S(1)}, bf16[128,1024]{1,0:T(8,128)(2,1)S(1)}, u32[]{:S(2)}, u32[]{:S(2)}) collective-permute-start(bf16[128,1024]{1,0:T(8,128)(2,1)S(1)} %get-tuple-element.24), channel_id=1, source_target_pairs={{0,752},{8,760},{16,0},{24,8},{32,16},{40,24},{48,32},{56,40},{64,... | collective-permute-start | bytes 786440 | tf_op jit(solution)/shard_map/ppermute | solution.py:21
  124.1 1.9 %collective-permute-start.7 = (bf16[128,1024]{1,0:T(8,128)(2,1)S(1)}, bf16[128,1024]{1,0:T(8,128)(2,1)S(1)}, u32[]{:S(2)}, u32[]{:S(2)}) collective-permute-start(bf16[128,1024]{1,0:T(8,128)(2,1)S(1)} %get-tuple-element.23), channel_id=1, source_target_pairs={{0,16},{8,24},{16,32},{24,40},{32,48},{40,56},{48,64},{56,72},{64,... | collective-permute-start | bytes 786440 | tf_op jit(solution)/shard_map/ppermute | solution.py:21
  126.0 0.0 collective-permute-done.9
  126.0 5.1 %collective-permute-start.10 = (f32[192,128]{1,0:T(8,128)S(1)}, f32[192,128]{1,0:T(8,128)S(1)}, u32[]{:S(2)}, u32[]{:S(2)}) collective-permute-start(f32[192,128]{1,0:T(8,128)S(1)} %maximum_select_fusion.1), channel_id=1, source_target_pairs={{0,1},{1,0},{2,3},{3,2},{4,5},{5,4},{6,7},{7,6},{8,9},{9,8},{10,11... | collective-permute-start | bytes 294920 | tf_op jit(solution)/shard_map/ppermute | solution.py:222
  131.1 1.8 %convert_element_type.9 = bf16[2,128,512]{2,1,0:T(8,128)(2,1)} convert(f32[2,128,512]{2,1,0:T(8,128)} %get-tuple-element.13) | non-fusion elementwise | flops 131072 | bytes 786432 | tf_op jit(solution)/shard_map/convert_element_type | solution.py:281
  132.9 2.9 %collective-permute-done.10 = f32[192,128]{1,0:T(8,128)S(1)} collective-permute-done((f32[192,128]{1,0:T(8,128)S(1)}, f32[192,128]{1,0:T(8,128)S(1)}, u32[]{:S(2)}, u32[]{:S(2)}) %collective-permute-start.10) | collective-permute-done | bytes 98336 | tf_op jit(solution)/shard_map/ppermute | solution.py:222
  135.8 0.7 copy.13
  136.5 0.0 collective-permute-done.4
  136.5 0.9 gather_fusion.4
  137.4 0.0 collective-permute-done.5
  137.4 0.9 gather_fusion.5
  138.3 0.0 collective-permute-done.6
  138.3 0.9 gather_fusion.6
  139.1 0.0 collective-permute-done.7
  139.1 0.9 gather_fusion.7
  140.1 1.2 convert_reduce_fusion
  141.3 0.5 all-gather.5.cloned.1.call-done
  141.8 9.1 %shard_map.103 = (bf16[2,128,512]{2,1,0:T(8,128)(2,1)}, bf16[2,128,512]{2,1,0:T(8,128)(2,1)}) custom-call(s32[2]{0:T(128)} %count_ref.3, s32[2,6]{1,0:T(2,128)} %tiles_ref.3, bf16[16,128,1024]{2,1,0:T(8,128)(2,1)} %bitcast.52, f32[16,3,8,128]{3,2,1,0:T(8,128)} %bitcast.59, bf16[2,128,512]{2,1,0:T(8,128)(2,1)} %bitcast.56, bf16[2,128,512]{2,1,0:T(8,128)(2,1)} %bitcast.57, ...), custom_call_target="tpu_custom_call" | custom-call | flops 1610612736 | bytes 7536640 | tf_op jit(solution)/shard_map/pallas_call | solution.py:208
  (10 shorter events, 0.2 us)
Async XLA Ops:
  7.2 31.0 %copy-start.1 = (s32[2,256]{1,0:T(2,128)S(1)}, s32[2,256]{1,0:T(2,128)}, u32[]{:S(2)}) copy-start(s32[2,256]{1,0:T(2,128)} %param.11) | copy-start | bytes 6148
  7.2 70.7 %all-gather.3.cloned.1.call-start = ((), (), s32[]{:S(2)}) async-start(), calls=%async_computation | async-start | bytes 4718592 | tf_op jit(solution)/shard_map/all_gather | solution.py:241
  9.2 0.8 copy-start
  10.0 131.8 %all-gather.5.cloned.1.call-start = ((), (), s32[]{:S(2)}) async-start(), calls=%async_computation.1 | async-start | bytes 4718592 | tf_op jit(solution)/shard_map/all_gather | solution.py:242
  13.0 25.2 %collective-permute-start = (bf16[128,1024]{1,0:T(8,128)(2,1)S(1)}, bf16[128,1024]{1,0:T(8,128)(2,1)S(1)}, u32[]{:S(2)}, u32[]{:S(2)}) collective-permute-start(bf16[128,1024]{1,0:T(8,128)(2,1)S(1)} %get-tuple-element.26), channel_id=1, source_target_pairs={{0,760},{8,0},{16,8},{24,16},{32,24},{40,32},{48,40},{56,48},{64,5... | collective-permute-start | bytes 786440 | tf_op jit(solution)/shard_map/ppermute | solution.py:21
  25.5 15.2 %collective-permute-start.2 = (bf16[128,1024]{1,0:T(8,128)(2,1)S(1)}, bf16[128,1024]{1,0:T(8,128)(2,1)S(1)}, u32[]{:S(2)}, u32[]{:S(2)}) collective-permute-start(bf16[128,1024]{1,0:T(8,128)(2,1)S(1)} %get-tuple-element.26), channel_id=1, source_target_pairs={{0,752},{8,760},{16,0},{24,8},{32,16},{40,24},{48,32},{56,40},{64,... | collective-permute-start | bytes 786440 | tf_op jit(solution)/shard_map/ppermute | solution.py:21
  33.0 6.8 %collective-permute-start.1 = (bf16[128,1024]{1,0:T(8,128)(2,1)S(1)}, bf16[128,1024]{1,0:T(8,128)(2,1)S(1)}, u32[]{:S(2)}, u32[]{:S(2)}) collective-permute-start(bf16[128,1024]{1,0:T(8,128)(2,1)S(1)} %get-tuple-element.27), channel_id=1, source_target_pairs={{0,8},{8,16},{16,24},{24,32},{32,40},{40,48},{48,56},{56,64},{64,7... | collective-permute-start | bytes 786440 | tf_op jit(solution)/shard_map/ppermute | solution.py:21
  36.2 13.3 %collective-permute-start.3 = (bf16[128,1024]{1,0:T(8,128)(2,1)S(1)}, bf16[128,1024]{1,0:T(8,128)(2,1)S(1)}, u32[]{:S(2)}, u32[]{:S(2)}) collective-permute-start(bf16[128,1024]{1,0:T(8,128)(2,1)S(1)} %get-tuple-element.27), channel_id=1, source_target_pairs={{0,16},{8,24},{16,32},{24,40},{32,48},{40,56},{48,64},{56,72},{64,... | collective-permute-start | bytes 786440 | tf_op jit(solution)/shard_map/ppermute | solution.py:21
  94.4 8.6 %collective-permute-start.8 = (f32[48,128]{1,0:T(8,128)S(1)}, f32[48,128]{1,0:T(8,128)S(1)}, u32[]{:S(2)}, u32[]{:S(2)}) collective-permute-start(f32[48,128]{1,0:T(8,128)S(1)} %bitcast.64), channel_id=1, source_target_pairs={{0,4},{1,5},{2,6},{3,7},{4,0},{5,1},{6,2},{7,3},{8,12},{9,13},{10,... | collective-permute-start | bytes 73736 | tf_op jit(solution)/shard_map/ppermute | solution.py:222
  103.0 23.0 %collective-permute-start.9 = (f32[96,128]{1,0:T(8,128)S(1)}, f32[96,128]{1,0:T(8,128)S(1)}, u32[]{:S(2)}, u32[]{:S(2)}) collective-permute-start(f32[96,128]{1,0:T(8,128)S(1)} %maximum_select_fusion.2), channel_id=1, source_target_pairs={{0,2},{1,3},{2,0},{3,1},{4,6},{5,7},{6,4},{7,5},{8,10},{9,11},{10,... | collective-permute-start | bytes 147464 | tf_op jit(solution)/shard_map/ppermute | solution.py:222
  106.8 29.7 %collective-permute-start.4 = (bf16[128,1024]{1,0:T(8,128)(2,1)S(1)}, bf16[128,1024]{1,0:T(8,128)(2,1)S(1)}, u32[]{:S(2)}, u32[]{:S(2)}) collective-permute-start(bf16[128,1024]{1,0:T(8,128)(2,1)S(1)} %get-tuple-element.22), channel_id=1, source_target_pairs={{0,760},{8,0},{16,8},{24,16},{32,24},{40,32},{48,40},{56,48},{64,5... | collective-permute-start | bytes 786440 | tf_op jit(solution)/shard_map/ppermute | solution.py:21
  111.6 25.8 %collective-permute-start.5 = (bf16[128,1024]{1,0:T(8,128)(2,1)S(1)}, bf16[128,1024]{1,0:T(8,128)(2,1)S(1)}, u32[]{:S(2)}, u32[]{:S(2)}) collective-permute-start(bf16[128,1024]{1,0:T(8,128)(2,1)S(1)} %get-tuple-element.25), channel_id=1, source_target_pairs={{0,8},{8,16},{16,24},{24,32},{32,40},{40,48},{48,56},{56,64},{64,7... | collective-permute-start | bytes 786440 | tf_op jit(solution)/shard_map/ppermute | solution.py:21
  114.5 23.7 %collective-permute-start.6 = (bf16[128,1024]{1,0:T(8,128)(2,1)S(1)}, bf16[128,1024]{1,0:T(8,128)(2,1)S(1)}, u32[]{:S(2)}, u32[]{:S(2)}) collective-permute-start(bf16[128,1024]{1,0:T(8,128)(2,1)S(1)} %get-tuple-element.24), channel_id=1, source_target_pairs={{0,752},{8,760},{16,0},{24,8},{32,16},{40,24},{48,32},{56,40},{64,... | collective-permute-start | bytes 786440 | tf_op jit(solution)/shard_map/ppermute | solution.py:21
  124.1 15.1 %collective-permute-start.7 = (bf16[128,1024]{1,0:T(8,128)(2,1)S(1)}, bf16[128,1024]{1,0:T(8,128)(2,1)S(1)}, u32[]{:S(2)}, u32[]{:S(2)}) collective-permute-start(bf16[128,1024]{1,0:T(8,128)(2,1)S(1)} %get-tuple-element.23), channel_id=1, source_target_pairs={{0,16},{8,24},{16,32},{24,40},{32,48},{40,56},{48,64},{56,72},{64,... | collective-permute-start | bytes 786440 | tf_op jit(solution)/shard_map/ppermute | solution.py:21
  126.0 9.8 %collective-permute-start.10 = (f32[192,128]{1,0:T(8,128)S(1)}, f32[192,128]{1,0:T(8,128)S(1)}, u32[]{:S(2)}, u32[]{:S(2)}) collective-permute-start(f32[192,128]{1,0:T(8,128)S(1)} %maximum_select_fusion.1), channel_id=1, source_target_pairs={{0,1},{1,0},{2,3},{3,2},{4,5},{5,4},{6,7},{7,6},{8,9},{9,8},{10,11... | collective-permute-start | bytes 294920 | tf_op jit(solution)/shard_map/ppermute | solution.py:222
Sparse Core Ops, SparseCore 0:
  10.4 67.4 all-gather.2
  80.2 61.5 all-gather.4

commit v11 on v10

--- a/solution.py
+++ b/solution.py
@@ -183,7 +183,7 @@
         vs_ref[0, :, cols] = (v_sum + ret_ref[0, :, pl.ds(width + pr * pair, pair)]).astype(vs_ref.dtype)
 
 
-def key_side(tile_count, tiles, qg_blocks, st, k3, v3, returned, scale):
+def key_side(tile_count, tiles, qg_blocks, st, k3, v3, returned, scale, out_dtype=jnp.bfloat16):
     blocks, slots = tiles.shape
     keys = slots * BLOCK
     width = k3.shape[-1]
@@ -208,7 +208,7 @@
     return pl.pallas_call(
         functools.partial(key_side_kernel, scale=scale),
         grid_spec=grid_spec,
-        out_shape=[jax.ShapeDtypeStruct((blocks, BLOCK, width), jnp.bfloat16)] * 2,
+        out_shape=[jax.ShapeDtypeStruct((blocks, BLOCK, width), out_dtype)] * 2,
         cost_estimate=cost,
     )(tile_count, tiles, qg_blocks, st, k3, v3, returned)
 
@@ -263,18 +263,33 @@
         [fetch_partners(terms[step], partner[step], step + 1) for step in range(ROUNDS)]
     )
     returned = jnp.sum(returned.astype(f32), 0)
+
+    k3 = key.reshape(blocks_dev, BLOCK, width)
+    v3 = value.reshape(blocks_dev, BLOCK, width)
+    own = jnp.arange(blocks_dev, dtype=jnp.int32)[:, None]
+    k_own, v_own = key_side(
+        tile_count,
+        own,
+        jnp.concatenate([query, out_grad], 1).reshape(blocks_dev, BLOCK, 2 * width),
+        stats.reshape(blocks_dev, 3, HEADS, BLOCK),
+        k3,
+        v3,
+        jnp.zeros((blocks_dev, BLOCK, 2 * width), f32),
+        scale,
+        out_dtype=f32,
+    )
+    returned = returned.reshape(blocks_dev, BLOCK, 2 * width) + jnp.concatenate([k_own, v_own], 2)
     returned, stats_cluster, qg_cluster = lax.optimization_barrier(
         (returned, stats_cluster, qg_cluster)
     )
-
     key_grad, value_grad = key_side(
-        tile_count,
-        tiles,
+        tile_count - 1,
+        tiles[:, 1:],
         qg_cluster.reshape(cluster_blocks, BLOCK, 2 * width),
         stats_cluster.reshape(cluster_blocks, 3, HEADS, BLOCK),
-        key.reshape(blocks_dev, BLOCK, width),
-        value.reshape(blocks_dev, BLOCK, width),
-        returned.reshape(blocks_dev, BLOCK, 2 * width),
+        k3,
+        v3,
+        returned,
         scale,
     )
 

time: 158 us -> 164 us (1.038)
  Pallas kernels: 24.7 us -> 30.6 us
  local copies, waits for them, and re-layouts: 13.6 us -> 18.7 us
  waiting for transfers between devices: 42.2 us -> 37.9 us
    pallas_call x1 -> x2, Pallas kernels: 9.15 us -> 14.9 us  [key_side(): pl.pallas_call(functools.partial(key_side_kernel, scale=scale), grid_spec...]
    ppermute x3, waiting for transfers between devices: 6.71 us -> 3.81 us  [doubling_gather(): other = lax.ppermute(x, axis, [(i, i ^ step) for i in range(size)])]
    concatenate x1 -> x0, other arithmetic: 1.88 us -> none  [shards(): jnp.concatenate([query, out_grad], 1)]
    unnamed x5 -> x18, local copies, waits for them, and re-layouts: 1.77 us -> 3.58 us
  transfers between devices with their start and end apart: 13 -> 13, of which waited for: 6 -> 4; matrix products, arithmetic and copies ran while one was open for 11% -> 12% of each run, Pallas kernels for 10% -> 13%
where the time goes in v11:
time: 164 us; the launch traced here: 163 us
  starting transfers between devices  56.8 us (35%)
  waiting for transfers between devices  37.9 us (23%)
  Pallas kernels  30.6 us (19%)
  local copies, waits for them, and re-layouts  18.7 us (11%)
  between operations  14.4 us (9%)
  other arithmetic  4.98 us (3%)
    ppermute x8, starting transfers between devices, passed_along(): return lax.ppermute(x, axis, [(i, (i + by) % size) for i in range(size)])  44.3 us
    all_gather x1, waiting for transfers between devices, shards(): kv_cluster = lax.all_gather(both, 'blk', axis=0, tiled=True)  25.3 us
    pallas_call x1, Pallas kernels, query_side(): pl.pallas_call(functools.partial(query_side_kernel, scale=scale), grid_sp...  15.7 us
    pallas_call x2, Pallas kernels, key_side(): pl.pallas_call(functools.partial(key_side_kernel, scale=scale), grid_spec...  14.9 us
    ppermute x3, starting transfers between devices, doubling_gather(): other = lax.ppermute(x, axis, [(i, i ^ step) for i in range(size)])  12.4 us
    ppermute x8, waiting for transfers between devices, passed_along(): return lax.ppermute(x, axis, [(i, (i + by) % size) for i in range(size)])  8.7 us
    gather x8, local copies, waits for them, and re-layouts, fetch_partners(): return jnp.concatenate([ahead[slots[:half]], behind[slots[half:]]], 0)  6.89 us
    ppermute x3, waiting for transfers between devices, doubling_gather(): other = lax.ppermute(x, axis, [(i, i ^ step) for i in range(size)])  3.81 us
  transfers between devices with their start and end apart: 13, of which 4 were waited for; matrix products, arithmetic and copies ran while one was open for 12% of the time, Pallas kernels for 13%

profile of v11, /device:TPU:1, one launch (start us, length us, event | category | flops | bytes accessed | tf_op | source)
XLA Modules:
  0.0 163.3 jit_solution(11145197785167162398)
XLA Ops:
  7.2 0.0 copy-start.5
  7.2 0.0 all-gather.3.cloned.1.call-start
  7.2 1.0 constant_dynamic-update-slice_fusion.1
  8.2 1.0 constant_dynamic-update-slice_fusion
  9.2 0.0 copy-start
  9.2 0.8 copy-done
  10.0 0.0 all-gather.3.cloned.1.call-update
  10.0 0.0 all-gather.5.cloned.1.call-start
  10.1 1.0 constant_dynamic-update-slice_fusion.3
  11.0 1.0 constant_dynamic-update-slice_fusion.2
  12.0 0.0 copy-start.1
  12.0 0.8 copy-done.1
  12.9 0.0 all-gather.5.cloned.1.call-update
  12.9 1.1 fusion.4
  13.9 12.4 %collective-permute-start = (bf16[128,1024]{1,0:T(8,128)(2,1)S(1)}, bf16[128,1024]{1,0:T(8,128)(2,1)S(1)}, u32[]{:S(2)}, u32[]{:S(2)}) collective-permute-start(bf16[128,1024]{1,0:T(8,128)(2,1)S(1)} %get-tuple-element.30), channel_id=1, source_target_pairs={{0,760},{8,0},{16,8},{24,16},{32,24},{40,32},{48,40},{56,48},{64,5... | collective-permute-start | bytes 786440 | tf_op jit(solution)/shard_map/ppermute | solution.py:21
  26.4 7.5 %collective-permute-start.2 = (bf16[128,1024]{1,0:T(8,128)(2,1)S(1)}, bf16[128,1024]{1,0:T(8,128)(2,1)S(1)}, u32[]{:S(2)}, u32[]{:S(2)}) collective-permute-start(bf16[128,1024]{1,0:T(8,128)(2,1)S(1)} %get-tuple-element.30), channel_id=1, source_target_pairs={{0,752},{8,760},{16,0},{24,8},{32,16},{40,24},{48,32},{56,40},{64,... | collective-permute-start | bytes 786440 | tf_op jit(solution)/shard_map/ppermute | solution.py:21
  33.9 3.3 %collective-permute-start.1 = (bf16[128,1024]{1,0:T(8,128)(2,1)S(1)}, bf16[128,1024]{1,0:T(8,128)(2,1)S(1)}, u32[]{:S(2)}, u32[]{:S(2)}) collective-permute-start(bf16[128,1024]{1,0:T(8,128)(2,1)S(1)} %get-tuple-element.31), channel_id=1, source_target_pairs={{0,8},{8,16},{16,24},{24,32},{32,40},{40,48},{48,56},{56,64},{64,7... | collective-permute-start | bytes 786440 | tf_op jit(solution)/shard_map/ppermute | solution.py:21
  37.1 1.9 %collective-permute-start.3 = (bf16[128,1024]{1,0:T(8,128)(2,1)S(1)}, bf16[128,1024]{1,0:T(8,128)(2,1)S(1)}, u32[]{:S(2)}, u32[]{:S(2)}) collective-permute-start(bf16[128,1024]{1,0:T(8,128)(2,1)S(1)} %get-tuple-element.31), channel_id=1, source_target_pairs={{0,16},{8,24},{16,32},{24,40},{32,48},{40,56},{48,64},{56,72},{64,... | collective-permute-start | bytes 786440 | tf_op jit(solution)/shard_map/ppermute | solution.py:21
  39.1 0.0 copy-done.5
  39.1 0.0 collective-permute-done
  39.1 0.9 gather_fusion
  40.0 0.7 collective-permute-done.1
  40.7 0.9 gather_fusion.1
  41.5 0.0 collective-permute-done.2
  41.5 0.9 gather_fusion.2
  42.4 8.0 %collective-permute-done.3 = bf16[128,1024]{1,0:T(8,128)(2,1)S(1)} collective-permute-done((bf16[128,1024]{1,0:T(8,128)(2,1)S(1)}, bf16[128,1024]{1,0:T(8,128)(2,1)S(1)}, u32[]{:S(2)}, u32[]{:S(2)}) %collective-permute-start.3) | collective-permute-done | bytes 262176 | tf_op jit(solution)/shard_map/ppermute | solution.py:21
  50.4 0.9 gather_fusion.3
  51.4 1.1 pad_maximum_fusion.pair_ref
  52.5 25.3 %all-gather.3.cloned.1.call-done = bf16[2048,1024]{1,0:T(8,128)(2,1)} async-done(((bf16[256,1024]{1,0:T(8,128)(2,1)}), bf16[2048,1024]{1,0:T(8,128)(2,1)}) %all-gather.3.cloned.1.call-update) | async-done | bytes 4194320 | tf_op jit(solution)/shard_map/all_gather | solution.py:241
  77.8 15.7 %shard_map.102 = (f32[2,128,512]{2,1,0:T(8,128)}, bf16[2,128,512]{2,1,0:T(8,128)(2,1)}, bf16[2,2,128,1024]{3,2,1,0:T(8,128)(2,1)}, f32[2,128,128]{2,1,0:T(8,128)}) custom-call(s32[2]{0:T(128)} %count_ref.3, s32[2,6]{1,0:T(2,128)} %tiles_ref.1, bf16[16,128,1024]{2,1,0:T(8,128)(2,1)} %bitcast.71, bf16[2,128,512]{2,1,0:T(8,128)(2,1)} %bitcast.65, ...), custom_call_target="tpu_custom_call" | custom-call | flops 1610612736 | bytes 9437184 | tf_op jit(solution)/shard_map/pallas_call | solution.py:132
  93.5 1.0 copy.11
  94.5 4.8 %collective-permute-start.8 = (f32[48,128]{1,0:T(8,128)S(1)}, f32[48,128]{1,0:T(8,128)S(1)}, u32[]{:S(2)}, u32[]{:S(2)}) collective-permute-start(f32[48,128]{1,0:T(8,128)S(1)} %bitcast.67), channel_id=1, source_target_pairs={{0,4},{1,5},{2,6},{3,7},{4,0},{5,1},{6,2},{7,3},{8,12},{9,13},{10,... | collective-permute-start | bytes 73736 | tf_op jit(solution)/shard_map/ppermute | solution.py:222
  99.4 3.8 %collective-permute-done.8 = f32[48,128]{1,0:T(8,128)S(1)} collective-permute-done((f32[48,128]{1,0:T(8,128)S(1)}, f32[48,128]{1,0:T(8,128)S(1)}, u32[]{:S(2)}, u32[]{:S(2)}) %collective-permute-start.8) | collective-permute-done | bytes 24608 | tf_op jit(solution)/shard_map/ppermute | solution.py:222
  103.2 2.5 %collective-permute-start.9 = (f32[96,128]{1,0:T(8,128)S(1)}, f32[96,128]{1,0:T(8,128)S(1)}, u32[]{:S(2)}, u32[]{:S(2)}) collective-permute-start(f32[96,128]{1,0:T(8,128)S(1)} %maximum_select_fusion.2), channel_id=1, source_target_pairs={{0,2},{1,3},{2,0},{3,1},{4,6},{5,7},{6,4},{7,5},{8,10},{9,11},{10,... | collective-permute-start | bytes 147464 | tf_op jit(solution)/shard_map/ppermute | solution.py:222
  105.7 1.3 slice_bitcast_fusion.3
  106.9 4.8 %collective-permute-start.4 = (bf16[128,1024]{1,0:T(8,128)(2,1)S(1)}, bf16[128,1024]{1,0:T(8,128)(2,1)S(1)}, u32[]{:S(2)}, u32[]{:S(2)}) collective-permute-start(bf16[128,1024]{1,0:T(8,128)(2,1)S(1)} %get-tuple-element.26), channel_id=1, source_target_pairs={{0,760},{8,0},{16,8},{24,16},{32,24},{40,32},{48,40},{56,48},{64,5... | collective-permute-start | bytes 786440 | tf_op jit(solution)/shard_map/ppermute | solution.py:21
  111.7 3.0 %collective-permute-start.5 = (bf16[128,1024]{1,0:T(8,128)(2,1)S(1)}, bf16[128,1024]{1,0:T(8,128)(2,1)S(1)}, u32[]{:S(2)}, u32[]{:S(2)}) collective-permute-start(bf16[128,1024]{1,0:T(8,128)(2,1)S(1)} %get-tuple-element.29), channel_id=1, source_target_pairs={{0,8},{8,16},{16,24},{24,32},{32,40},{40,48},{48,56},{56,64},{64,7... | collective-permute-start | bytes 786440 | tf_op jit(solution)/shard_map/ppermute | solution.py:21
  114.7 9.5 %collective-permute-start.6 = (bf16[128,1024]{1,0:T(8,128)(2,1)S(1)}, bf16[128,1024]{1,0:T(8,128)(2,1)S(1)}, u32[]{:S(2)}, u32[]{:S(2)}) collective-permute-start(bf16[128,1024]{1,0:T(8,128)(2,1)S(1)} %get-tuple-element.28), channel_id=1, source_target_pairs={{0,752},{8,760},{16,0},{24,8},{32,16},{40,24},{48,32},{56,40},{64,... | collective-permute-start | bytes 786440 | tf_op jit(solution)/shard_map/ppermute | solution.py:21
  124.2 1.9 %collective-permute-start.7 = (bf16[128,1024]{1,0:T(8,128)(2,1)S(1)}, bf16[128,1024]{1,0:T(8,128)(2,1)S(1)}, u32[]{:S(2)}, u32[]{:S(2)}) collective-permute-start(bf16[128,1024]{1,0:T(8,128)(2,1)S(1)} %get-tuple-element.27), channel_id=1, source_target_pairs={{0,16},{8,24},{16,32},{24,40},{32,48},{40,56},{48,64},{56,72},{64,... | collective-permute-start | bytes 786440 | tf_op jit(solution)/shard_map/ppermute | solution.py:21
  126.1 0.0 collective-permute-done.9
  126.2 5.1 %collective-permute-start.10 = (f32[192,128]{1,0:T(8,128)S(1)}, f32[192,128]{1,0:T(8,128)S(1)}, u32[]{:S(2)}, u32[]{:S(2)}) collective-permute-start(f32[192,128]{1,0:T(8,128)S(1)} %maximum_select_fusion.1), channel_id=1, source_target_pairs={{0,1},{1,0},{2,3},{3,2},{4,5},{5,4},{6,7},{7,6},{8,9},{9,8},{10,11... | collective-permute-start | bytes 294920 | tf_op jit(solution)/shard_map/ppermute | solution.py:222
  131.3 0.0 copy-done.7
  131.3 0.5 broadcast_add_fusion.count_ref
  131.8 0.0 copy-done.6
  131.8 0.6 slice.92.tiles_ref
  132.4 1.8 %convert_element_type.9 = bf16[2,128,512]{2,1,0:T(8,128)(2,1)} convert(f32[2,128,512]{2,1,0:T(8,128)} %get-tuple-element.15) | non-fusion elementwise | flops 131072 | bytes 786432 | tf_op jit(solution)/shard_map/convert_element_type | solution.py:296
  134.2 0.6 iota.4.tiles_ref
  134.7 1.1 broadcast_in_dim.2.ret_ref
  135.9 0.0 copy-done.4
  135.9 6.0 %shard_map.103 = (f32[2,128,512]{2,1,0:T(8,128)}, f32[2,128,512]{2,1,0:T(8,128)}) custom-call(s32[2]{0:T(128)} %count_ref.3, s32[2,1]{1,0:T(2,128)} %iota.4.tiles_ref, bf16[2,128,1024]{2,1,0:T(8,128)(2,1)} %bitcast.55, f32[2,3,8,128]{3,2,1,0:T(8,128)} %bitcast.69, bf16[2,128,512]{2,1,0:T(8,128)(2,1)} %bitcast.56, bf16[2,128,512]{2,1,0:T(8,128)(2,1)} %bitcast.58, ...), custom_call_target="tpu_custom_call" | custom-call | flops 268435456 | bytes 3694592 | tf_op jit(solution)/shard_map/pallas_call | solution.py:208
  141.9 0.0 collective-permute-done.10
  141.9 0.7 copy.12
  142.6 0.0 collective-permute-done.4
  142.6 0.9 gather_fusion.4
  143.5 0.0 collective-permute-done.5
  143.5 0.9 gather_fusion.5
  144.3 0.0 copy-start.3
  144.4 0.0 collective-permute-done.6
  144.4 0.9 gather_fusion.6
  145.2 0.0 collective-permute-done.7
  145.2 0.9 gather_fusion.7
  146.2 0.2 convert_reduce_fusion
  146.4 1.2 maximum_add_fusion.ret_ref
  147.6 8.9 %shard_map.104 = (bf16[2,128,512]{2,1,0:T(8,128)(2,1)}, bf16[2,128,512]{2,1,0:T(8,128)(2,1)}) custom-call(s32[2]{0:T(128)} %broadcast_add_fusion.count_ref, s32[2,5]{1,0:T(2,128)} %slice.92.tiles_ref, bf16[16,128,1024]{2,1,0:T(8,128)(2,1)} %bitcast.54, f32[16,3,8,128]{3,2,1,0:T(8,128)} %bitcast.63, bf16[2,128,512]{2,1,0:T(8,128)(2,1)} %bitcast.57, ...), custom_call_target="tpu_custom_call" | custom-call | flops 1342177280 | bytes 7536640 | tf_op jit(solution)/shard_map/pallas_call | solution.py:208
  (17 shorter events, 0.2 us)
Async XLA Ops:
  7.2 31.9 %copy-start.5 = (s32[2,256]{1,0:T(2,128)S(1)}, s32[2,256]{1,0:T(2,128)}, u32[]{:S(2)}) copy-start(s32[2,256]{1,0:T(2,128)} %param.11) | copy-start | bytes 6148
  7.2 70.7 %all-gather.3.cloned.1.call-start = ((), (), s32[]{:S(2)}) async-start(), calls=%async_computation | async-start | bytes 4718592 | tf_op jit(solution)/shard_map/all_gather | solution.py:241
  9.2 0.8 copy-start
  10.0 137.6 %all-gather.5.cloned.1.call-start = ((), (), s32[]{:S(2)}) async-start(), calls=%async_computation.1 | async-start | bytes 4718592 | tf_op jit(solution)/shard_map/all_gather | solution.py:242
  12.0 0.8 copy-start.1
  13.9 25.2 %collective-permute-start = (bf16[128,1024]{1,0:T(8,128)(2,1)S(1)}, bf16[128,1024]{1,0:T(8,128)(2,1)S(1)}, u32[]{:S(2)}, u32[]{:S(2)}) collective-permute-start(bf16[128,1024]{1,0:T(8,128)(2,1)S(1)} %get-tuple-element.30), channel_id=1, source_target_pairs={{0,760},{8,0},{16,8},{24,16},{32,24},{40,32},{48,40},{56,48},{64,5... | collective-permute-start | bytes 786440 | tf_op jit(solution)/shard_map/ppermute | solution.py:21
  26.4 15.2 %collective-permute-start.2 = (bf16[128,1024]{1,0:T(8,128)(2,1)S(1)}, bf16[128,1024]{1,0:T(8,128)(2,1)S(1)}, u32[]{:S(2)}, u32[]{:S(2)}) collective-permute-start(bf16[128,1024]{1,0:T(8,128)(2,1)S(1)} %get-tuple-element.30), channel_id=1, source_target_pairs={{0,752},{8,760},{16,0},{24,8},{32,16},{40,24},{48,32},{56,40},{64,... | collective-permute-start | bytes 786440 | tf_op jit(solution)/shard_map/ppermute | solution.py:21
  33.9 6.8 %collective-permute-start.1 = (bf16[128,1024]{1,0:T(8,128)(2,1)S(1)}, bf16[128,1024]{1,0:T(8,128)(2,1)S(1)}, u32[]{:S(2)}, u32[]{:S(2)}) collective-permute-start(bf16[128,1024]{1,0:T(8,128)(2,1)S(1)} %get-tuple-element.31), channel_id=1, source_target_pairs={{0,8},{8,16},{16,24},{24,32},{32,40},{40,48},{48,56},{56,64},{64,7... | collective-permute-start | bytes 786440 | tf_op jit(solution)/shard_map/ppermute | solution.py:21
  37.1 13.3 %collective-permute-start.3 = (bf16[128,1024]{1,0:T(8,128)(2,1)S(1)}, bf16[128,1024]{1,0:T(8,128)(2,1)S(1)}, u32[]{:S(2)}, u32[]{:S(2)}) collective-permute-start(bf16[128,1024]{1,0:T(8,128)(2,1)S(1)} %get-tuple-element.31), channel_id=1, source_target_pairs={{0,16},{8,24},{16,32},{24,40},{32,48},{40,56},{48,64},{56,72},{64,... | collective-permute-start | bytes 786440 | tf_op jit(solution)/shard_map/ppermute | solution.py:21
  77.8 53.4 %copy-start.7 = (s32[2]{0:T(128)S(1)}, s32[2]{0:T(128)}, u32[]{:S(2)}) copy-start(s32[2]{0:T(128)} %count_ref.3) | copy-start | bytes 28
  77.8 53.9 %copy-start.6 = (s32[2,6]{1,0:T(2,128)S(1)}, s32[2,6]{1,0:T(2,128)}, u32[]{:S(2)}) copy-start(s32[2,6]{1,0:T(2,128)} %tiles_ref.1) | copy-start | bytes 148
  94.5 41.4 %copy-start.4 = (f32[2,128,24]{1,2,0:T(8,128)}, f32[2,128,24]{1,2,0:T(8,128)S(1)}, u32[]{:S(2)}) copy-start(f32[2,128,24]{1,2,0:T(8,128)S(1)} %copy.11) | copy-start | bytes 73732
  94.5 8.7 %collective-permute-start.8 = (f32[48,128]{1,0:T(8,128)S(1)}, f32[48,128]{1,0:T(8,128)S(1)}, u32[]{:S(2)}, u32[]{:S(2)}) collective-permute-start(f32[48,128]{1,0:T(8,128)S(1)} %bitcast.67), channel_id=1, source_target_pairs={{0,4},{1,5},{2,6},{3,7},{4,0},{5,1},{6,2},{7,3},{8,12},{9,13},{10,... | collective-permute-start | bytes 73736 | tf_op jit(solution)/shard_map/ppermute | solution.py:222
  103.2 23.0 %collective-permute-start.9 = (f32[96,128]{1,0:T(8,128)S(1)}, f32[96,128]{1,0:T(8,128)S(1)}, u32[]{:S(2)}, u32[]{:S(2)}) collective-permute-start(f32[96,128]{1,0:T(8,128)S(1)} %maximum_select_fusion.2), channel_id=1, source_target_pairs={{0,2},{1,3},{2,0},{3,1},{4,6},{5,7},{6,4},{7,5},{8,10},{9,11},{10,... | collective-permute-start | bytes 147464 | tf_op jit(solution)/shard_map/ppermute | solution.py:222
  106.9 35.7 %collective-permute-start.4 = (bf16[128,1024]{1,0:T(8,128)(2,1)S(1)}, bf16[128,1024]{1,0:T(8,128)(2,1)S(1)}, u32[]{:S(2)}, u32[]{:S(2)}) collective-permute-start(bf16[128,1024]{1,0:T(8,128)(2,1)S(1)} %get-tuple-element.26), channel_id=1, source_target_pairs={{0,760},{8,0},{16,8},{24,16},{32,24},{40,32},{48,40},{56,48},{64,5... | collective-permute-start | bytes 786440 | tf_op jit(solution)/shard_map/ppermute | solution.py:21
  111.7 31.7 %collective-permute-start.5 = (bf16[128,1024]{1,0:T(8,128)(2,1)S(1)}, bf16[128,1024]{1,0:T(8,128)(2,1)S(1)}, u32[]{:S(2)}, u32[]{:S(2)}) collective-permute-start(bf16[128,1024]{1,0:T(8,128)(2,1)S(1)} %get-tuple-element.29), channel_id=1, source_target_pairs={{0,8},{8,16},{16,24},{24,32},{32,40},{40,48},{48,56},{56,64},{64,7... | collective-permute-start | bytes 786440 | tf_op jit(solution)/shard_map/ppermute | solution.py:21
  114.7 29.6 %collective-permute-start.6 = (bf16[128,1024]{1,0:T(8,128)(2,1)S(1)}, bf16[128,1024]{1,0:T(8,128)(2,1)S(1)}, u32[]{:S(2)}, u32[]{:S(2)}) collective-permute-start(bf16[128,1024]{1,0:T(8,128)(2,1)S(1)} %get-tuple-element.28), channel_id=1, source_target_pairs={{0,752},{8,760},{16,0},{24,8},{32,16},{40,24},{48,32},{56,40},{64,... | collective-permute-start | bytes 786440 | tf_op jit(solution)/shard_map/ppermute | solution.py:21
  124.2 21.0 %collective-permute-start.7 = (bf16[128,1024]{1,0:T(8,128)(2,1)S(1)}, bf16[128,1024]{1,0:T(8,128)(2,1)S(1)}, u32[]{:S(2)}, u32[]{:S(2)}) collective-permute-start(bf16[128,1024]{1,0:T(8,128)(2,1)S(1)} %get-tuple-element.27), channel_id=1, source_target_pairs={{0,16},{8,24},{16,32},{24,40},{32,48},{40,56},{48,64},{56,72},{64,... | collective-permute-start | bytes 786440 | tf_op jit(solution)/shard_map/ppermute | solution.py:21
  126.2 15.7 %collective-permute-start.10 = (f32[192,128]{1,0:T(8,128)S(1)}, f32[192,128]{1,0:T(8,128)S(1)}, u32[]{:S(2)}, u32[]{:S(2)}) collective-permute-start(f32[192,128]{1,0:T(8,128)S(1)} %maximum_select_fusion.1), channel_id=1, source_target_pairs={{0,1},{1,0},{2,3},{3,2},{4,5},{5,4},{6,7},{7,6},{8,9},{9,8},{10,11... | collective-permute-start | bytes 294920 | tf_op jit(solution)/shard_map/ppermute | solution.py:222
  144.3 2.1 %copy-start.2 = (f32[2,128,512]{2,1,0:T(8,128)S(1)}, f32[2,128,512]{2,1,0:T(8,128)}, u32[]{:S(2)}) copy-start(f32[2,128,512]{2,1,0:T(8,128)} %get-tuple-element.19) | copy-start | bytes 1572868
  144.3 2.1 %copy-start.3 = (f32[2,128,512]{2,1,0:T(8,128)S(1)}, f32[2,128,512]{2,1,0:T(8,128)}, u32[]{:S(2)}) copy-start(f32[2,128,512]{2,1,0:T(8,128)} %get-tuple-element.20) | copy-start | bytes 1572868
Sparse Core Ops, SparseCore 0:
  10.4 67.4 all-gather.2
  80.2 61.5 all-gather.4

commit v12 on v10

--- a/solution.py
+++ b/solution.py
@@ -172,7 +172,7 @@
             top, total, delta = [
                 jnp.concatenate([st_ref[i, j, pl.ds(h, 1), :] for i in ids], 1) for j in range(3)
             ]
-            p = jnp.where(live, jnp.exp(s - top) / total, 0.0)
+            p = jnp.where(live, jnp.exp(s - top) * (1.0 / total), 0.0)
             w = p.astype(jnp.bfloat16)
             z = (p * (d - delta)).astype(jnp.bfloat16)
             k_out.append(jnp.dot(z, qp, preferred_element_type=jnp.float32))

time: 158 us -> 158 us (level)
  no operation moved by 1% of the time
where the time goes in v12:
time: 158 us
  starting transfers between devices  56.7 us (36%)
  waiting for transfers between devices  42.2 us (27%)
  Pallas kernels  24.8 us (16%)
  between operations  14.3 us (9%)
  local copies, waits for them, and re-layouts  13.6 us (9%)
  other arithmetic  6.19 us (4%)
    ppermute x8, starting transfers between devices, passed_along(): return lax.ppermute(x, axis, [(i, (i + by) % size) for i in range(size)])  44.3 us
    all_gather x1, waiting for transfers between devices, shards(): kv_cluster = lax.all_gather(both, 'blk', axis=0, tiled=True)  26.2 us
    pallas_call x1, Pallas kernels, query_side(): pl.pallas_call(functools.partial(query_side_kernel, scale=scale), grid_sp...  15.6 us
    ppermute x3, starting transfers between devices, doubling_gather(): other = lax.ppermute(x, axis, [(i, i ^ step) for i in range(size)])  12.4 us
    pallas_call x1, Pallas kernels, key_side(): pl.pallas_call(functools.partial(key_side_kernel, scale=scale), grid_spec...  9.19 us
    ppermute x8, waiting for transfers between devices, passed_along(): return lax.ppermute(x, axis, [(i, (i + by) % size) for i in range(size)])  8.7 us
    gather x8, local copies, waits for them, and re-layouts, fetch_partners(): return jnp.concatenate([ahead[slots[:half]], behind[slots[half:]]], 0)  6.89 us
    ppermute x3, waiting for transfers between devices, doubling_gather(): other = lax.ppermute(x, axis, [(i, i ^ step) for i in range(size)])  6.71 us
  transfers between devices with their start and end apart: 13, of which 6 were waited for; matrix products, arithmetic and copies ran while one was open for 11% of the time, Pallas kernels for 10%

profile of v12, /device:TPU:1, one launch (start us, length us, event | category | flops | bytes accessed | tf_op | source)
XLA Modules:
  0.0 157.9 jit_solution(4464021054412452518)
XLA Ops:
  7.2 0.0 copy-start.1
  7.2 0.0 all-gather.3.cloned.1.call-start
  7.2 1.0 constant_dynamic-update-slice_fusion.1
  8.2 1.0 constant_dynamic-update-slice_fusion
  9.2 0.0 copy-start
  9.2 0.8 copy-done
  10.0 0.0 all-gather.3.cloned.1.call-update
  10.0 0.0 all-gather.5.cloned.1.call-start
  10.1 1.9 %pad_maximum_fusion.3 = bf16[256,1024]{1,0:T(8,128)(2,1)} fusion(bf16[256,512]{1,0:T(8,128)(2,1)} %param.10, bf16[256,512]{1,0:T(8,128)(2,1)} %param.7), kind=kLoop, calls=%fused_computation.14 | loop fusion | flops 1048576 | bytes 1048576 | tf_op jit(solution)/shard_map/concatenate | solution.py:242
  11.9 0.0 all-gather.5.cloned.1.call-update
  12.0 1.1 fusion.4
  13.0 12.4 %collective-permute-start = (bf16[128,1024]{1,0:T(8,128)(2,1)S(1)}, bf16[128,1024]{1,0:T(8,128)(2,1)S(1)}, u32[]{:S(2)}, u32[]{:S(2)}) collective-permute-start(bf16[128,1024]{1,0:T(8,128)(2,1)S(1)} %get-tuple-element.26), channel_id=1, source_target_pairs={{0,760},{8,0},{16,8},{24,16},{32,24},{40,32},{48,40},{56,48},{64,5... | collective-permute-start | bytes 786440 | tf_op jit(solution)/shard_map/ppermute | solution.py:21
  25.5 7.5 %collective-permute-start.2 = (bf16[128,1024]{1,0:T(8,128)(2,1)S(1)}, bf16[128,1024]{1,0:T(8,128)(2,1)S(1)}, u32[]{:S(2)}, u32[]{:S(2)}) collective-permute-start(bf16[128,1024]{1,0:T(8,128)(2,1)S(1)} %get-tuple-element.26), channel_id=1, source_target_pairs={{0,752},{8,760},{16,0},{24,8},{32,16},{40,24},{48,32},{56,40},{64,... | collective-permute-start | bytes 786440 | tf_op jit(solution)/shard_map/ppermute | solution.py:21
  33.0 3.3 %collective-permute-start.1 = (bf16[128,1024]{1,0:T(8,128)(2,1)S(1)}, bf16[128,1024]{1,0:T(8,128)(2,1)S(1)}, u32[]{:S(2)}, u32[]{:S(2)}) collective-permute-start(bf16[128,1024]{1,0:T(8,128)(2,1)S(1)} %get-tuple-element.27), channel_id=1, source_target_pairs={{0,8},{8,16},{16,24},{24,32},{32,40},{40,48},{48,56},{56,64},{64,7... | collective-permute-start | bytes 786440 | tf_op jit(solution)/shard_map/ppermute | solution.py:21
  36.2 1.9 %collective-permute-start.3 = (bf16[128,1024]{1,0:T(8,128)(2,1)S(1)}, bf16[128,1024]{1,0:T(8,128)(2,1)S(1)}, u32[]{:S(2)}, u32[]{:S(2)}) collective-permute-start(bf16[128,1024]{1,0:T(8,128)(2,1)S(1)} %get-tuple-element.27), channel_id=1, source_target_pairs={{0,16},{8,24},{16,32},{24,40},{32,48},{40,56},{48,64},{56,72},{64,... | collective-permute-start | bytes 786440 | tf_op jit(solution)/shard_map/ppermute | solution.py:21
  38.2 0.0 copy-done.1
  38.2 0.0 collective-permute-done
  38.2 0.9 gather_fusion
  39.1 0.7 collective-permute-done.1
  39.8 0.9 gather_fusion.1
  40.6 0.0 collective-permute-done.2
  40.6 0.9 gather_fusion.2
  41.5 8.0 %collective-permute-done.3 = bf16[128,1024]{1,0:T(8,128)(2,1)S(1)} collective-permute-done((bf16[128,1024]{1,0:T(8,128)(2,1)S(1)}, bf16[128,1024]{1,0:T(8,128)(2,1)S(1)}, u32[]{:S(2)}, u32[]{:S(2)}) %collective-permute-start.3) | collective-permute-done | bytes 262176 | tf_op jit(solution)/shard_map/ppermute | solution.py:21
  49.5 0.9 gather_fusion.3
  50.5 1.1 pad_maximum_fusion.pair_ref
  51.6 26.2 %all-gather.3.cloned.1.call-done = bf16[2048,1024]{1,0:T(8,128)(2,1)} async-done(((bf16[256,1024]{1,0:T(8,128)(2,1)}), bf16[2048,1024]{1,0:T(8,128)(2,1)}) %all-gather.3.cloned.1.call-update) | async-done | bytes 4194320 | tf_op jit(solution)/shard_map/all_gather | solution.py:241
  77.8 15.6 %shard_map.102 = (f32[2,128,512]{2,1,0:T(8,128)}, bf16[2,128,512]{2,1,0:T(8,128)(2,1)}, bf16[2,2,128,1024]{3,2,1,0:T(8,128)(2,1)}, f32[2,128,128]{2,1,0:T(8,128)}) custom-call(s32[2]{0:T(128)} %count_ref.3, s32[2,6]{1,0:T(2,128)} %tiles_ref.3, bf16[16,128,1024]{2,1,0:T(8,128)(2,1)} %bitcast.66, bf16[2,128,512]{2,1,0:T(8,128)(2,1)} %bitcast.61, ...), custom_call_target="tpu_custom_call" | custom-call | flops 1610612736 | bytes 9437184 | tf_op jit(solution)/shard_map/pallas_call | solution.py:132
  93.4 1.0 copy.12
  94.4 4.8 %collective-permute-start.8 = (f32[48,128]{1,0:T(8,128)S(1)}, f32[48,128]{1,0:T(8,128)S(1)}, u32[]{:S(2)}, u32[]{:S(2)}) collective-permute-start(f32[48,128]{1,0:T(8,128)S(1)} %bitcast.64), channel_id=1, source_target_pairs={{0,4},{1,5},{2,6},{3,7},{4,0},{5,1},{6,2},{7,3},{8,12},{9,13},{10,... | collective-permute-start | bytes 73736 | tf_op jit(solution)/shard_map/ppermute | solution.py:222
  99.2 3.8 %collective-permute-done.8 = f32[48,128]{1,0:T(8,128)S(1)} collective-permute-done((f32[48,128]{1,0:T(8,128)S(1)}, f32[48,128]{1,0:T(8,128)S(1)}, u32[]{:S(2)}, u32[]{:S(2)}) %collective-permute-start.8) | collective-permute-done | bytes 24608 | tf_op jit(solution)/shard_map/ppermute | solution.py:222
  103.0 2.5 %collective-permute-start.9 = (f32[96,128]{1,0:T(8,128)S(1)}, f32[96,128]{1,0:T(8,128)S(1)}, u32[]{:S(2)}, u32[]{:S(2)}) collective-permute-start(f32[96,128]{1,0:T(8,128)S(1)} %maximum_select_fusion.2), channel_id=1, source_target_pairs={{0,2},{1,3},{2,0},{3,1},{4,6},{5,7},{6,4},{7,5},{8,10},{9,11},{10,... | collective-permute-start | bytes 147464 | tf_op jit(solution)/shard_map/ppermute | solution.py:222
  105.5 1.3 slice_bitcast_fusion.3
  106.8 4.8 %collective-permute-start.4 = (bf16[128,1024]{1,0:T(8,128)(2,1)S(1)}, bf16[128,1024]{1,0:T(8,128)(2,1)S(1)}, u32[]{:S(2)}, u32[]{:S(2)}) collective-permute-start(bf16[128,1024]{1,0:T(8,128)(2,1)S(1)} %get-tuple-element.22), channel_id=1, source_target_pairs={{0,760},{8,0},{16,8},{24,16},{32,24},{40,32},{48,40},{56,48},{64,5... | collective-permute-start | bytes 786440 | tf_op jit(solution)/shard_map/ppermute | solution.py:21
  111.6 3.0 %collective-permute-start.5 = (bf16[128,1024]{1,0:T(8,128)(2,1)S(1)}, bf16[128,1024]{1,0:T(8,128)(2,1)S(1)}, u32[]{:S(2)}, u32[]{:S(2)}) collective-permute-start(bf16[128,1024]{1,0:T(8,128)(2,1)S(1)} %get-tuple-element.25), channel_id=1, source_target_pairs={{0,8},{8,16},{16,24},{24,32},{32,40},{40,48},{48,56},{56,64},{64,7... | collective-permute-start | bytes 786440 | tf_op jit(solution)/shard_map/ppermute | solution.py:21
  114.5 9.5 %collective-permute-start.6 = (bf16[128,1024]{1,0:T(8,128)(2,1)S(1)}, bf16[128,1024]{1,0:T(8,128)(2,1)S(1)}, u32[]{:S(2)}, u32[]{:S(2)}) collective-permute-start(bf16[128,1024]{1,0:T(8,128)(2,1)S(1)} %get-tuple-element.24), channel_id=1, source_target_pairs={{0,752},{8,760},{16,0},{24,8},{32,16},{40,24},{48,32},{56,40},{64,... | collective-permute-start | bytes 786440 | tf_op jit(solution)/shard_map/ppermute | solution.py:21
  124.1 1.9 %collective-permute-start.7 = (bf16[128,1024]{1,0:T(8,128)(2,1)S(1)}, bf16[128,1024]{1,0:T(8,128)(2,1)S(1)}, u32[]{:S(2)}, u32[]{:S(2)}) collective-permute-start(bf16[128,1024]{1,0:T(8,128)(2,1)S(1)} %get-tuple-element.23), channel_id=1, source_target_pairs={{0,16},{8,24},{16,32},{24,40},{32,48},{40,56},{48,64},{56,72},{64,... | collective-permute-start | bytes 786440 | tf_op jit(solution)/shard_map/ppermute | solution.py:21
  126.0 0.0 collective-permute-done.9
  126.0 5.1 %collective-permute-start.10 = (f32[192,128]{1,0:T(8,128)S(1)}, f32[192,128]{1,0:T(8,128)S(1)}, u32[]{:S(2)}, u32[]{:S(2)}) collective-permute-start(f32[192,128]{1,0:T(8,128)S(1)} %maximum_select_fusion.1), channel_id=1, source_target_pairs={{0,1},{1,0},{2,3},{3,2},{4,5},{5,4},{6,7},{7,6},{8,9},{9,8},{10,11... | collective-permute-start | bytes 294920 | tf_op jit(solution)/shard_map/ppermute | solution.py:222
  131.1 1.8 %convert_element_type.9 = bf16[2,128,512]{2,1,0:T(8,128)(2,1)} convert(f32[2,128,512]{2,1,0:T(8,128)} %get-tuple-element.13) | non-fusion elementwise | flops 131072 | bytes 786432 | tf_op jit(solution)/shard_map/convert_element_type | solution.py:281
  132.9 2.9 %collective-permute-done.10 = f32[192,128]{1,0:T(8,128)S(1)} collective-permute-done((f32[192,128]{1,0:T(8,128)S(1)}, f32[192,128]{1,0:T(8,128)S(1)}, u32[]{:S(2)}, u32[]{:S(2)}) %collective-permute-start.10) | collective-permute-done | bytes 98336 | tf_op jit(solution)/shard_map/ppermute | solution.py:222
  135.8 0.7 copy.13
  136.5 0.0 collective-permute-done.4
  136.5 0.9 gather_fusion.4
  137.4 0.0 collective-permute-done.5
  137.4 0.9 gather_fusion.5
  138.3 0.0 collective-permute-done.6
  138.3 0.9 gather_fusion.6
  139.1 0.0 collective-permute-done.7
  139.1 0.9 gather_fusion.7
  140.1 1.2 convert_reduce_fusion
  141.3 0.5 all-gather.5.cloned.1.call-done
  141.8 9.2 %shard_map.103 = (bf16[2,128,512]{2,1,0:T(8,128)(2,1)}, bf16[2,128,512]{2,1,0:T(8,128)(2,1)}) custom-call(s32[2]{0:T(128)} %count_ref.3, s32[2,6]{1,0:T(2,128)} %tiles_ref.3, bf16[16,128,1024]{2,1,0:T(8,128)(2,1)} %bitcast.52, f32[16,3,8,128]{3,2,1,0:T(8,128)} %bitcast.59, bf16[2,128,512]{2,1,0:T(8,128)(2,1)} %bitcast.56, bf16[2,128,512]{2,1,0:T(8,128)(2,1)} %bitcast.57, ...), custom_call_target="tpu_custom_call" | custom-call | flops 1610612736 | bytes 7536640 | tf_op jit(solution)/shard_map/pallas_call | solution.py:208
  (10 shorter events, 0.2 us)
Async XLA Ops:
  7.2 31.0 %copy-start.1 = (s32[2,256]{1,0:T(2,128)S(1)}, s32[2,256]{1,0:T(2,128)}, u32[]{:S(2)}) copy-start(s32[2,256]{1,0:T(2,128)} %param.11) | copy-start | bytes 6148
  7.2 70.7 %all-gather.3.cloned.1.call-start = ((), (), s32[]{:S(2)}) async-start(), calls=%async_computation | async-start | bytes 4718592 | tf_op jit(solution)/shard_map/all_gather | solution.py:241
  9.2 0.8 copy-start
  10.0 131.8 %all-gather.5.cloned.1.call-start = ((), (), s32[]{:S(2)}) async-start(), calls=%async_computation.1 | async-start | bytes 4718592 | tf_op jit(solution)/shard_map/all_gather | solution.py:242
  13.0 25.2 %collective-permute-start = (bf16[128,1024]{1,0:T(8,128)(2,1)S(1)}, bf16[128,1024]{1,0:T(8,128)(2,1)S(1)}, u32[]{:S(2)}, u32[]{:S(2)}) collective-permute-start(bf16[128,1024]{1,0:T(8,128)(2,1)S(1)} %get-tuple-element.26), channel_id=1, source_target_pairs={{0,760},{8,0},{16,8},{24,16},{32,24},{40,32},{48,40},{56,48},{64,5... | collective-permute-start | bytes 786440 | tf_op jit(solution)/shard_map/ppermute | solution.py:21
  25.5 15.2 %collective-permute-start.2 = (bf16[128,1024]{1,0:T(8,128)(2,1)S(1)}, bf16[128,1024]{1,0:T(8,128)(2,1)S(1)}, u32[]{:S(2)}, u32[]{:S(2)}) collective-permute-start(bf16[128,1024]{1,0:T(8,128)(2,1)S(1)} %get-tuple-element.26), channel_id=1, source_target_pairs={{0,752},{8,760},{16,0},{24,8},{32,16},{40,24},{48,32},{56,40},{64,... | collective-permute-start | bytes 786440 | tf_op jit(solution)/shard_map/ppermute | solution.py:21
  33.0 6.8 %collective-permute-start.1 = (bf16[128,1024]{1,0:T(8,128)(2,1)S(1)}, bf16[128,1024]{1,0:T(8,128)(2,1)S(1)}, u32[]{:S(2)}, u32[]{:S(2)}) collective-permute-start(bf16[128,1024]{1,0:T(8,128)(2,1)S(1)} %get-tuple-element.27), channel_id=1, source_target_pairs={{0,8},{8,16},{16,24},{24,32},{32,40},{40,48},{48,56},{56,64},{64,7... | collective-permute-start | bytes 786440 | tf_op jit(solution)/shard_map/ppermute | solution.py:21
  36.2 13.3 %collective-permute-start.3 = (bf16[128,1024]{1,0:T(8,128)(2,1)S(1)}, bf16[128,1024]{1,0:T(8,128)(2,1)S(1)}, u32[]{:S(2)}, u32[]{:S(2)}) collective-permute-start(bf16[128,1024]{1,0:T(8,128)(2,1)S(1)} %get-tuple-element.27), channel_id=1, source_target_pairs={{0,16},{8,24},{16,32},{24,40},{32,48},{40,56},{48,64},{56,72},{64,... | collective-permute-start | bytes 786440 | tf_op jit(solution)/shard_map/ppermute | solution.py:21
  94.4 8.6 %collective-permute-start.8 = (f32[48,128]{1,0:T(8,128)S(1)}, f32[48,128]{1,0:T(8,128)S(1)}, u32[]{:S(2)}, u32[]{:S(2)}) collective-permute-start(f32[48,128]{1,0:T(8,128)S(1)} %bitcast.64), channel_id=1, source_target_pairs={{0,4},{1,5},{2,6},{3,7},{4,0},{5,1},{6,2},{7,3},{8,12},{9,13},{10,... | collective-permute-start | bytes 73736 | tf_op jit(solution)/shard_map/ppermute | solution.py:222
  103.0 23.0 %collective-permute-start.9 = (f32[96,128]{1,0:T(8,128)S(1)}, f32[96,128]{1,0:T(8,128)S(1)}, u32[]{:S(2)}, u32[]{:S(2)}) collective-permute-start(f32[96,128]{1,0:T(8,128)S(1)} %maximum_select_fusion.2), channel_id=1, source_target_pairs={{0,2},{1,3},{2,0},{3,1},{4,6},{5,7},{6,4},{7,5},{8,10},{9,11},{10,... | collective-permute-start | bytes 147464 | tf_op jit(solution)/shard_map/ppermute | solution.py:222
  106.8 29.7 %collective-permute-start.4 = (bf16[128,1024]{1,0:T(8,128)(2,1)S(1)}, bf16[128,1024]{1,0:T(8,128)(2,1)S(1)}, u32[]{:S(2)}, u32[]{:S(2)}) collective-permute-start(bf16[128,1024]{1,0:T(8,128)(2,1)S(1)} %get-tuple-element.22), channel_id=1, source_target_pairs={{0,760},{8,0},{16,8},{24,16},{32,24},{40,32},{48,40},{56,48},{64,5... | collective-permute-start | bytes 786440 | tf_op jit(solution)/shard_map/ppermute | solution.py:21
  111.6 25.8 %collective-permute-start.5 = (bf16[128,1024]{1,0:T(8,128)(2,1)S(1)}, bf16[128,1024]{1,0:T(8,128)(2,1)S(1)}, u32[]{:S(2)}, u32[]{:S(2)}) collective-permute-start(bf16[128,1024]{1,0:T(8,128)(2,1)S(1)} %get-tuple-element.25), channel_id=1, source_target_pairs={{0,8},{8,16},{16,24},{24,32},{32,40},{40,48},{48,56},{56,64},{64,7... | collective-permute-start | bytes 786440 | tf_op jit(solution)/shard_map/ppermute | solution.py:21
  114.5 23.7 %collective-permute-start.6 = (bf16[128,1024]{1,0:T(8,128)(2,1)S(1)}, bf16[128,1024]{1,0:T(8,128)(2,1)S(1)}, u32[]{:S(2)}, u32[]{:S(2)}) collective-permute-start(bf16[128,1024]{1,0:T(8,128)(2,1)S(1)} %get-tuple-element.24), channel_id=1, source_target_pairs={{0,752},{8,760},{16,0},{24,8},{32,16},{40,24},{48,32},{56,40},{64,... | collective-permute-start | bytes 786440 | tf_op jit(solution)/shard_map/ppermute | solution.py:21
  124.1 15.1 %collective-permute-start.7 = (bf16[128,1024]{1,0:T(8,128)(2,1)S(1)}, bf16[128,1024]{1,0:T(8,128)(2,1)S(1)}, u32[]{:S(2)}, u32[]{:S(2)}) collective-permute-start(bf16[128,1024]{1,0:T(8,128)(2,1)S(1)} %get-tuple-element.23), channel_id=1, source_target_pairs={{0,16},{8,24},{16,32},{24,40},{32,48},{40,56},{48,64},{56,72},{64,... | collective-permute-start | bytes 786440 | tf_op jit(solution)/shard_map/ppermute | solution.py:21
  126.0 9.8 %collective-permute-start.10 = (f32[192,128]{1,0:T(8,128)S(1)}, f32[192,128]{1,0:T(8,128)S(1)}, u32[]{:S(2)}, u32[]{:S(2)}) collective-permute-start(f32[192,128]{1,0:T(8,128)S(1)} %maximum_select_fusion.1), channel_id=1, source_target_pairs={{0,1},{1,0},{2,3},{3,2},{4,5},{5,4},{6,7},{7,6},{8,9},{9,8},{10,11... | collective-permute-start | bytes 294920 | tf_op jit(solution)/shard_map/ppermute | solution.py:222
Sparse Core Ops, SparseCore 0:
  10.4 67.4 all-gather.2
  80.2 61.5 all-gather.4
